TPU v7x, 32 devices: a whole 2x2x4 slice. The times are simulated.
32 devices in a mesh: groups: 2 (over y), tiles: 4 (over z), band: 2 (over x), stokes: 2 (over core).
Axes of the slice: x: 2, y: 2, z: 4, core: 2. Of those that a mesh axis runs over, the one named last changes fastest.
Arguments:
- right_side: float32 [3, 128, 2048], P(None, ('groups', 'tiles'), ('band', 'stokes')), parts along dimension 1, may hold values from -4 to 4
- noise_block: float32 [6, 128, 2048], P(None, ('groups', 'tiles'), ('band', 'stokes')), parts along dimension 1, may hold values from -0.09 to 0.4, as said below
- edges: float32 [2, 128, 2048], P(None, ('groups', 'tiles'), ('band', 'stokes')), parts along dimension 1, may hold values from 0.5 to 2
Outputs:
- correction: float32 [3, 128, 2048], P(None, ('groups', 'tiles'), ('band', 'stokes')), parts along dimension 1
There are 2 independent parts, one for each index of `groups`. A program takes and returns all parts, laid end to end along the dimension named above; each array names one. Nothing has to cross between parts.
Inputs may be any that keep to these rules, and one draw needn't show every extreme that they name: `noise_block`: entries 0 to 2 are positive and each exceeds the sum of the magnitudes of the two couplings in its row of the 3 x 3 matrix.
All inputs are finite; a program needn't handle non-finite values.
Results may differ from a plain program's by a relative error of at most 0.00002.
Values sent between devices are 32-bit elements; how exact they have to be, the bound alone decides.
No kernel may reach another device: no remote copies, remote signals or barrier semaphores. Data moves between devices by JAX's collectives and lax.ppermute only.
A program may use at most 64 MiB of HBM per device.

v0:
```python
import jax
import jax.numpy as jnp
from jax import lax
from jax.sharding import PartitionSpec as P

LEVELS = 5
PRE = 2
POST = 2
COARSE_SWEEPS = 8

OMEGA = 0.8

ROWS = "tiles"
COLS = ("band", "stokes")
GRID = ("tiles", "band", "stokes")

HALO = PRE - 1 + POST
GATHER_PIXELS = 32768


def with_halo(cells, width):
    for axis, dim in ((ROWS, 1), (COLS, 2)):
        count = lax.axis_size(axis)
        ends = count - 1
        head = lax.slice_in_dim(cells, 0, width, axis=dim)
        tail = lax.slice_in_dim(cells, cells.shape[dim] - width, cells.shape[dim], axis=dim)
        cells = jnp.concatenate(
            [
                lax.ppermute(tail, axis, [(i, i + 1) for i in range(ends)]),
                cells,
                lax.ppermute(head, axis, [(i + 1, i) for i in range(ends)]),
            ],
            axis=dim,
        )
    return cells


def crop(x, k):
    if k == 0:
        return x
    return x[..., k:-k, k:-k]


HIGH = lax.Precision.HIGHEST


def pairs(n, pick=None):
    rows = lax.broadcasted_iota(jnp.int32, (n, n // 2), 0)
    cols = lax.broadcasted_iota(jnp.int32, (n, n // 2), 1)
    hit = (rows // 2 == cols) if pick is None else (rows == 2 * cols + pick)
    return hit.astype(jnp.float32)


def sum_rows(x, m):
    return jnp.einsum("...hw,hv->...vw", x, m, precision=HIGH)


def sum_cols(x, m):
    return jnp.einsum("...hw,wv->...hv", x, m, precision=HIGH)


def restrict_sum(x):
    return sum_cols(sum_rows(x, pairs(x.shape[-2])), pairs(x.shape[-1]))


def restrict_down(down):
    return sum_cols(sum_rows(down, pairs(down.shape[-2], 1)), pairs(down.shape[-1]))


def restrict_right(right):
    return sum_rows(sum_cols(right, pairs(right.shape[-1], 1)), pairs(right.shape[-2]))


def prolong(coarse):
    height, width = coarse.shape[-2] * 2, coarse.shape[-1] * 2
    taller = jnp.einsum("...vw,hv->...hw", coarse, pairs(height), precision=HIGH)
    return jnp.einsum("...hv,wv->...hw", taller, pairs(width), precision=HIGH)


def apply_planes(iterate, padded, noise, couplings):
    first = noise[0] * iterate[0] + noise[3] * iterate[1] + noise[4] * iterate[2]
    second = noise[3] * iterate[0] + noise[1] * iterate[1] + noise[5] * iterate[2]
    third = noise[4] * iterate[0] + noise[5] * iterate[1] + noise[2] * iterate[2]
    totals = couplings[0] + couplings[1] + couplings[2] + couplings[3]
    image = []
    for local, core, rim in zip((first, second, third), iterate, padded):
        neighbours = (
            couplings[0] * rim[2:, 1:-1]
            + couplings[1] * rim[:-2, 1:-1]
            + couplings[2] * rim[1:-1, 2:]
            + couplings[3] * rim[1:-1, :-2]
        )
        image.append(local + totals * core - neighbours)
    return image


def apply_ext(padded, noise, couplings):
    return apply_planes([p[1:-1, 1:-1] for p in padded], padded, noise, couplings)


def diagonal_of(noise, couplings):
    totals = couplings[0] + couplings[1] + couplings[2] + couplings[3]
    return [noise[k] + totals for k in range(3)]


def couplings_from(down, right):
    upward = jnp.pad(down, ((1, 0), (0, 0)))[:-1, :]
    leftward = jnp.pad(right, ((0, 0), (1, 0)))[:, :-1]
    return [down, upward, right, leftward]


def crops(planes, k):
    return [crop(p, k) for p in planes]


def smooth_whole(iterate, source, noise, couplings, diagonal):
    image = apply_planes(iterate, [jnp.pad(p, 1) for p in iterate], noise, couplings)
    return [i + OMEGA * (s - a) / d for i, s, a, d in zip(iterate, source, image, diagonal)]


def cycle_whole(source, noise, down, right, level_index):
    couplings = couplings_from(down, right)
    diagonal = diagonal_of(noise, couplings)
    iterate = [OMEGA * s / d for s, d in zip(source, diagonal)]
    if level_index == LEVELS - 1:
        for sweep_index in range(COARSE_SWEEPS - 1):
            iterate = smooth_whole(iterate, source, noise, couplings, diagonal)
        return iterate
    for sweep_index in range(PRE - 1):
        iterate = smooth_whole(iterate, source, noise, couplings, diagonal)
    image = apply_planes(iterate, [jnp.pad(p, 1) for p in iterate], noise, couplings)
    residual = [s - a for s, a in zip(source, image)]
    coarse = cycle_whole(
        [restrict_sum(r) for r in residual],
        [restrict_sum(n) for n in noise],
        restrict_down(down),
        restrict_right(right),
        level_index + 1,
    )
    iterate = [i + prolong(c) for i, c in zip(iterate, coarse)]
    for sweep_index in range(POST):
        iterate = smooth_whole(iterate, source, noise, couplings, diagonal)
    return iterate


def gather_grid(block):
    count_rows = lax.axis_size(ROWS)
    count_cols = lax.axis_size(COLS)
    planes, height, width = block.shape
    stacked = lax.all_gather(block, GRID, axis=0, tiled=False)
    stacked = stacked.reshape(count_rows, count_cols, planes, height, width)
    whole = stacked.transpose(2, 0, 3, 1, 4).reshape(planes, count_rows * height, count_cols * width)
    return [whole[k] for k in range(planes)]


def own_window(whole, height, width, ring):
    row = lax.axis_index(ROWS) * height
    col = lax.axis_index(COLS) * width
    padded = jnp.pad(whole, ring) if ring else whole
    return lax.dynamic_slice(padded, (row, col), (height + 2 * ring, width + 2 * ring))


def inside(height, width, ext):
    rows = lax.axis_index(ROWS) * height - ext + lax.broadcasted_iota(
        jnp.int32, (height + 2 * ext, width + 2 * ext), 0
    )
    cols = lax.axis_index(COLS) * width - ext + lax.broadcasted_iota(
        jnp.int32, (height + 2 * ext, width + 2 * ext), 1
    )
    return (
        (rows >= 0)
        & (rows < lax.axis_size(ROWS) * height)
        & (cols >= 0)
        & (cols < lax.axis_size(COLS) * width)
    )


def sweep_ext(iterate, source, noise, couplings, diagonal, mask):
    image = apply_ext(iterate, noise, couplings)
    new = [
        i[1:-1, 1:-1] + OMEGA * (s - a) / d for i, s, a, d in zip(iterate, source, image, diagonal)
    ]
    if mask is None:
        return new
    return [jnp.where(mask, n, 0.0) for n in new]


def level_split(source, noise, couplings, below):
    height = source[0].shape[0] - 2 * HALO
    width = source[0].shape[1] - 2 * HALO
    diagonal = diagonal_of(noise, couplings)
    ext = HALO
    mask = inside(height, width, ext)
    iterate = [jnp.where(mask, OMEGA * s / d, 0.0) for s, d in zip(source, diagonal)]
    for sweep_index in range(PRE - 1):
        ext -= 1
        cut = HALO - ext
        iterate = sweep_ext(
            iterate, crops(source, cut), crops(noise, cut), crops(couplings, cut),
            crops(diagonal, cut), inside(height, width, ext),
        )
    image = apply_ext(crops(iterate, ext - 1), crops(noise, HALO), crops(couplings, HALO))
    residual = [s - a for s, a in zip(crops(source, HALO), image)]
    coarse = below(residual)
    ring = (POST + 1) // 2
    iterate = [
        i + crop(prolong(c), 2 * ring - POST) for i, c in zip(crops(iterate, ext - POST), coarse)
    ]
    for sweep_index in range(POST):
        ext = POST - 1 - sweep_index
        cut = HALO - ext
        iterate = sweep_ext(
            iterate, crops(source, cut), crops(noise, cut), crops(couplings, cut),
            crops(diagonal, cut), inside(height, width, ext) if ext else None,
        )
    return iterate


def on_device(right_side, noise_block, edges):
    count_rows = lax.axis_size(ROWS)
    count_cols = lax.axis_size(COLS)
    height0, width0 = right_side.shape[1], right_side.shape[2]

    noises = [noise_block]
    downs = [edges[0]]
    rights = [edges[1]]
    for level in range(1, LEVELS):
        noises.append(restrict_sum(noises[-1]))
        downs.append(restrict_down(downs[-1]))
        rights.append(restrict_right(rights[-1]))

    gathered = LEVELS - 1
    for level in range(LEVELS):
        height, width = height0 >> level, width0 >> level
        whole = count_rows * height * count_cols * width
        if whole <= GATHER_PIXELS or height <= HALO or width <= HALO or level == LEVELS - 1:
            gathered = level
            break

    if gathered == 0:
        whole = gather_grid(jnp.concatenate([right_side, noise_block, edges]))
        correction = cycle_whole(whole[:3], whole[3:9], whole[9], whole[10], 0)
        return jnp.stack([own_window(c, height0, width0, 0) for c in correction])

    packed = gather_grid(
        jnp.concatenate([noises[gathered], downs[gathered][None], rights[gathered][None]])
    )
    whole_noise, whole_down, whole_right = packed[:6], packed[6], packed[7]
    split_inputs = []
    for level in range(gathered):
        parts = [noises[level], downs[level][None], rights[level][None]]
        if level == 0:
            parts = [right_side] + parts
        ringed = with_halo(jnp.concatenate(parts), HALO + 1)
        ringed = [ringed[k] for k in range(ringed.shape[0])]
        source = crops(ringed[:3], 1) if level == 0 else None
        if level == 0:
            ringed = ringed[3:]
        down, right = ringed[6], ringed[7]
        couplings = [down[1:-1, 1:-1], down[:-2, 1:-1], right[1:-1, 1:-1], right[1:-1, :-2]]
        split_inputs.append((source, crops(ringed[:6], 1), couplings))

    ring = (POST + 1) // 2

    def run(level, source):
        height, width = height0 >> level, width0 >> level
        _, noise, couplings = split_inputs[level]

        def below(residual):
            coarse_source = jnp.stack([restrict_sum(r) for r in residual])
            if level + 1 == gathered:
                correction = cycle_whole(
                    gather_grid(coarse_source), whole_noise, whole_down, whole_right, gathered
                )
                return [own_window(c, height // 2, width // 2, ring) for c in correction]
            coarse = run(level + 1, list(with_halo(coarse_source, HALO)))
            return list(with_halo(jnp.stack(coarse), ring))

        return level_split(source, noise, couplings, below)

    return jnp.stack(run(0, split_inputs[0][0]))


def solution(mesh):
    in_specs = (
        P(None, ("groups", "tiles"), ("band", "stokes")),
        P(None, ("groups", "tiles"), ("band", "stokes")),
        P(None, ("groups", "tiles"), ("band", "stokes")),
    )
    out_specs = P(None, ("groups", "tiles"), ("band", "stokes"))
    return jax.shard_map(
        on_device, mesh=mesh, in_specs=in_specs, out_specs=out_specs, check_vma=False
    )
```

profile of v0, /device:TPU:0, one launch (start us, length us, event | category | flops | bytes accessed | tf_op | source)
XLA Modules:
  0.0 111.7 jit_solution(13481772282940744759)
XLA Ops:
  6.5 0.9 constant_dynamic-update-slice_fusion.2
  7.5 0.9 constant_dynamic-update-slice_fusion.1
  8.4 0.8 constant_dynamic-update-slice_fusion
  9.3 1.3 %collective-permute-start.1 = (f32[11,4,512]{2,1,0:T(4,128)S(1)}, f32[11,4,512]{2,1,0:T(4,128)S(1)}, u32[]{:S(2)}, u32[]{:S(2)}) collective-permute-start(f32[11,4,512]{2,1,0:T(4,128)S(1)} %get-tuple-element.71), channel_id=1, source_target_pairs={{4,0},{8,4},{12,8},{5,1},{9,5},{13,9},{6,2},{10,6},{14,10},{7,3},{... | collective-permute-start | bytes 270344 | tf_op jit(solution)/shard_map/ppermute | solution.py:31
  10.6 5.6 %collective-permute-start = (f32[11,4,512]{2,1,0:T(4,128)S(1)}, f32[11,4,512]{2,1,0:T(4,128)S(1)}, u32[]{:S(2)}, u32[]{:S(2)}) collective-permute-start(f32[11,4,512]{2,1,0:T(4,128)S(1)} %get-tuple-element.70), channel_id=1, source_target_pairs={{0,4},{4,8},{8,12},{1,5},{5,9},{9,13},{2,6},{6,10},{10,14},{3,7},{... | collective-permute-start | bytes 270344 | tf_op jit(solution)/shard_map/ppermute | solution.py:29
  19.6 1.3 %collective-permute-start.3 = (f32[11,24,4]{2,1,0:T(8,128)S(1)}, f32[11,24,4]{2,1,0:T(8,128)S(1)}, u32[]{:S(2)}, u32[]{:S(2)}) collective-permute-start(f32[11,24,4]{2,1,0:T(8,128)S(1)} %get-tuple-element.66), channel_id=1, source_target_pairs={{1,0},{2,1},{3,2},{5,4},{6,5},{7,6},{9,8},{10,9},{11,10},{13,12},{... | collective-permute-start | bytes 12680 | tf_op jit(solution)/shard_map/ppermute | solution.py:31
  20.9 3.0 %collective-permute-start.2 = (f32[11,24,4]{2,1,0:T(8,128)S(1)}, f32[11,24,4]{2,1,0:T(8,128)S(1)}, u32[]{:S(2)}, u32[]{:S(2)}) collective-permute-start(f32[11,24,4]{2,1,0:T(8,128)S(1)} %get-tuple-element.65), channel_id=1, source_target_pairs={{0,1},{1,2},{2,3},{4,5},{5,6},{6,7},{8,9},{9,10},{10,11},{12,13},{... | collective-permute-start | bytes 12680 | tf_op jit(solution)/shard_map/ppermute | solution.py:29
  24.0 0.9 collective-permute-done.2
  29.1 26.1 %all-gather = f32[48,8,256]{2,1,0:T(8,128)S(1)} all-gather(f32[3,8,256]{2,1,0:T(8,128)S(1)} %pad_maximum_fusion.6), channel_id=2, replica_groups=mesh['groups'=2,'tiles'=4,'band'=2,'stokes'=2] {'tiles','band','stokes'}, dimensions={0}, use_global_device_ids=true | all-gather | bytes 417792 | tf_op jit(solution)/shard_map/all_gather | solution.py:150
  55.2 2.7 %all-gather.4.cloned.1.call-done = f32[128,8,256]{2,1,0:T(8,128)} async-done(((f32[8,8,256]{2,1,0:T(8,128)}), f32[128,8,256]{2,1,0:T(8,128)}) %all-gather.4.cloned.1.call-update) | async-done | bytes 1048592 | tf_op jit(solution)/shard_map/all_gather | solution.py:150
  57.9 1.4 %copy.8 = f32[4,4,8,8,256]{4,3,1,0,2:T(8,128)S(1)} copy(f32[4,4,8,8,256]{4,3,2,1,0:T(8,128)} %bitcast.225) | data formatting | bytes 2097152 | tf_op jit(solution)/shard_map/reshape | solution.py:151
  63.1 0.8 fusion.13
  64.4 0.9 fusion.10
  65.3 0.9 fusion.12
  66.1 0.9 fusion.9
  67.0 0.9 fusion.7
  67.9 0.9 fusion.8
  68.7 0.9 fusion.4
  69.6 0.9 fusion.5
  71.0 0.9 fusion.669
  72.9 0.9 fusion.446
  73.8 0.9 fusion.458
  78.5 0.7 fusion.60
  90.1 0.9 convolution_add_fusion.5
  91.0 0.9 convolution_add_fusion.4
  93.3 2.2 %fusion.14 = f32[32,1024]{1,0:T(8,128)S(1)} fusion(f32[32,1024]{1,0:T(8,128)S(1)} %get-tuple-element.32, f32[32,512]{1,0:T(8,128)S(1)} %fusion.700, s32[1024]{0:T(1024)S(1)} %get-tuple-element.112, s32[1024]{0:T(1024)S(1)} %get-tuple-element.113, pred[1024]{0:T(1024)(128)(4,1)S(1)} %fusion.1042), kind=kOutput, calls=%fused_computation.16 | convolution fusion | flops 202407936 | bytes 336896 | tf_op jit(solution)/shard_map/...hv,wv->...hw/dot_general | solution.py:77
  95.5 2.2 %fusion.15 = f32[32,1024]{1,0:T(8,128)S(1)} fusion(f32[32,1024]{1,0:T(8,128)S(1)} %get-tuple-element.52, f32[32,512]{1,0:T(8,128)S(1)} %fusion.698, s32[1024]{0:T(1024)S(1)} %get-tuple-element.112, s32[1024]{0:T(1024)S(1)} %get-tuple-element.113, pred[1024]{0:T(1024)(128)(4,1)S(1)} %fusion.1042), kind=kOutput, calls=%fused_computation.17 | convolution fusion | flops 202407936 | bytes 336896 | tf_op jit(solution)/shard_map/...hv,wv->...hw/dot_general | solution.py:77
  97.7 1.3 %fusion.225 = (f32[32,1024]{1,0:T(8,128)S(1)}, f32[32,1024]{1,0:T(8,128)S(1)}) fusion(f32[32,1024]{1,0:T(8,128)S(1)} %fusion.14, f32[32,1024]{1,0:T(8,128)S(1)} %bitcast.221, f32[32,1024]{1,0:T(8,128)S(1)} %bitcast.154, f32[32,1024]{1,0:T(8,128)S(1)} %bitcast.164, f32[32,1024]{1,0:T(8,128)S(1)} %bitcast.172, f32[32,1024]{1,0:T(8,128)S(1)} %bitcast.180, ...), kind=kOutput, calls=%fused_computation.290 | convolution fusion | flops 203161600 | bytes 1516544 | tf_op jit(solution)/shard_map/...hv,wv->...hw/dot_general | solution.py:77
  100.2 0.7 convolution_add_fusion
  100.9 0.7 convolution_add_fusion.1
  101.9 0.7 convolution_add_fusion.2
  104.2 0.6 pad_maximum_fusion.4
  (151 shorter events, 32.4 us)
Async XLA Ops:
  6.5 10.2 %copy-start = (f32[6,16,512]{2,1,0:T(8,128)S(1)}, f32[6,16,512]{2,1,0:T(8,128)}, u32[]{:S(2)}) copy-start(f32[6,16,512]{2,1,0:T(8,128)} %param.4) | copy-start | bytes 589828
  6.5 9.7 %copy-start.1 = (f32[2,16,512]{2,1,0:T(8,128)S(1)}, f32[2,16,512]{2,1,0:T(8,128)}, u32[]{:S(2)}) copy-start(f32[2,16,512]{2,1,0:T(8,128)} %param.5) | copy-start | bytes 196612
  6.5 51.4 %all-gather.4.cloned.1.call-start = ((), (), s32[]{:S(2)}) async-start(), calls=%async_computation | async-start | bytes 1114112 | tf_op jit(solution)/shard_map/all_gather | solution.py:150
  9.3 10.1 %collective-permute-start.1 = (f32[11,4,512]{2,1,0:T(4,128)S(1)}, f32[11,4,512]{2,1,0:T(4,128)S(1)}, u32[]{:S(2)}, u32[]{:S(2)}) collective-permute-start(f32[11,4,512]{2,1,0:T(4,128)S(1)} %get-tuple-element.71), channel_id=1, source_target_pairs={{4,0},{8,4},{12,8},{5,1},{9,5},{13,9},{6,2},{10,6},{14,10},{7,3},{... | collective-permute-start | bytes 270344 | tf_op jit(solution)/shard_map/ppermute | solution.py:31
  10.6 8.8 %collective-permute-start = (f32[11,4,512]{2,1,0:T(4,128)S(1)}, f32[11,4,512]{2,1,0:T(4,128)S(1)}, u32[]{:S(2)}, u32[]{:S(2)}) collective-permute-start(f32[11,4,512]{2,1,0:T(4,128)S(1)} %get-tuple-element.70), channel_id=1, source_target_pairs={{0,4},{4,8},{8,12},{1,5},{5,9},{9,13},{2,6},{6,10},{10,14},{3,7},{... | collective-permute-start | bytes 270344 | tf_op jit(solution)/shard_map/ppermute | solution.py:29
  19.6 4.4 %collective-permute-start.3 = (f32[11,24,4]{2,1,0:T(8,128)S(1)}, f32[11,24,4]{2,1,0:T(8,128)S(1)}, u32[]{:S(2)}, u32[]{:S(2)}) collective-permute-start(f32[11,24,4]{2,1,0:T(8,128)S(1)} %get-tuple-element.66), channel_id=1, source_target_pairs={{1,0},{2,1},{3,2},{5,4},{6,5},{7,6},{9,8},{10,9},{11,10},{13,12},{... | collective-permute-start | bytes 12680 | tf_op jit(solution)/shard_map/ppermute | solution.py:31
  20.9 4.0 %collective-permute-start.2 = (f32[11,24,4]{2,1,0:T(8,128)S(1)}, f32[11,24,4]{2,1,0:T(8,128)S(1)}, u32[]{:S(2)}, u32[]{:S(2)}) collective-permute-start(f32[11,24,4]{2,1,0:T(8,128)S(1)} %get-tuple-element.65), channel_id=1, source_target_pairs={{0,1},{1,2},{2,3},{4,5},{5,6},{6,7},{8,9},{9,10},{10,11},{12,13},{... | collective-permute-start | bytes 12680 | tf_op jit(solution)/shard_map/ppermute | solution.py:29
Sparse Core Ops, SparseCore 0:
  19.2 38.6 all-gather.3
where the time goes:
time: 112 us
  matrix products  45.2 us (40%)
  blocking collectives  26.1 us (23%)
  between operations  14.2 us (13%)
  starting transfers between devices  11.2 us (10%)
  other arithmetic  7.13 us (6%)
  local copies, waits for them, and re-layouts  4.34 us (4%)
  waiting for transfers between devices  3.63 us (3%)
    all_gather x1, blocking collectives, gather_grid(): stacked = lax.all_gather(block, GRID, axis=0, tiled=False)  26.1 us
    dot_general x39, matrix products, sum_cols(): return jnp.einsum('...hw,wv->...hv', x, m, precision=HIGH)  20.5 us
    dot_general x39, matrix products, sum_rows(): return jnp.einsum('...hw,hv->...vw', x, m, precision=HIGH)  11 us
    dot_general x12, matrix products, prolong(): return jnp.einsum('...hv,wv->...hw', taller, pairs(width), precision=HIGH)  10.9 us
    ppermute x2, starting transfers between devices, with_halo(): lax.ppermute(tail, axis, [(i, i + 1) for i in range(ends)])  8.6 us
    dot_general x12, matrix products, prolong(): jnp.einsum('...vw,hv->...hw', coarse, pairs(height), precision=HIGH)  2.73 us
    all_gather x1, waiting for transfers between devices, gather_grid(): stacked = lax.all_gather(block, GRID, axis=0, tiled=False)  2.68 us
    ppermute x2, starting transfers between devices, with_halo(): lax.ppermute(head, axis, [(i + 1, i) for i in range(ends)])  2.58 us
  transfers between devices with their start and end apart: 5, of which 2 were waited for; matrix products, arithmetic and copies ran while one was open for 7% of the time, Pallas kernels for 0%

commit v1 on v0

--- a/solution.py
+++ b/solution.py
@@ -15,7 +15,7 @@
 GRID = ("tiles", "band", "stokes")
 
 HALO = PRE - 1 + POST
-GATHER_PIXELS = 32768
+GATHER_PIXELS = 8192
 
 
 def with_halo(cells, width):

time: 112 us -> 133 us (1.19); the launches traced: 112 us -> 131 us
  starting transfers between devices: 11.2 us -> 31.7 us
  blocking collectives: 26.1 us -> 43.5 us
  matrix products: 45.2 us -> 31.2 us
  between operations: 14.2 us -> 1.12 us
  waiting for transfers between devices: 3.63 us -> 14.2 us
  local copies, waits for them, and re-layouts: 4.34 us -> 1.34 us
    all_gather x1 -> x2, blocking collectives: 26.1 us -> 43.5 us  [gather_grid(): stacked = lax.all_gather(block, GRID, axis=0, tiled=False)]
    ppermute x2 -> x8, waiting for transfers between devices: 0.01 us -> 14.1 us  [with_halo(): lax.ppermute(head, axis, [(i + 1, i) for i in range(ends)])]
    ppermute x2 -> x8, starting transfers between devices: 8.6 us -> 21.4 us  [with_halo(): lax.ppermute(tail, axis, [(i, i + 1) for i in range(ends)])]
    ppermute x2 -> x8, starting transfers between devices: 2.58 us -> 10.3 us  [with_halo(): lax.ppermute(head, axis, [(i + 1, i) for i in range(ends)])]
    dot_general x39 -> x34, matrix products: 20.5 us -> 13.2 us  [sum_cols(): return jnp.einsum('...hw,wv->...hv', x, m, precision=HIGH)]
    dot_general x12, matrix products: 10.9 us -> 6.43 us  [prolong(): return jnp.einsum('...hv,wv->...hw', taller, pairs(width), precision=HIGH)]
    all_gather x1 -> x0, waiting for transfers between devices: 2.68 us -> none  [gather_grid(): stacked = lax.all_gather(block, GRID, axis=0, tiled=False)]
    dot_general x39 -> x34, matrix products: 11 us -> 9.11 us  [sum_rows(): return jnp.einsum('...hw,hv->...vw', x, m, precision=HIGH)]
  transfers between devices with their start and end apart: 5 -> 16, of which waited for: 2 -> 4; matrix products, arithmetic and copies ran while one was open for 7% -> 10% of each run, Pallas kernels for 0% -> 0%
where the time goes in v1:
time: 133 us; the launch traced here: 131 us
  blocking collectives  43.5 us (33%)
  starting transfers between devices  31.7 us (24%)
  matrix products  31.2 us (23%)
  waiting for transfers between devices  14.2 us (11%)
  other arithmetic  7.65 us (6%)
  local copies, waits for them, and re-layouts  1.34 us (1%)
    all_gather x2, blocking collectives, gather_grid(): stacked = lax.all_gather(block, GRID, axis=0, tiled=False)  43.5 us
    ppermute x8, starting transfers between devices, with_halo(): lax.ppermute(tail, axis, [(i, i + 1) for i in range(ends)])  21.4 us
    ppermute x8, waiting for transfers between devices, with_halo(): lax.ppermute(head, axis, [(i + 1, i) for i in range(ends)])  14.1 us
    dot_general x34, matrix products, sum_cols(): return jnp.einsum('...hw,wv->...hv', x, m, precision=HIGH)  13.2 us
    ppermute x8, starting transfers between devices, with_halo(): lax.ppermute(head, axis, [(i + 1, i) for i in range(ends)])  10.3 us
    dot_general x34, matrix products, sum_rows(): return jnp.einsum('...hw,hv->...vw', x, m, precision=HIGH)  9.11 us
    dot_general x12, matrix products, prolong(): return jnp.einsum('...hv,wv->...hw', taller, pairs(width), precision=HIGH)  6.43 us
    select_n x12, other arithmetic, sweep_ext(): return [jnp.where(mask, n, 0.0) for n in new]  3.04 us
  transfers between devices with their start and end apart: 16, of which 4 were waited for; matrix products, arithmetic and copies ran while one was open for 10% of the time, Pallas kernels for 0%

profile of v1, /device:TPU:0, one launch (start us, length us, event | category | flops | bytes accessed | tf_op | source)
XLA Modules:
  0.0 130.7 jit_solution(6289125263452982993)
XLA Ops:
  0.1 1.2 fusion.25
  1.9 0.6 copy-done.1
  3.6 5.1 %collective-permute-start.8 = (f32[8,4,256]{2,1,0:T(4,128)S(1)}, f32[8,4,256]{2,1,0:T(4,128)S(1)}, u32[]{:S(2)}, u32[]{:S(2)}) collective-permute-start(f32[8,4,256]{2,1,0:T(4,128)S(1)} %get-tuple-element.91), channel_id=1, source_target_pairs={{0,4},{4,8},{8,12},{1,5},{5,9},{9,13},{2,6},{6,10},{10,14},{3,7},{... | collective-permute-start | bytes 98312 | tf_op jit(solution)/shard_map/ppermute | solution.py:29
  8.7 1.3 collective-permute-start.9
  10.1 4.6 %collective-permute-start = (f32[11,4,512]{2,1,0:T(4,128)S(1)}, f32[11,4,512]{2,1,0:T(4,128)S(1)}, u32[]{:S(2)}, u32[]{:S(2)}) collective-permute-start(f32[11,4,512]{2,1,0:T(4,128)S(1)} %get-tuple-element.59), channel_id=1, source_target_pairs={{0,4},{4,8},{8,12},{1,5},{5,9},{9,13},{2,6},{6,10},{10,14},{3,7},{... | collective-permute-start | bytes 270344 | tf_op jit(solution)/shard_map/ppermute | solution.py:29
  14.7 1.3 collective-permute-start.1
  17.8 23.4 %all-gather.1 = f32[128,4,128]{2,0,1:T(8,128)S(1)} all-gather(f32[8,4,128]{2,0,1:T(8,128)S(1)} %pad_maximum_fusion.13), channel_id=3, replica_groups=mesh['groups'=2,'tiles'=4,'band'=2,'stokes'=2] {'tiles','band','stokes'}, dimensions={0}, use_global_device_ids=true | all-gather | bytes 278528 | tf_op jit(solution)/shard_map/all_gather | solution.py:150
  48.6 2.3 %collective-permute-start.2 = (f32[11,24,4]{2,1,0:T(8,128)S(1)}, f32[11,24,4]{2,1,0:T(8,128)S(1)}, u32[]{:S(2)}, u32[]{:S(2)}) collective-permute-start(f32[11,24,4]{2,1,0:T(8,128)S(1)} %get-tuple-element.57), channel_id=1, source_target_pairs={{0,1},{1,2},{2,3},{4,5},{5,6},{6,7},{8,9},{9,10},{10,11},{12,13},{... | collective-permute-start | bytes 12680 | tf_op jit(solution)/shard_map/ppermute | solution.py:29
  50.9 1.3 collective-permute-start.3
  52.3 3.0 %collective-permute-start.10 = (f32[8,16,4]{2,1,0:T(8,128)S(1)}, f32[8,16,4]{2,1,0:T(8,128)S(1)}, u32[]{:S(2)}, u32[]{:S(2)}) collective-permute-start(f32[8,16,4]{2,1,0:T(8,128)S(1)} %get-tuple-element.81), channel_id=1, source_target_pairs={{0,1},{1,2},{2,3},{4,5},{5,6},{6,7},{8,9},{9,10},{10,11},{12,13},{... | collective-permute-start | bytes 6152 | tf_op jit(solution)/shard_map/ppermute | solution.py:29
  55.3 1.3 collective-permute-start.11
  60.8 1.3 collective-permute-start.4
  62.1 1.3 collective-permute-start.5
  63.7 4.1 %collective-permute-done.5 = f32[3,3,256]{2,1,0:T(4,128)S(1)} collective-permute-done((f32[3,3,256]{2,1,0:T(4,128)S(1)}, f32[3,3,256]{2,1,0:T(4,128)S(1)}, u32[]{:S(2)}, u32[]{:S(2)}) %collective-permute-start.5) | collective-permute-done | bytes 9248 | tf_op jit(solution)/shard_map/ppermute | solution.py:31
  67.8 2.6 %collective-permute-start.6 = (f32[3,14,3]{2,1,0:T(8,128)S(1)}, f32[3,14,3]{2,1,0:T(8,128)S(1)}, u32[]{:S(2)}, u32[]{:S(2)}) collective-permute-start(f32[3,14,3]{2,1,0:T(8,128)S(1)} %get-tuple-element.101), channel_id=1, source_target_pairs={{0,1},{1,2},{2,3},{4,5},{5,6},{6,7},{8,9},{9,10},{10,11},{12,13},{... | collective-permute-start | bytes 1520 | tf_op jit(solution)/shard_map/ppermute | solution.py:29
  70.5 1.3 collective-permute-start.7
  71.8 4.1 %collective-permute-done.7 = f32[3,14,3]{2,1,0:T(8,128)S(1)} collective-permute-done((f32[3,14,3]{2,1,0:T(8,128)S(1)}, f32[3,14,3]{2,1,0:T(8,128)S(1)}, u32[]{:S(2)}, u32[]{:S(2)}) %collective-permute-start.7) | collective-permute-done | bytes 536 | tf_op jit(solution)/shard_map/ppermute | solution.py:31
  78.5 20.1 %all-gather = f32[48,4,128]{2,1,0:T(4,128)S(1)} all-gather(f32[3,4,128]{2,1,0:T(4,128)S(1)} %pad_maximum_fusion.14), channel_id=2, replica_groups=mesh['groups'=2,'tiles'=4,'band'=2,'stokes'=2] {'tiles','band','stokes'}, dimensions={0}, use_global_device_ids=true | all-gather | bytes 104448 | tf_op jit(solution)/shard_map/all_gather | solution.py:150
  101.2 0.5 fusion.841
  109.0 0.9 convolution_add_fusion.4
  109.8 0.9 convolution_add_fusion.5
  110.7 0.5 fusion.320
  114.3 1.3 collective-permute-start.12
  115.6 1.3 collective-permute-start.13
  116.9 4.2 %collective-permute-done.13 = f32[3,1,256]{2,1,0:T(1,128)S(1)} collective-permute-done((f32[3,1,256]{2,1,0:T(1,128)S(1)}, f32[3,1,256]{2,1,0:T(1,128)S(1)}, u32[]{:S(2)}, u32[]{:S(2)}) %collective-permute-start.13) | collective-permute-done | bytes 3104 | tf_op jit(solution)/shard_map/ppermute | solution.py:31
  121.2 1.3 collective-permute-start.14
  122.5 1.3 collective-permute-start.15
  123.8 1.8 %collective-permute-done.15 = f32[3,10,1]{2,1,0:T(8,128)S(1)} collective-permute-done((f32[3,10,1]{2,1,0:T(8,128)S(1)}, f32[3,10,1]{2,1,0:T(8,128)S(1)}, u32[]{:S(2)}, u32[]{:S(2)}) %collective-permute-start.15) | collective-permute-done | bytes 152 | tf_op jit(solution)/shard_map/ppermute | solution.py:31
  126.3 0.7 convolution_add_fusion.2
  127.0 0.7 convolution_add_fusion.1
  127.7 0.7 convolution_add_fusion
  130.0 0.6 pad_maximum_fusion.6
  (204 shorter events, 33.0 us)
Async XLA Ops:
  0.0 1.3 copy-start
  1.6 0.8 copy-start.1
  3.6 6.4 %copy-start.2 = (f32[3,16,512]{2,1,0:T(8,128)S(1)}, f32[3,16,512]{2,1,0:T(8,128)}, u32[]{:S(2)}) copy-start(f32[3,16,512]{2,1,0:T(8,128)} %param.3) | copy-start | bytes 294916
  3.6 44.8 %collective-permute-start.8 = (f32[8,4,256]{2,1,0:T(4,128)S(1)}, f32[8,4,256]{2,1,0:T(4,128)S(1)}, u32[]{:S(2)}, u32[]{:S(2)}) collective-permute-start(f32[8,4,256]{2,1,0:T(4,128)S(1)} %get-tuple-element.91), channel_id=1, source_target_pairs={{0,4},{4,8},{8,12},{1,5},{5,9},{9,13},{2,6},{6,10},{10,14},{3,7},{... | collective-permute-start | bytes 98312 | tf_op jit(solution)/shard_map/ppermute | solution.py:29
  8.7 39.7 %collective-permute-start.9 = (f32[8,4,256]{2,1,0:T(4,128)S(1)}, f32[8,4,256]{2,1,0:T(4,128)S(1)}, u32[]{:S(2)}, u32[]{:S(2)}) collective-permute-start(f32[8,4,256]{2,1,0:T(4,128)S(1)} %get-tuple-element.92), channel_id=1, source_target_pairs={{4,0},{8,4},{12,8},{5,1},{9,5},{13,9},{6,2},{10,6},{14,10},{7,3},{... | collective-permute-start | bytes 98312 | tf_op jit(solution)/shard_map/ppermute | solution.py:31
  10.1 38.4 %collective-permute-start = (f32[11,4,512]{2,1,0:T(4,128)S(1)}, f32[11,4,512]{2,1,0:T(4,128)S(1)}, u32[]{:S(2)}, u32[]{:S(2)}) collective-permute-start(f32[11,4,512]{2,1,0:T(4,128)S(1)} %get-tuple-element.59), channel_id=1, source_target_pairs={{0,4},{4,8},{8,12},{1,5},{5,9},{9,13},{2,6},{6,10},{10,14},{3,7},{... | collective-permute-start | bytes 270344 | tf_op jit(solution)/shard_map/ppermute | solution.py:29
  14.7 33.8 %collective-permute-start.1 = (f32[11,4,512]{2,1,0:T(4,128)S(1)}, f32[11,4,512]{2,1,0:T(4,128)S(1)}, u32[]{:S(2)}, u32[]{:S(2)}) collective-permute-start(f32[11,4,512]{2,1,0:T(4,128)S(1)} %get-tuple-element.60), channel_id=1, source_target_pairs={{4,0},{8,4},{12,8},{5,1},{9,5},{13,9},{6,2},{10,6},{14,10},{7,3},{... | collective-permute-start | bytes 270344 | tf_op jit(solution)/shard_map/ppermute | solution.py:31
  48.6 8.0 %collective-permute-start.2 = (f32[11,24,4]{2,1,0:T(8,128)S(1)}, f32[11,24,4]{2,1,0:T(8,128)S(1)}, u32[]{:S(2)}, u32[]{:S(2)}) collective-permute-start(f32[11,24,4]{2,1,0:T(8,128)S(1)} %get-tuple-element.57), channel_id=1, source_target_pairs={{0,1},{1,2},{2,3},{4,5},{5,6},{6,7},{8,9},{9,10},{10,11},{12,13},{... | collective-permute-start | bytes 12680 | tf_op jit(solution)/shard_map/ppermute | solution.py:29
  50.9 5.7 %collective-permute-start.3 = (f32[11,24,4]{2,1,0:T(8,128)S(1)}, f32[11,24,4]{2,1,0:T(8,128)S(1)}, u32[]{:S(2)}, u32[]{:S(2)}) collective-permute-start(f32[11,24,4]{2,1,0:T(8,128)S(1)} %get-tuple-element.58), channel_id=1, source_target_pairs={{1,0},{2,1},{3,2},{5,4},{6,5},{7,6},{9,8},{10,9},{11,10},{13,12},{... | collective-permute-start | bytes 12680 | tf_op jit(solution)/shard_map/ppermute | solution.py:31
  52.3 11.2 %collective-permute-start.10 = (f32[8,16,4]{2,1,0:T(8,128)S(1)}, f32[8,16,4]{2,1,0:T(8,128)S(1)}, u32[]{:S(2)}, u32[]{:S(2)}) collective-permute-start(f32[8,16,4]{2,1,0:T(8,128)S(1)} %get-tuple-element.81), channel_id=1, source_target_pairs={{0,1},{1,2},{2,3},{4,5},{5,6},{6,7},{8,9},{9,10},{10,11},{12,13},{... | collective-permute-start | bytes 6152 | tf_op jit(solution)/shard_map/ppermute | solution.py:29
  55.3 8.2 %collective-permute-start.11 = (f32[8,16,4]{2,1,0:T(8,128)S(1)}, f32[8,16,4]{2,1,0:T(8,128)S(1)}, u32[]{:S(2)}, u32[]{:S(2)}) collective-permute-start(f32[8,16,4]{2,1,0:T(8,128)S(1)} %get-tuple-element.82), channel_id=1, source_target_pairs={{1,0},{2,1},{3,2},{5,4},{6,5},{7,6},{9,8},{10,9},{11,10},{13,12},{... | collective-permute-start | bytes 6152 | tf_op jit(solution)/shard_map/ppermute | solution.py:31
  60.8 2.8 %collective-permute-start.4 = (f32[3,3,256]{2,1,0:T(4,128)S(1)}, f32[3,3,256]{2,1,0:T(4,128)S(1)}, u32[]{:S(2)}, u32[]{:S(2)}) collective-permute-start(f32[3,3,256]{2,1,0:T(4,128)S(1)} %get-tuple-element.105), channel_id=1, source_target_pairs={{0,4},{4,8},{8,12},{1,5},{5,9},{9,13},{2,6},{6,10},{10,14},{3,7},{... | collective-permute-start | bytes 27656 | tf_op jit(solution)/shard_map/ppermute | solution.py:29
  62.1 5.6 %collective-permute-start.5 = (f32[3,3,256]{2,1,0:T(4,128)S(1)}, f32[3,3,256]{2,1,0:T(4,128)S(1)}, u32[]{:S(2)}, u32[]{:S(2)}) collective-permute-start(f32[3,3,256]{2,1,0:T(4,128)S(1)} %get-tuple-element.106), channel_id=1, source_target_pairs={{4,0},{8,4},{12,8},{5,1},{9,5},{13,9},{6,2},{10,6},{14,10},{7,3},{... | collective-permute-start | bytes 27656 | tf_op jit(solution)/shard_map/ppermute | solution.py:31
  67.8 4.0 %collective-permute-start.6 = (f32[3,14,3]{2,1,0:T(8,128)S(1)}, f32[3,14,3]{2,1,0:T(8,128)S(1)}, u32[]{:S(2)}, u32[]{:S(2)}) collective-permute-start(f32[3,14,3]{2,1,0:T(8,128)S(1)} %get-tuple-element.101), channel_id=1, source_target_pairs={{0,1},{1,2},{2,3},{4,5},{5,6},{6,7},{8,9},{9,10},{10,11},{12,13},{... | collective-permute-start | bytes 1520 | tf_op jit(solution)/shard_map/ppermute | solution.py:29
  70.5 5.5 %collective-permute-start.7 = (f32[3,14,3]{2,1,0:T(8,128)S(1)}, f32[3,14,3]{2,1,0:T(8,128)S(1)}, u32[]{:S(2)}, u32[]{:S(2)}) collective-permute-start(f32[3,14,3]{2,1,0:T(8,128)S(1)} %get-tuple-element.102), channel_id=1, source_target_pairs={{1,0},{2,1},{3,2},{5,4},{6,5},{7,6},{9,8},{10,9},{11,10},{13,12},{... | collective-permute-start | bytes 1520 | tf_op jit(solution)/shard_map/ppermute | solution.py:31
  114.3 2.6 %collective-permute-start.12 = (f32[3,1,256]{2,1,0:T(1,128)S(1)}, f32[3,1,256]{2,1,0:T(1,128)S(1)}, u32[]{:S(2)}, u32[]{:S(2)}) collective-permute-start(f32[3,1,256]{2,1,0:T(1,128)S(1)} %get-tuple-element.103), channel_id=1, source_target_pairs={{0,4},{4,8},{8,12},{1,5},{5,9},{9,13},{2,6},{6,10},{10,14},{3,7},{... | collective-permute-start | bytes 9224 | tf_op jit(solution)/shard_map/ppermute | solution.py:29
  115.6 5.5 %collective-permute-start.13 = (f32[3,1,256]{2,1,0:T(1,128)S(1)}, f32[3,1,256]{2,1,0:T(1,128)S(1)}, u32[]{:S(2)}, u32[]{:S(2)}) collective-permute-start(f32[3,1,256]{2,1,0:T(1,128)S(1)} %get-tuple-element.104), channel_id=1, source_target_pairs={{4,0},{8,4},{12,8},{5,1},{9,5},{13,9},{6,2},{10,6},{14,10},{7,3},{... | collective-permute-start | bytes 9224 | tf_op jit(solution)/shard_map/ppermute | solution.py:31
  121.2 2.6 %collective-permute-start.14 = (f32[3,10,1]{2,1,0:T(8,128)S(1)}, f32[3,10,1]{2,1,0:T(8,128)S(1)}, u32[]{:S(2)}, u32[]{:S(2)}) collective-permute-start(f32[3,10,1]{2,1,0:T(8,128)S(1)} %get-tuple-element.95), channel_id=1, source_target_pairs={{0,1},{1,2},{2,3},{4,5},{5,6},{6,7},{8,9},{9,10},{10,11},{12,13},{... | collective-permute-start | bytes 368 | tf_op jit(solution)/shard_map/ppermute | solution.py:29
  122.5 3.1 %collective-permute-start.15 = (f32[3,10,1]{2,1,0:T(8,128)S(1)}, f32[3,10,1]{2,1,0:T(8,128)S(1)}, u32[]{:S(2)}, u32[]{:S(2)}) collective-permute-start(f32[3,10,1]{2,1,0:T(8,128)S(1)} %get-tuple-element.96), channel_id=1, source_target_pairs={{1,0},{2,1},{3,2},{5,4},{6,5},{7,6},{9,8},{10,9},{11,10},{13,12},{... | collective-permute-start | bytes 368 | tf_op jit(solution)/shard_map/ppermute | solution.py:31

commit v2 on v0

--- a/solution.py
+++ b/solution.py
@@ -118,7 +118,8 @@
     return [i + OMEGA * (s - a) / d for i, s, a, d in zip(iterate, source, image, diagonal)]
 
 
-def cycle_whole(source, noise, down, right, level_index):
+def cycle_whole(source, hierarchy, level_index):
+    noise, down, right = hierarchy[0]
     couplings = couplings_from(down, right)
     diagonal = diagonal_of(noise, couplings)
     iterate = [OMEGA * s / d for s, d in zip(source, diagonal)]
@@ -129,28 +130,38 @@
     for sweep_index in range(PRE - 1):
         iterate = smooth_whole(iterate, source, noise, couplings, diagonal)
     image = apply_planes(iterate, [jnp.pad(p, 1) for p in iterate], noise, couplings)
-    residual = [s - a for s, a in zip(source, image)]
-    coarse = cycle_whole(
-        [restrict_sum(r) for r in residual],
-        [restrict_sum(n) for n in noise],
-        restrict_down(down),
-        restrict_right(right),
-        level_index + 1,
-    )
-    iterate = [i + prolong(c) for i, c in zip(iterate, coarse)]
+    residual = restrict_sum(jnp.stack([s - a for s, a in zip(source, image)]))
+    coarse = prolong(
+        jnp.stack(cycle_whole([residual[k] for k in range(3)], hierarchy[1:], level_index + 1))
+    )
+    iterate = [iterate[k] + coarse[k] for k in range(3)]
     for sweep_index in range(POST):
         iterate = smooth_whole(iterate, source, noise, couplings, diagonal)
     return iterate
 
 
 def gather_grid(block):
+    return gather_grids([block])[0]
+
+
+def gather_grids(blocks):
     count_rows = lax.axis_size(ROWS)
     count_cols = lax.axis_size(COLS)
-    planes, height, width = block.shape
-    stacked = lax.all_gather(block, GRID, axis=0, tiled=False)
-    stacked = stacked.reshape(count_rows, count_cols, planes, height, width)
-    whole = stacked.transpose(2, 0, 3, 1, 4).reshape(planes, count_rows * height, count_cols * width)
-    return [whole[k] for k in range(planes)]
+    planes = blocks[0].shape[0]
+    flat = jnp.concatenate([b.reshape(planes, -1) for b in blocks], axis=1)
+    stacked = lax.all_gather(flat, GRID, axis=0, tiled=False)
+    grids = []
+    offset = 0
+    for b in blocks:
+        _, height, width = b.shape
+        part = stacked[:, :, offset:offset + height * width]
+        offset += height * width
+        part = part.reshape(count_rows, count_cols, planes, height, width)
+        whole = part.transpose(2, 0, 3, 1, 4).reshape(
+            planes, count_rows * height, count_cols * width
+        )
+        grids.append([whole[k] for k in range(planes)])
+    return grids
 
 
 def own_window(whole, height, width, ring):
@@ -238,14 +249,20 @@
             break
 
     if gathered == 0:
-        whole = gather_grid(jnp.concatenate([right_side, noise_block, edges]))
-        correction = cycle_whole(whole[:3], whole[3:9], whole[9], whole[10], 0)
+        packed = gather_grids(
+            [jnp.concatenate([noises[l], downs[l][None], rights[l][None]]) for l in range(LEVELS)]
+        )
+        hierarchy = [(p[:6], p[6], p[7]) for p in packed]
+        correction = cycle_whole(gather_grid(right_side), hierarchy, 0)
         return jnp.stack([own_window(c, height0, width0, 0) for c in correction])
 
-    packed = gather_grid(
-        jnp.concatenate([noises[gathered], downs[gathered][None], rights[gathered][None]])
-    )
-    whole_noise, whole_down, whole_right = packed[:6], packed[6], packed[7]
+    packed = gather_grids(
+        [
+            jnp.concatenate([noises[l], downs[l][None], rights[l][None]])
+            for l in range(gathered, LEVELS)
+        ]
+    )
+    hierarchy = [(p[:6], p[6], p[7]) for p in packed]
     split_inputs = []
     for level in range(gathered):
         parts = [noises[level], downs[level][None], rights[level][None]]
@@ -267,11 +284,9 @@
         _, noise, couplings = split_inputs[level]
 
         def below(residual):
-            coarse_source = jnp.stack([restrict_sum(r) for r in residual])
+            coarse_source = restrict_sum(jnp.stack(residual))
             if level + 1 == gathered:
-                correction = cycle_whole(
-                    gather_grid(coarse_source), whole_noise, whole_down, whole_right, gathered
-                )
+                correction = cycle_whole(gather_grid(coarse_source), hierarchy, gathered)
                 return [own_window(c, height // 2, width // 2, ring) for c in correction]
             coarse = run(level + 1, list(with_halo(coarse_source, HALO)))
             return list(with_halo(jnp.stack(coarse), ring))

time: 112 us -> 90.3 us (0.81)
  matrix products: 45.2 us -> 16.5 us
  waiting for transfers between devices: 3.63 us -> 8.6 us
  other arithmetic: 7.13 us -> 10.4 us
  local copies, waits for them, and re-layouts: 4.34 us -> 7.08 us
  starting transfers between devices: 11.2 us -> 8.82 us
  blocking collectives: 26.1 us -> 24.1 us
    dot_general x39 -> x16, matrix products: 20.5 us -> 5.06 us  [sum_cols(): return jnp.einsum('...hw,wv->...hv', x, m, precision=HIGH)]
    ppermute x2, waiting for transfers between devices: 0.01 us -> 7.94 us  [with_halo(): lax.ppermute(head, axis, [(i + 1, i) for i in range(ends)])]
    dot_general x39 -> x16, matrix products: 11 us -> 4.34 us  [sum_rows(): return jnp.einsum('...hw,hv->...vw', x, m, precision=HIGH)]
    dot_general x12 -> x6, matrix products: 10.9 us -> 5.65 us  [prolong(): return jnp.einsum('...hv,wv->...hw', taller, pairs(width), precision=HIGH)]
    slice x2 -> x25, local copies, waits for them, and re-layouts: 0.13 us -> 4.45 us  [the longest x4 3.97 us: gather_grids(): part = stacked[:, :, offset:offset + height * width]]
    all_gather x1, waiting for transfers between devices: 2.68 us -> 0.02 us  [gather_grids(): stacked = lax.all_gather(flat, GRID, axis=0, tiled=False)]
    another operation x1 -> x15, other arithmetic: 0.01 us -> 2.57 us  [the longest x6 1.28 us: cycle_whole(): residual = restrict_sum(jnp.stack([s - a for s, a in zip(source, image)]))]
    ppermute x2, starting transfers between devices: 8.6 us -> 6.23 us  [with_halo(): lax.ppermute(tail, axis, [(i, i + 1) for i in range(ends)])]
  transfers between devices with their start and end apart: 5 -> 5, of which waited for: 2 -> 3; matrix products, arithmetic and copies ran while one was open for 7% -> 4% of each run, Pallas kernels for 0% -> 0%
where the time goes in v2:
time: 90.3 us; the launch traced here: 89.9 us
  blocking collectives  24.1 us (27%)
  matrix products  16.5 us (18%)
  between operations  14.4 us (16%)
  other arithmetic  10.4 us (12%)
  starting transfers between devices  8.82 us (10%)
  waiting for transfers between devices  8.6 us (10%)
  local copies, waits for them, and re-layouts  7.08 us (8%)
    all_gather x1, blocking collectives, gather_grids(): stacked = lax.all_gather(flat, GRID, axis=0, tiled=False)  24.1 us
    ppermute x2, waiting for transfers between devices, with_halo(): lax.ppermute(head, axis, [(i + 1, i) for i in range(ends)])  7.94 us
    ppermute x2, starting transfers between devices, with_halo(): lax.ppermute(tail, axis, [(i, i + 1) for i in range(ends)])  6.23 us
    dot_general x6, matrix products, prolong(): return jnp.einsum('...hv,wv->...hw', taller, pairs(width), precision=HIGH)  5.65 us
    dot_general x16, matrix products, sum_cols(): return jnp.einsum('...hw,wv->...hv', x, m, precision=HIGH)  5.06 us
    dot_general x16, matrix products, sum_rows(): return jnp.einsum('...hw,hv->...vw', x, m, precision=HIGH)  4.34 us
    slice x4, local copies, waits for them, and re-layouts, gather_grids(): part = stacked[:, :, offset:offset + height * width]  3.97 us
    ppermute x2, starting transfers between devices, with_halo(): lax.ppermute(head, axis, [(i + 1, i) for i in range(ends)])  2.58 us
  transfers between devices with their start and end apart: 5, of which 3 were waited for; matrix products, arithmetic and copies ran while one was open for 4% of the time, Pallas kernels for 0%

profile of v2, /device:TPU:0, one launch (start us, length us, event | category | flops | bytes accessed | tf_op | source)
XLA Modules:
  0.0 89.9 jit_solution(4792942737481246025)
XLA Ops:
  6.8 1.0 %fusion.490 = f32[8,512]{1,0:T(8,128)S(1)} fusion(f32[2,16,512]{2,1,0:T(8,128)} %param.5, s32[8]{0:T(128)S(1)} %multiply_add_fusion.6), kind=kOutput, calls=%fused_computation.813 | convolution fusion | flops 786560 | bytes 49184 | tf_op jit(solution)/shard_map/...hw,hv->...vw/dot_general | solution.py:55
  7.7 0.4 fusion.11
  9.3 1.1 %convolution_bitcast_fusion.2 = f32[6,8,512]{2,1,0:T(8,128)S(1)} fusion(f32[6,16,512]{2,1,0:T(8,128)} %param.4, s32[16]{0:T(128)S(1)} %get-tuple-element.139, s32[16]{0:T(128)S(1)} %get-tuple-element.140, pred[16]{0:T(512)(128)(4,1)S(1)} %compare_and_fusion.6), kind=kOutput, calls=%fused_computation.6 | convolution fusion | flops 4718848 | bytes 295056 | tf_op jit(solution)/shard_map/...hw,hv->...vw/dot_general | solution.py:55
  10.4 0.5 fusion.975
  13.8 0.7 pad_maximum_fusion.5
  14.6 4.9 %collective-permute-start = (f32[11,4,512]{2,1,0:T(4,128)S(1)}, f32[11,4,512]{2,1,0:T(4,128)S(1)}, u32[]{:S(2)}, u32[]{:S(2)}) collective-permute-start(f32[11,4,512]{2,1,0:T(4,128)S(1)} %get-tuple-element.94), channel_id=1, source_target_pairs={{0,4},{4,8},{8,12},{1,5},{5,9},{9,13},{2,6},{6,10},{10,14},{3,7},{... | collective-permute-start | bytes 270344 | tf_op jit(solution)/shard_map/ppermute | solution.py:29
  19.5 1.3 %collective-permute-start.1 = (f32[11,4,512]{2,1,0:T(4,128)S(1)}, f32[11,4,512]{2,1,0:T(4,128)S(1)}, u32[]{:S(2)}, u32[]{:S(2)}) collective-permute-start(f32[11,4,512]{2,1,0:T(4,128)S(1)} %get-tuple-element.95), channel_id=1, source_target_pairs={{4,0},{8,4},{12,8},{5,1},{9,5},{13,9},{6,2},{10,6},{14,10},{7,3},{... | collective-permute-start | bytes 270344 | tf_op jit(solution)/shard_map/ppermute | solution.py:31
  21.0 0.6 collective-permute-done
  21.6 4.3 %collective-permute-done.1 = f32[11,4,512]{2,1,0:T(4,128)S(1)} collective-permute-done((f32[11,4,512]{2,1,0:T(4,128)S(1)}, f32[11,4,512]{2,1,0:T(4,128)S(1)}, u32[]{:S(2)}, u32[]{:S(2)}) %collective-permute-start.1) | collective-permute-done | bytes 90144 | tf_op jit(solution)/shard_map/ppermute | solution.py:31
  26.1 1.3 %collective-permute-start.2 = (f32[11,24,4]{2,1,0:T(8,128)S(1)}, f32[11,24,4]{2,1,0:T(8,128)S(1)}, u32[]{:S(2)}, u32[]{:S(2)}) collective-permute-start(f32[11,24,4]{2,1,0:T(8,128)S(1)} %get-tuple-element.88), channel_id=1, source_target_pairs={{0,1},{1,2},{2,3},{4,5},{5,6},{6,7},{8,9},{9,10},{10,11},{12,13},{... | collective-permute-start | bytes 12680 | tf_op jit(solution)/shard_map/ppermute | solution.py:29
  27.4 1.3 %collective-permute-start.3 = (f32[11,24,4]{2,1,0:T(8,128)S(1)}, f32[11,24,4]{2,1,0:T(8,128)S(1)}, u32[]{:S(2)}, u32[]{:S(2)}) collective-permute-start(f32[11,24,4]{2,1,0:T(8,128)S(1)} %get-tuple-element.89), channel_id=1, source_target_pairs={{1,0},{2,1},{3,2},{5,4},{6,5},{7,6},{9,8},{10,9},{11,10},{13,12},{... | collective-permute-start | bytes 12680 | tf_op jit(solution)/shard_map/ppermute | solution.py:31
  28.7 3.6 %collective-permute-done.3 = f32[11,24,4]{2,1,0:T(8,128)S(1)} collective-permute-done((f32[11,24,4]{2,1,0:T(8,128)S(1)}, f32[11,24,4]{2,1,0:T(8,128)S(1)}, u32[]{:S(2)}, u32[]{:S(2)}) %collective-permute-start.3) | collective-permute-done | bytes 4256 | tf_op jit(solution)/shard_map/ppermute | solution.py:31
  32.4 0.4 pad_maximum_fusion
  34.9 0.4 fusion.977
  35.4 24.1 %all_gather.9 = f32[16,3,2048]{2,1,0:T(4,128)S(1)} all-gather(f32[1,3,2048]{2,1,0:T(4,128)S(1)} %all_gather_reshape.3), channel_id=1, replica_groups=mesh['groups'=2,'tiles'=4,'band'=2,'stokes'=2] {'tiles','band','stokes'}, dimensions={0}, use_global_device_ids=true | all-gather | bytes 417792 | tf_op jit(solution)/shard_map/all_gather | solution.py:152
  60.0 0.8 slice.1949
  60.8 0.8 slice.1937
  61.6 1.0 %slice.1925 = f32[16,8,512]{2,1,0:T(8,128)S(1)} slice(f32[16,8,2720]{2,1,0:T(8,128)} %bitcast.874), slice={[0:16], [0:8], [2048:2560]} | slice | bytes 524288 | tf_op jit(solution)/shard_map/slice | solution.py:157
  62.6 1.3 %slice.1913 = f32[16,8,2048]{2,1,0:T(8,128)S(1)} slice(f32[16,8,2720]{2,1,0:T(8,128)} %bitcast.875), slice={[0:16], [0:8], [0:2048]} | slice | bytes 2097152 | tf_op jit(solution)/shard_map/slice | solution.py:157
  65.6 0.3 copy.173
  66.8 0.5 fusion.74
  67.3 0.3 fusion.84
  67.9 1.0 %fusion.3 = f32[3,16,512]{2,1,0:T(8,128)S(1)} fusion(f32[3,16,1024]{2,1,0:T(8,128)S(1)} %convolution_bitcast_fusion.1, s32[1024]{0:T(1024)S(1)} %get-tuple-element.155, s32[1024]{0:T(1024)S(1)} %get-tuple-element.156, pred[1024]{0:T(1024)(128)(4,1)S(1)} %fusion.720), kind=kOutput, calls=%fused_computation.3 | convolution fusion | flops 303038464 | bytes 304128 | tf_op jit(solution)/shard_map/...hw,wv->...hv/dot_general | solution.py:59
  69.5 0.4 fusion.973
  72.7 0.9 %fusion.971 = f32[3,16,512]{2,1,0:T(8,128)S(1)} fusion(f32[3,16,256]{2,1,0:T(8,128)S(1)} %convolution_bitcast_fusion.3, s32[512]{0:T(512)S(1)} %get-tuple-element.141, s32[512]{0:T(512)S(1)} %get-tuple-element.142, pred[512]{0:T(512)(128)(4,1)S(1)} %fusion.926), kind=kOutput, calls=%fused_computation.1497 | convolution fusion | flops 75759616 | bytes 152064 | tf_op jit(solution)/shard_map/...hv,wv->...hw/dot_general | solution.py:77
  74.4 2.4 %fusion.1 = f32[3,32,1024]{2,1,0:T(8,128)S(1)} fusion(f32[3,32,512]{2,1,0:T(8,128)S(1)} %convolution_bitcast_fusion, s32[1024]{0:T(1024)S(1)} %get-tuple-element.155, s32[1024]{0:T(1024)S(1)} %get-tuple-element.156, pred[1024]{0:T(1024)(128)(4,1)S(1)} %fusion.720), kind=kOutput, calls=%fused_computation.2 | convolution fusion | flops 605028352 | bytes 599040 | tf_op jit(solution)/shard_map/...hv,wv->...hw/dot_general | solution.py:77
  77.1 0.5 fusion.142
  78.7 0.7 convolution_add_fusion.2
  79.4 0.7 convolution_add_fusion
  80.0 0.7 convolution_add_fusion.1
  81.0 0.3 fusion.211
  82.4 0.6 pad_maximum_fusion.4
  (179 shorter events, 16.1 us)
Async XLA Ops:
  6.5 5.4 %copy-start.1 = (f32[2,16,512]{2,1,0:T(8,128)S(1)}, f32[2,16,512]{2,1,0:T(8,128)}, u32[]{:S(2)}) copy-start(f32[2,16,512]{2,1,0:T(8,128)} %param.5) | copy-start | bytes 196612
  6.5 53.4 %all-gather.3.cloned.1.call-start = ((), (), s32[]{:S(2)}) async-start(), calls=%async_computation | async-start | bytes 1531904 | tf_op jit(solution)/shard_map/all_gather | solution.py:152
  7.7 6.7 %copy-start.2 = (f32[3,16,512]{2,1,0:T(8,128)S(1)}, f32[3,16,512]{2,1,0:T(8,128)}, u32[]{:S(2)}) copy-start(f32[3,16,512]{2,1,0:T(8,128)} %param.3) | copy-start | bytes 294916
  7.7 6.8 %copy-start = (f32[6,16,512]{2,1,0:T(8,128)S(1)}, f32[6,16,512]{2,1,0:T(8,128)}, u32[]{:S(2)}) copy-start(f32[6,16,512]{2,1,0:T(8,128)} %param.4) | copy-start | bytes 589828
  14.6 7.1 %collective-permute-start = (f32[11,4,512]{2,1,0:T(4,128)S(1)}, f32[11,4,512]{2,1,0:T(4,128)S(1)}, u32[]{:S(2)}, u32[]{:S(2)}) collective-permute-start(f32[11,4,512]{2,1,0:T(4,128)S(1)} %get-tuple-element.94), channel_id=1, source_target_pairs={{0,4},{4,8},{8,12},{1,5},{5,9},{9,13},{2,6},{6,10},{10,14},{3,7},{... | collective-permute-start | bytes 270344 | tf_op jit(solution)/shard_map/ppermute | solution.py:29
  19.5 6.4 %collective-permute-start.1 = (f32[11,4,512]{2,1,0:T(4,128)S(1)}, f32[11,4,512]{2,1,0:T(4,128)S(1)}, u32[]{:S(2)}, u32[]{:S(2)}) collective-permute-start(f32[11,4,512]{2,1,0:T(4,128)S(1)} %get-tuple-element.95), channel_id=1, source_target_pairs={{4,0},{8,4},{12,8},{5,1},{9,5},{13,9},{6,2},{10,6},{14,10},{7,3},{... | collective-permute-start | bytes 270344 | tf_op jit(solution)/shard_map/ppermute | solution.py:31
  26.1 2.6 %collective-permute-start.2 = (f32[11,24,4]{2,1,0:T(8,128)S(1)}, f32[11,24,4]{2,1,0:T(8,128)S(1)}, u32[]{:S(2)}, u32[]{:S(2)}) collective-permute-start(f32[11,24,4]{2,1,0:T(8,128)S(1)} %get-tuple-element.88), channel_id=1, source_target_pairs={{0,1},{1,2},{2,3},{4,5},{5,6},{6,7},{8,9},{9,10},{10,11},{12,13},{... | collective-permute-start | bytes 12680 | tf_op jit(solution)/shard_map/ppermute | solution.py:29
  27.4 5.0 %collective-permute-start.3 = (f32[11,24,4]{2,1,0:T(8,128)S(1)}, f32[11,24,4]{2,1,0:T(8,128)S(1)}, u32[]{:S(2)}, u32[]{:S(2)}) collective-permute-start(f32[11,24,4]{2,1,0:T(8,128)S(1)} %get-tuple-element.89), channel_id=1, source_target_pairs={{1,0},{2,1},{3,2},{5,4},{6,5},{7,6},{9,8},{10,9},{11,10},{13,12},{... | collective-permute-start | bytes 12680 | tf_op jit(solution)/shard_map/ppermute | solution.py:31
Sparse Core Ops, SparseCore 0:
  14.6 43.2 all-gather.2

commit v3 on v2

--- a/solution.py
+++ b/solution.py
@@ -144,12 +144,23 @@
     return gather_grids([block])[0]
 
 
+def gather_axis(x, axis):
+    count = lax.axis_size(axis)
+    me = lax.axis_index(axis)
+    pieces = [x] + [
+        lax.ppermute(x, axis, [(i, (i + k) % count) for i in range(count)]) for k in range(1, count)
+    ]
+    order = (me - jnp.arange(count)) % count
+    return jnp.take(jnp.stack(pieces), order, axis=0, mode="clip")
+
+
 def gather_grids(blocks):
     count_rows = lax.axis_size(ROWS)
     count_cols = lax.axis_size(COLS)
     planes = blocks[0].shape[0]
     flat = jnp.concatenate([b.reshape(planes, -1) for b in blocks], axis=1)
-    stacked = lax.all_gather(flat, GRID, axis=0, tiled=False)
+    stacked = gather_axis(gather_axis(flat, COLS), ROWS)
+    stacked = stacked.reshape((count_rows * count_cols,) + flat.shape)
     grids = []
     offset = 0
     for b in blocks:

time: 90.3 us -> 115 us (1.27)
  the two profiles are of different devices: /device:TPU:0 before, /device:TPU:16 now
where the time goes in v3:
time: 115 us; the launch traced here: 114 us
  starting transfers between devices  31.9 us (28%)
  waiting for transfers between devices  31.8 us (28%)
  matrix products  18.1 us (16%)
  other arithmetic  15.6 us (14%)
  local copies, waits for them, and re-layouts  14.7 us (13%)
  between operations  2.18 us (2%)
    ppermute x12, waiting for transfers between devices, gather_axis(): lax.ppermute(x, axis, [(i, (i + k) % count) for i in range(count)])  28.5 us
    ppermute x12, starting transfers between devices, gather_axis(): lax.ppermute(x, axis, [(i, (i + k) % count) for i in range(count)])  23.3 us
    squeeze x16, local copies, waits for them, and re-layouts, gather_grids(): grids.append([whole[k] for k in range(planes)])  8.36 us
    dot_general x6, matrix products, prolong(): return jnp.einsum('...hv,wv->...hw', taller, pairs(width), precision=HIGH)  5.87 us
    dot_general x16, matrix products, sum_rows(): return jnp.einsum('...hw,hv->...vw', x, m, precision=HIGH)  5.56 us
    dot_general x16, matrix products, sum_cols(): return jnp.einsum('...hw,wv->...hv', x, m, precision=HIGH)  5.29 us
    ppermute x2, starting transfers between devices, with_halo(): lax.ppermute(tail, axis, [(i, i + 1) for i in range(ends)])  5 us
    ppermute x2, starting transfers between devices, with_halo(): lax.ppermute(head, axis, [(i + 1, i) for i in range(ends)])  3.65 us
  transfers between devices with their start and end apart: 16, of which 8 were waited for; matrix products, arithmetic and copies ran while one was open for 10% of the time, Pallas kernels for 0%

profile of v3, /device:TPU:16, one launch (start us, length us, event | category | flops | bytes accessed | tf_op | source)
XLA Modules:
  0.0 114.3 jit_solution(15717743941032698061)
XLA Ops:
  0.4 1.0 fusion.494
  2.8 1.3 %convolution_bitcast_fusion.2 = f32[6,8,512]{2,1,0:T(8,128)S(1)} fusion(f32[6,16,512]{2,1,0:T(8,128)} %param.4, s32[16]{0:T(128)S(1)} %get-tuple-element.139, s32[16]{0:T(128)S(1)} %get-tuple-element.140, pred[16]{0:T(512)(128)(4,1)S(1)} %compare_and_fusion.6), kind=kOutput, calls=%fused_computation.11 | convolution fusion | flops 4718848 | bytes 295056 | tf_op jit(solution)/shard_map/...hw,hv->...vw/dot_general | solution.py:55
  8.4 1.0 collective-permute-start.12
  10.2 3.5 %collective-permute-start = (f32[11,4,512]{2,1,0:T(4,128)S(1)}, f32[11,4,512]{2,1,0:T(4,128)S(1)}, u32[]{:S(2)}, u32[]{:S(2)}) collective-permute-start(f32[11,4,512]{2,1,0:T(4,128)S(1)} %get-tuple-element.94), channel_id=1, source_target_pairs={{0,4},{4,8},{8,12},{1,5},{5,9},{9,13},{2,6},{6,10},{10,14},{3,7},{... | collective-permute-start | bytes 270344 | tf_op jit(solution)/shard_map/ppermute | solution.py:29
  13.6 2.4 %collective-permute-start.1 = (f32[11,4,512]{2,1,0:T(4,128)S(1)}, f32[11,4,512]{2,1,0:T(4,128)S(1)}, u32[]{:S(2)}, u32[]{:S(2)}) collective-permute-start(f32[11,4,512]{2,1,0:T(4,128)S(1)} %get-tuple-element.95), channel_id=1, source_target_pairs={{4,0},{8,4},{12,8},{5,1},{9,5},{13,9},{6,2},{10,6},{14,10},{7,3},{... | collective-permute-start | bytes 270344 | tf_op jit(solution)/shard_map/ppermute | solution.py:31
  21.5 1.5 %collective-permute-start.2 = (f32[11,24,4]{2,1,0:T(8,128)S(1)}, f32[11,24,4]{2,1,0:T(8,128)S(1)}, u32[]{:S(2)}, u32[]{:S(2)}) collective-permute-start(f32[11,24,4]{2,1,0:T(8,128)S(1)} %get-tuple-element.88), channel_id=1, source_target_pairs={{0,1},{1,2},{2,3},{4,5},{5,6},{6,7},{8,9},{9,10},{10,11},{12,13},{... | collective-permute-start | bytes 12680 | tf_op jit(solution)/shard_map/ppermute | solution.py:29
  23.0 1.3 %collective-permute-start.3 = (f32[11,24,4]{2,1,0:T(8,128)S(1)}, f32[11,24,4]{2,1,0:T(8,128)S(1)}, u32[]{:S(2)}, u32[]{:S(2)}) collective-permute-start(f32[11,24,4]{2,1,0:T(8,128)S(1)} %get-tuple-element.89), channel_id=1, source_target_pairs={{1,0},{2,1},{3,2},{5,4},{6,5},{7,6},{9,8},{10,9},{11,10},{13,12},{... | collective-permute-start | bytes 12680 | tf_op jit(solution)/shard_map/ppermute | solution.py:31
  24.3 3.3 %collective-permute-done.3 = f32[11,24,4]{2,1,0:T(8,128)S(1)} collective-permute-done((f32[11,24,4]{2,1,0:T(8,128)S(1)}, f32[11,24,4]{2,1,0:T(8,128)S(1)}, u32[]{:S(2)}, u32[]{:S(2)}) %collective-permute-start.3) | collective-permute-done | bytes 4256 | tf_op jit(solution)/shard_map/ppermute | solution.py:31
  31.6 5.1 %collective-permute-start.5 = (f32[3,2048]{1,0:T(4,128)S(1)}, f32[3,2048]{1,0:T(4,128)S(1)}, u32[]{:S(2)}, u32[]{:S(2)}) collective-permute-start(f32[3,2048]{1,0:T(4,128)S(1)} %bitcast.936), channel_id=1, source_target_pairs={{0,2},{1,3},{2,0},{3,1},{4,6},{5,7},{6,4},{7,5},{8,10},{9,11},{10,... | collective-permute-start | bytes 73736 | tf_op jit(solution)/shard_map/ppermute | solution.py:151
  37.2 1.2 %collective-permute-start.10 = (f32[8,2720]{1,0:T(8,128)S(1)}, f32[8,2720]{1,0:T(8,128)S(1)}, u32[]{:S(2)}, u32[]{:S(2)}) collective-permute-start(f32[8,2720]{1,0:T(8,128)S(1)} %pad_maximum_fusion.9), channel_id=1, source_target_pairs={{0,1},{1,2},{2,3},{3,0},{4,5},{5,6},{6,7},{7,4},{8,9},{9,10},{10,1... | collective-permute-start | bytes 261128 | tf_op jit(solution)/shard_map/ppermute | solution.py:151
  38.9 1.1 collective-permute-done.4
  40.7 1.9 %collective-permute-start.7 = (f32[4,3,2048]{2,1,0:T(4,128)S(1)}, f32[4,3,2048]{2,1,0:T(4,128)S(1)}, u32[]{:S(2)}, u32[]{:S(2)}) collective-permute-start(f32[4,3,2048]{2,1,0:T(4,128)S(1)} %gather_fusion), channel_id=1, source_target_pairs={{0,4},{4,8},{8,12},{12,0},{1,5},{5,9},{9,13},{13,1},{2,6},{6,10},{... | collective-permute-start | bytes 294920 | tf_op jit(solution)/shard_map/ppermute | solution.py:151
  42.6 1.1 collective-permute-start.9
  44.4 3.8 %collective-permute-start.14 = (f32[4,8,2720]{2,1,0:T(8,128)S(1)}, f32[4,8,2720]{2,1,0:T(8,128)S(1)}, u32[]{:S(2)}, u32[]{:S(2)}) collective-permute-start(f32[4,8,2720]{2,1,0:T(8,128)S(1)} %gather_fusion.2), channel_id=1, source_target_pairs={{0,8},{4,12},{8,0},{12,4},{1,9},{5,13},{9,1},{13,5},{2,10},{6,14},... | collective-permute-start | bytes 1044488 | tf_op jit(solution)/shard_map/ppermute | solution.py:151
  48.2 1.5 %collective-permute-done.8 = f32[4,3,2048]{2,1,0:T(4,128)S(1)} collective-permute-done((f32[4,3,2048]{2,1,0:T(4,128)S(1)}, f32[4,3,2048]{2,1,0:T(4,128)S(1)}, u32[]{:S(2)}, u32[]{:S(2)}) %collective-permute-start.8) | collective-permute-done | bytes 98336 | tf_op jit(solution)/shard_map/ppermute | solution.py:151
  49.7 8.3 %collective-permute-start.15 = (f32[4,8,2720]{2,1,0:T(8,128)S(1)}, f32[4,8,2720]{2,1,0:T(8,128)S(1)}, u32[]{:S(2)}, u32[]{:S(2)}) collective-permute-start(f32[4,8,2720]{2,1,0:T(8,128)S(1)} %gather_fusion.2), channel_id=1, source_target_pairs={{0,12},{4,0},{8,4},{12,8},{1,13},{5,1},{9,5},{13,9},{2,14},{6,2},{... | collective-permute-start | bytes 1044488 | tf_op jit(solution)/shard_map/ppermute | solution.py:151
  58.0 4.9 %collective-permute-done.7 = f32[4,3,2048]{2,1,0:T(4,128)S(1)} collective-permute-done((f32[4,3,2048]{2,1,0:T(4,128)S(1)}, f32[4,3,2048]{2,1,0:T(4,128)S(1)}, u32[]{:S(2)}, u32[]{:S(2)}) %collective-permute-start.7) | collective-permute-done | bytes 98336 | tf_op jit(solution)/shard_map/ppermute | solution.py:151
  62.9 4.4 %collective-permute-done.9 = f32[4,3,2048]{2,1,0:T(4,128)S(1)} collective-permute-done((f32[4,3,2048]{2,1,0:T(4,128)S(1)}, f32[4,3,2048]{2,1,0:T(4,128)S(1)}, u32[]{:S(2)}, u32[]{:S(2)}) %collective-permute-start.9) | collective-permute-done | bytes 98336 | tf_op jit(solution)/shard_map/ppermute | solution.py:151
  67.4 0.9 gather_fusion.1
  68.7 6.5 %collective-permute-done.14 = f32[4,8,2720]{2,1,0:T(8,128)S(1)} collective-permute-done((f32[4,8,2720]{2,1,0:T(8,128)S(1)}, f32[4,8,2720]{2,1,0:T(8,128)S(1)}, u32[]{:S(2)}, u32[]{:S(2)}) %collective-permute-start.14) | collective-permute-done | bytes 348192 | tf_op jit(solution)/shard_map/ppermute | solution.py:151
  75.2 9.6 %collective-permute-done.13 = f32[4,8,2720]{2,1,0:T(8,128)S(1)} collective-permute-done((f32[4,8,2720]{2,1,0:T(8,128)S(1)}, f32[4,8,2720]{2,1,0:T(8,128)S(1)}, u32[]{:S(2)}, u32[]{:S(2)}) %collective-permute-start.13) | collective-permute-done | bytes 348192 | tf_op jit(solution)/shard_map/ppermute | solution.py:151
  85.5 0.7 slice.1933
  88.4 0.7 squeeze.253
  89.0 0.7 squeeze.251
  90.4 0.7 squeeze.248
  92.6 0.7 squeeze.242
  93.4 0.7 squeeze.239
  94.3 0.7 squeeze.234
  97.8 1.0 fusion.3
  103.3 1.1 %fusion.988 = f32[3,16,512]{2,1,0:T(8,128)S(1)} fusion(f32[3,16,256]{2,1,0:T(8,128)S(1)} %convolution_bitcast_fusion.3, s32[512]{0:T(512)S(1)} %copy-done.50, s32[512]{0:T(512)S(1)} %copy-done.52, pred[512]{0:T(512)(128)(4,1)S(1)} %copy-done.75), kind=kOutput, calls=%fused_computation.1523 | convolution fusion | flops 75759616 | bytes 152064 | tf_op jit(solution)/shard_map/...hv,wv->...hw/dot_general | solution.py:77
  105.1 2.4 %fusion.1 = f32[3,32,1024]{2,1,0:T(8,128)S(1)} fusion(f32[3,32,512]{2,1,0:T(8,128)S(1)} %convolution_bitcast_fusion.1, s32[1024]{0:T(1024)S(1)} %copy-done.47, s32[1024]{0:T(1024)S(1)} %copy-done.48, pred[1024]{0:T(1024)(128)(4,1)S(1)} %copy-done.67), kind=kOutput, calls=%fused_computation.7 | convolution fusion | flops 605028352 | bytes 599040 | tf_op jit(solution)/shard_map/...hv,wv->...hw/dot_general | solution.py:77
  109.8 0.7 convolution_add_fusion.2
  (367 shorter events, 36.8 us)
Async XLA Ops:
  0.0 6.4 %copy-start.39 = (f32[2,16,512]{2,1,0:T(8,128)S(1)}, f32[2,16,512]{2,1,0:T(8,128)}, u32[]{:S(2)}) copy-start(f32[2,16,512]{2,1,0:T(8,128)} %param.5) | copy-start | bytes 196612
  0.0 30.5 %copy-start.60 = (pred[16]{0:T(512)(128)(4,1)}, pred[16]{0:T(512)(128)(4,1)S(1)}, u32[]{:S(2)}) copy-start(pred[16]{0:T(512)(128)(4,1)S(1)} %compare_and_fusion.6) | copy-start | bytes 52
  0.0 30.8 %copy-start.74 = (pred[512]{0:T(512)(128)(4,1)}, pred[512]{0:T(512)(128)(4,1)S(1)}, u32[]{:S(2)}) copy-start(pred[512]{0:T(512)(128)(4,1)S(1)} %fusion.938) | copy-start | bytes 1540
  0.1 7.2 %copy-start.78 = (pred[8]{0:T(512)(128)(4,1)}, pred[8]{0:T(512)(128)(4,1)S(1)}, u32[]{:S(2)}) copy-start(pred[8]{0:T(512)(128)(4,1)S(1)} %compare_and_fusion.5) | copy-start | bytes 28
  0.1 6.3 %copy-start.76 = (pred[256]{0:T(512)(128)(4,1)}, pred[256]{0:T(512)(128)(4,1)S(1)}, u32[]{:S(2)}) copy-start(pred[256]{0:T(512)(128)(4,1)S(1)} %compare_and_fusion.4) | copy-start | bytes 772
  0.2 30.3 %copy-start.62 = (s32[16]{0:T(128)}, s32[16]{0:T(128)S(1)}, u32[]{:S(2)}) copy-start(s32[16]{0:T(128)S(1)} %get-tuple-element.139) | copy-start | bytes 196
  0.2 30.3 %copy-start.64 = (s32[16]{0:T(128)}, s32[16]{0:T(128)S(1)}, u32[]{:S(2)}) copy-start(s32[16]{0:T(128)S(1)} %get-tuple-element.140) | copy-start | bytes 196
  0.3 7.0 %copy-start.68 = (s32[8]{0:T(128)}, s32[8]{0:T(128)S(1)}, u32[]{:S(2)}) copy-start(s32[8]{0:T(128)S(1)} %get-tuple-element.143) | copy-start | bytes 100
  0.3 7.0 %copy-start.70 = (s32[8]{0:T(128)}, s32[8]{0:T(128)S(1)}, u32[]{:S(2)}) copy-start(s32[8]{0:T(128)S(1)} %get-tuple-element.144) | copy-start | bytes 100
  0.3 4.9 %copy-start.56 = (s32[256]{0:T(256)}, s32[256]{0:T(256)S(1)}, u32[]{:S(2)}) copy-start(s32[256]{0:T(256)S(1)} %get-tuple-element.147) | copy-start | bytes 3076
  0.3 4.9 %copy-start.58 = (s32[256]{0:T(256)}, s32[256]{0:T(256)S(1)}, u32[]{:S(2)}) copy-start(s32[256]{0:T(256)S(1)} %get-tuple-element.148) | copy-start | bytes 3076
  0.3 30.5 %copy-start.49 = (s32[512]{0:T(512)}, s32[512]{0:T(512)S(1)}, u32[]{:S(2)}) copy-start(s32[512]{0:T(512)S(1)} %get-tuple-element.141) | copy-start | bytes 6148
  0.4 30.5 %copy-start.51 = (s32[512]{0:T(512)}, s32[512]{0:T(512)S(1)}, u32[]{:S(2)}) copy-start(s32[512]{0:T(512)S(1)} %get-tuple-element.142) | copy-start | bytes 6148
  2.8 7.2 %copy-start.41 = (f32[3,16,512]{2,1,0:T(8,128)S(1)}, f32[3,16,512]{2,1,0:T(8,128)}, u32[]{:S(2)}) copy-start(f32[3,16,512]{2,1,0:T(8,128)} %param.3) | copy-start | bytes 294916
  4.1 5.9 %copy-start.21 = (f32[6,16,512]{2,1,0:T(8,128)S(1)}, f32[6,16,512]{2,1,0:T(8,128)}, u32[]{:S(2)}) copy-start(f32[6,16,512]{2,1,0:T(8,128)} %param.4) | copy-start | bytes 589828
  8.4 34.2 %collective-permute-start.12 = (f32[8,2720]{1,0:T(8,128)S(1)}, f32[8,2720]{1,0:T(8,128)S(1)}, u32[]{:S(2)}, u32[]{:S(2)}) collective-permute-start(f32[8,2720]{1,0:T(8,128)S(1)} %pad_maximum_fusion.9), channel_id=1, source_target_pairs={{0,3},{1,0},{2,1},{3,2},{4,7},{5,4},{6,5},{7,6},{8,11},{9,8},{10,9... | collective-permute-start | bytes 261128 | tf_op jit(solution)/shard_map/ppermute | solution.py:151
  9.4 34.4 %collective-permute-start.11 = (f32[8,2720]{1,0:T(8,128)S(1)}, f32[8,2720]{1,0:T(8,128)S(1)}, u32[]{:S(2)}, u32[]{:S(2)}) collective-permute-start(f32[8,2720]{1,0:T(8,128)S(1)} %pad_maximum_fusion.9), channel_id=1, source_target_pairs={{0,2},{1,3},{2,0},{3,1},{4,6},{5,7},{6,4},{7,5},{8,10},{9,11},{10,... | collective-permute-start | bytes 261128 | tf_op jit(solution)/shard_map/ppermute | solution.py:151
  10.2 11.2 %collective-permute-start = (f32[11,4,512]{2,1,0:T(4,128)S(1)}, f32[11,4,512]{2,1,0:T(4,128)S(1)}, u32[]{:S(2)}, u32[]{:S(2)}) collective-permute-start(f32[11,4,512]{2,1,0:T(4,128)S(1)} %get-tuple-element.94), channel_id=1, source_target_pairs={{0,4},{4,8},{8,12},{1,5},{5,9},{9,13},{2,6},{6,10},{10,14},{3,7},{... | collective-permute-start | bytes 270344 | tf_op jit(solution)/shard_map/ppermute | solution.py:29
  13.6 7.7 %collective-permute-start.1 = (f32[11,4,512]{2,1,0:T(4,128)S(1)}, f32[11,4,512]{2,1,0:T(4,128)S(1)}, u32[]{:S(2)}, u32[]{:S(2)}) collective-permute-start(f32[11,4,512]{2,1,0:T(4,128)S(1)} %get-tuple-element.95), channel_id=1, source_target_pairs={{4,0},{8,4},{12,8},{5,1},{9,5},{13,9},{6,2},{10,6},{14,10},{7,3},{... | collective-permute-start | bytes 270344 | tf_op jit(solution)/shard_map/ppermute | solution.py:31
  21.5 2.8 %collective-permute-start.2 = (f32[11,24,4]{2,1,0:T(8,128)S(1)}, f32[11,24,4]{2,1,0:T(8,128)S(1)}, u32[]{:S(2)}, u32[]{:S(2)}) collective-permute-start(f32[11,24,4]{2,1,0:T(8,128)S(1)} %get-tuple-element.88), channel_id=1, source_target_pairs={{0,1},{1,2},{2,3},{4,5},{5,6},{6,7},{8,9},{9,10},{10,11},{12,13},{... | collective-permute-start | bytes 12680 | tf_op jit(solution)/shard_map/ppermute | solution.py:29
  23.0 4.6 %collective-permute-start.3 = (f32[11,24,4]{2,1,0:T(8,128)S(1)}, f32[11,24,4]{2,1,0:T(8,128)S(1)}, u32[]{:S(2)}, u32[]{:S(2)}) collective-permute-start(f32[11,24,4]{2,1,0:T(8,128)S(1)} %get-tuple-element.89), channel_id=1, source_target_pairs={{1,0},{2,1},{3,2},{5,4},{6,5},{7,6},{9,8},{10,9},{11,10},{13,12},{... | collective-permute-start | bytes 12680 | tf_op jit(solution)/shard_map/ppermute | solution.py:31
  29.8 13.9 %copy-start.18 = (f32[20,516]{1,0:T(8,128)}, f32[20,516]{1,0:T(8,128)S(1)}, u32[]{:S(2)}) copy-start(f32[20,516]{1,0:T(8,128)S(1)} %fusion.256) | copy-start | bytes 123844
  31.4 5.8 %collective-permute-start.6 = (f32[3,2048]{1,0:T(4,128)S(1)}, f32[3,2048]{1,0:T(4,128)S(1)}, u32[]{:S(2)}, u32[]{:S(2)}) collective-permute-start(f32[3,2048]{1,0:T(4,128)S(1)} %bitcast.935), channel_id=1, source_target_pairs={{0,3},{1,0},{2,1},{3,2},{4,7},{5,4},{6,5},{7,6},{8,11},{9,8},{10,9... | collective-permute-start | bytes 73736 | tf_op jit(solution)/shard_map/ppermute | solution.py:151
  31.6 7.3 %collective-permute-start.5 = (f32[3,2048]{1,0:T(4,128)S(1)}, f32[3,2048]{1,0:T(4,128)S(1)}, u32[]{:S(2)}, u32[]{:S(2)}) collective-permute-start(f32[3,2048]{1,0:T(4,128)S(1)} %bitcast.936), channel_id=1, source_target_pairs={{0,2},{1,3},{2,0},{3,1},{4,6},{5,7},{6,4},{7,5},{8,10},{9,11},{10,... | collective-permute-start | bytes 73736 | tf_op jit(solution)/shard_map/ppermute | solution.py:151
  36.6 3.3 %collective-permute-start.4 = (f32[3,2048]{1,0:T(4,128)S(1)}, f32[3,2048]{1,0:T(4,128)S(1)}, u32[]{:S(2)}, u32[]{:S(2)}) collective-permute-start(f32[3,2048]{1,0:T(4,128)S(1)} %bitcast.937), channel_id=1, source_target_pairs={{0,1},{1,2},{2,3},{3,0},{4,5},{5,6},{6,7},{7,4},{8,9},{9,10},{10,1... | collective-permute-start | bytes 73736 | tf_op jit(solution)/shard_map/ppermute | solution.py:151
  37.2 6.6 %collective-permute-start.10 = (f32[8,2720]{1,0:T(8,128)S(1)}, f32[8,2720]{1,0:T(8,128)S(1)}, u32[]{:S(2)}, u32[]{:S(2)}) collective-permute-start(f32[8,2720]{1,0:T(8,128)S(1)} %pad_maximum_fusion.9), channel_id=1, source_target_pairs={{0,1},{1,2},{2,3},{3,0},{4,5},{5,6},{6,7},{7,4},{8,9},{9,10},{10,1... | collective-permute-start | bytes 261128 | tf_op jit(solution)/shard_map/ppermute | solution.py:151
  40.6 9.0 %collective-permute-start.8 = (f32[4,3,2048]{2,1,0:T(4,128)S(1)}, f32[4,3,2048]{2,1,0:T(4,128)S(1)}, u32[]{:S(2)}, u32[]{:S(2)}) collective-permute-start(f32[4,3,2048]{2,1,0:T(4,128)S(1)} %gather_fusion), channel_id=1, source_target_pairs={{0,8},{4,12},{8,0},{12,4},{1,9},{5,13},{9,1},{13,5},{2,10},{6,14},... | collective-permute-start | bytes 294920 | tf_op jit(solution)/shard_map/ppermute | solution.py:151
  40.7 22.2 %collective-permute-start.7 = (f32[4,3,2048]{2,1,0:T(4,128)S(1)}, f32[4,3,2048]{2,1,0:T(4,128)S(1)}, u32[]{:S(2)}, u32[]{:S(2)}) collective-permute-start(f32[4,3,2048]{2,1,0:T(4,128)S(1)} %gather_fusion), channel_id=1, source_target_pairs={{0,4},{4,8},{8,12},{12,0},{1,5},{5,9},{9,13},{13,1},{2,6},{6,10},{... | collective-permute-start | bytes 294920 | tf_op jit(solution)/shard_map/ppermute | solution.py:151
  42.6 24.7 %collective-permute-start.9 = (f32[4,3,2048]{2,1,0:T(4,128)S(1)}, f32[4,3,2048]{2,1,0:T(4,128)S(1)}, u32[]{:S(2)}, u32[]{:S(2)}) collective-permute-start(f32[4,3,2048]{2,1,0:T(4,128)S(1)} %gather_fusion), channel_id=1, source_target_pairs={{0,12},{4,0},{8,4},{12,8},{1,13},{5,1},{9,5},{13,9},{2,14},{6,2},{... | collective-permute-start | bytes 294920 | tf_op jit(solution)/shard_map/ppermute | solution.py:151
  44.4 30.8 %collective-permute-start.14 = (f32[4,8,2720]{2,1,0:T(8,128)S(1)}, f32[4,8,2720]{2,1,0:T(8,128)S(1)}, u32[]{:S(2)}, u32[]{:S(2)}) collective-permute-start(f32[4,8,2720]{2,1,0:T(8,128)S(1)} %gather_fusion.2), channel_id=1, source_target_pairs={{0,8},{4,12},{8,0},{12,4},{1,9},{5,13},{9,1},{13,5},{2,10},{6,14},... | collective-permute-start | bytes 1044488 | tf_op jit(solution)/shard_map/ppermute | solution.py:151
  48.2 36.6 %collective-permute-start.13 = (f32[4,8,2720]{2,1,0:T(8,128)S(1)}, f32[4,8,2720]{2,1,0:T(8,128)S(1)}, u32[]{:S(2)}, u32[]{:S(2)}) collective-permute-start(f32[4,8,2720]{2,1,0:T(8,128)S(1)} %gather_fusion.2), channel_id=1, source_target_pairs={{0,4},{4,8},{8,12},{12,0},{1,5},{5,9},{9,13},{13,1},{2,6},{6,10},{... | collective-permute-start | bytes 1044488 | tf_op jit(solution)/shard_map/ppermute | solution.py:151
  49.7 35.0 %collective-permute-start.15 = (f32[4,8,2720]{2,1,0:T(8,128)S(1)}, f32[4,8,2720]{2,1,0:T(8,128)S(1)}, u32[]{:S(2)}, u32[]{:S(2)}) collective-permute-start(f32[4,8,2720]{2,1,0:T(8,128)S(1)} %gather_fusion.2), channel_id=1, source_target_pairs={{0,12},{4,0},{8,4},{12,8},{1,13},{5,1},{9,5},{13,9},{2,14},{6,2},{... | collective-permute-start | bytes 1044488 | tf_op jit(solution)/shard_map/ppermute | solution.py:151
  (65 other events, 123.7 us)

commit v4 on v2

--- a/solution.py
+++ b/solution.py
@@ -148,14 +148,21 @@
     count_rows = lax.axis_size(ROWS)
     count_cols = lax.axis_size(COLS)
     planes = blocks[0].shape[0]
-    flat = jnp.concatenate([b.reshape(planes, -1) for b in blocks], axis=1)
+    runs = [-(-b.shape[1] * b.shape[2] // 128) * 128 for b in blocks]
+    flat = jnp.concatenate(
+        [
+            jnp.pad(b.reshape(planes, -1), ((0, 0), (0, run - b.shape[1] * b.shape[2])))
+            for b, run in zip(blocks, runs)
+        ],
+        axis=1,
+    )
     stacked = lax.all_gather(flat, GRID, axis=0, tiled=False)
     grids = []
     offset = 0
-    for b in blocks:
+    for b, run in zip(blocks, runs):
         _, height, width = b.shape
         part = stacked[:, :, offset:offset + height * width]
-        offset += height * width
+        offset += run
         part = part.reshape(count_rows, count_cols, planes, height, width)
         whole = part.transpose(2, 0, 3, 1, 4).reshape(
             planes, count_rows * height, count_cols * width

time: 90.3 us -> 90.3 us (level)
  no operation moved by 1% of the time
where the time goes in v4:
time: 90.3 us; the launch traced here: 89.9 us
  blocking collectives  24.1 us (27%)
  matrix products  16.5 us (18%)
  between operations  14.4 us (16%)
  other arithmetic  10.4 us (12%)
  starting transfers between devices  8.82 us (10%)
  waiting for transfers between devices  8.6 us (10%)
  local copies, waits for them, and re-layouts  7.08 us (8%)
    all_gather x1, blocking collectives, gather_grids(): stacked = lax.all_gather(flat, GRID, axis=0, tiled=False)  24.1 us
    ppermute x2, waiting for transfers between devices, with_halo(): lax.ppermute(head, axis, [(i + 1, i) for i in range(ends)])  7.94 us
    ppermute x2, starting transfers between devices, with_halo(): lax.ppermute(tail, axis, [(i, i + 1) for i in range(ends)])  6.23 us
    dot_general x6, matrix products, prolong(): return jnp.einsum('...hv,wv->...hw', taller, pairs(width), precision=HIGH)  5.65 us
    dot_general x16, matrix products, sum_cols(): return jnp.einsum('...hw,wv->...hv', x, m, precision=HIGH)  5.06 us
    dot_general x16, matrix products, sum_rows(): return jnp.einsum('...hw,hv->...vw', x, m, precision=HIGH)  4.34 us
    slice x4, local copies, waits for them, and re-layouts, gather_grids(): part = stacked[:, :, offset:offset + height * width]  3.97 us
    ppermute x2, starting transfers between devices, with_halo(): lax.ppermute(head, axis, [(i + 1, i) for i in range(ends)])  2.58 us
  transfers between devices with their start and end apart: 5, of which 3 were waited for; matrix products, arithmetic and copies ran while one was open for 4% of the time, Pallas kernels for 0%

profile of v4, /device:TPU:0, one launch (start us, length us, event | category | flops | bytes accessed | tf_op | source)
XLA Modules:
  0.0 89.9 jit_solution(15207737289644031752)
XLA Ops:
  6.8 1.0 %fusion.490 = f32[8,512]{1,0:T(8,128)S(1)} fusion(f32[2,16,512]{2,1,0:T(8,128)} %param.5, s32[8]{0:T(128)S(1)} %multiply_add_fusion.6), kind=kOutput, calls=%fused_computation.814 | convolution fusion | flops 786560 | bytes 49184 | tf_op jit(solution)/shard_map/...hw,hv->...vw/dot_general | solution.py:55
  7.7 0.4 fusion.11
  9.3 1.1 %convolution_bitcast_fusion.2 = f32[6,8,512]{2,1,0:T(8,128)S(1)} fusion(f32[6,16,512]{2,1,0:T(8,128)} %param.4, s32[16]{0:T(128)S(1)} %get-tuple-element.139, s32[16]{0:T(128)S(1)} %get-tuple-element.140, pred[16]{0:T(512)(128)(4,1)S(1)} %compare_and_fusion.6), kind=kOutput, calls=%fused_computation.6 | convolution fusion | flops 4718848 | bytes 295056 | tf_op jit(solution)/shard_map/...hw,hv->...vw/dot_general | solution.py:55
  10.4 0.5 fusion.975
  13.8 0.7 select_maximum_fusion
  14.6 4.9 %collective-permute-start = (f32[11,4,512]{2,1,0:T(4,128)S(1)}, f32[11,4,512]{2,1,0:T(4,128)S(1)}, u32[]{:S(2)}, u32[]{:S(2)}) collective-permute-start(f32[11,4,512]{2,1,0:T(4,128)S(1)} %get-tuple-element.94), channel_id=1, source_target_pairs={{0,4},{4,8},{8,12},{1,5},{5,9},{9,13},{2,6},{6,10},{10,14},{3,7},{... | collective-permute-start | bytes 270344 | tf_op jit(solution)/shard_map/ppermute | solution.py:29
  19.5 1.3 %collective-permute-start.1 = (f32[11,4,512]{2,1,0:T(4,128)S(1)}, f32[11,4,512]{2,1,0:T(4,128)S(1)}, u32[]{:S(2)}, u32[]{:S(2)}) collective-permute-start(f32[11,4,512]{2,1,0:T(4,128)S(1)} %get-tuple-element.95), channel_id=1, source_target_pairs={{4,0},{8,4},{12,8},{5,1},{9,5},{13,9},{6,2},{10,6},{14,10},{7,3},{... | collective-permute-start | bytes 270344 | tf_op jit(solution)/shard_map/ppermute | solution.py:31
  21.0 0.6 collective-permute-done
  21.6 4.3 %collective-permute-done.1 = f32[11,4,512]{2,1,0:T(4,128)S(1)} collective-permute-done((f32[11,4,512]{2,1,0:T(4,128)S(1)}, f32[11,4,512]{2,1,0:T(4,128)S(1)}, u32[]{:S(2)}, u32[]{:S(2)}) %collective-permute-start.1) | collective-permute-done | bytes 90144 | tf_op jit(solution)/shard_map/ppermute | solution.py:31
  26.1 1.3 %collective-permute-start.2 = (f32[11,24,4]{2,1,0:T(8,128)S(1)}, f32[11,24,4]{2,1,0:T(8,128)S(1)}, u32[]{:S(2)}, u32[]{:S(2)}) collective-permute-start(f32[11,24,4]{2,1,0:T(8,128)S(1)} %get-tuple-element.88), channel_id=1, source_target_pairs={{0,1},{1,2},{2,3},{4,5},{5,6},{6,7},{8,9},{9,10},{10,11},{12,13},{... | collective-permute-start | bytes 12680 | tf_op jit(solution)/shard_map/ppermute | solution.py:29
  27.4 1.3 %collective-permute-start.3 = (f32[11,24,4]{2,1,0:T(8,128)S(1)}, f32[11,24,4]{2,1,0:T(8,128)S(1)}, u32[]{:S(2)}, u32[]{:S(2)}) collective-permute-start(f32[11,24,4]{2,1,0:T(8,128)S(1)} %get-tuple-element.89), channel_id=1, source_target_pairs={{1,0},{2,1},{3,2},{5,4},{6,5},{7,6},{9,8},{10,9},{11,10},{13,12},{... | collective-permute-start | bytes 12680 | tf_op jit(solution)/shard_map/ppermute | solution.py:31
  28.7 3.6 %collective-permute-done.3 = f32[11,24,4]{2,1,0:T(8,128)S(1)} collective-permute-done((f32[11,24,4]{2,1,0:T(8,128)S(1)}, f32[11,24,4]{2,1,0:T(8,128)S(1)}, u32[]{:S(2)}, u32[]{:S(2)}) %collective-permute-start.3) | collective-permute-done | bytes 4256 | tf_op jit(solution)/shard_map/ppermute | solution.py:31
  32.4 0.4 pad_maximum_fusion
  34.9 0.4 fusion.977
  35.4 24.1 %all_gather.13 = f32[16,3,2048]{2,1,0:T(4,128)S(1)} all-gather(f32[1,3,2048]{2,1,0:T(4,128)S(1)} %all_gather.12), channel_id=1, replica_groups=mesh['groups'=2,'tiles'=4,'band'=2,'stokes'=2] {'tiles','band','stokes'}, dimensions={0}, use_global_device_ids=true | all-gather | bytes 417792 | tf_op jit(solution)/shard_map/all_gather | solution.py:159
  60.0 0.8 slice.1949
  60.8 0.8 slice.1937
  61.6 1.0 %slice.1925 = f32[16,8,512]{2,1,0:T(8,128)S(1)} slice(f32[16,8,2816]{2,1,0:T(8,128)} %bitcast.874), slice={[0:16], [0:8], [2048:2560]} | slice | bytes 524288 | tf_op jit(solution)/shard_map/slice | solution.py:164
  62.6 1.3 %slice.1913 = f32[16,8,2048]{2,1,0:T(8,128)S(1)} slice(f32[16,8,2816]{2,1,0:T(8,128)} %bitcast.875), slice={[0:16], [0:8], [0:2048]} | slice | bytes 2097152 | tf_op jit(solution)/shard_map/slice | solution.py:164
  65.6 0.3 copy.173
  66.8 0.5 fusion.74
  67.3 0.3 fusion.84
  67.9 1.0 %fusion.3 = f32[3,16,512]{2,1,0:T(8,128)S(1)} fusion(f32[3,16,1024]{2,1,0:T(8,128)S(1)} %convolution_bitcast_fusion.1, s32[1024]{0:T(1024)S(1)} %get-tuple-element.155, s32[1024]{0:T(1024)S(1)} %get-tuple-element.156, pred[1024]{0:T(1024)(128)(4,1)S(1)} %fusion.720), kind=kOutput, calls=%fused_computation.3 | convolution fusion | flops 303038464 | bytes 304128 | tf_op jit(solution)/shard_map/...hw,wv->...hv/dot_general | solution.py:59
  69.5 0.4 fusion.973
  72.7 0.9 %fusion.971 = f32[3,16,512]{2,1,0:T(8,128)S(1)} fusion(f32[3,16,256]{2,1,0:T(8,128)S(1)} %convolution_bitcast_fusion.3, s32[512]{0:T(512)S(1)} %get-tuple-element.141, s32[512]{0:T(512)S(1)} %get-tuple-element.142, pred[512]{0:T(512)(128)(4,1)S(1)} %fusion.926), kind=kOutput, calls=%fused_computation.1498 | convolution fusion | flops 75759616 | bytes 152064 | tf_op jit(solution)/shard_map/...hv,wv->...hw/dot_general | solution.py:77
  74.4 2.4 %fusion.1 = f32[3,32,1024]{2,1,0:T(8,128)S(1)} fusion(f32[3,32,512]{2,1,0:T(8,128)S(1)} %convolution_bitcast_fusion, s32[1024]{0:T(1024)S(1)} %get-tuple-element.155, s32[1024]{0:T(1024)S(1)} %get-tuple-element.156, pred[1024]{0:T(1024)(128)(4,1)S(1)} %fusion.720), kind=kOutput, calls=%fused_computation.2 | convolution fusion | flops 605028352 | bytes 599040 | tf_op jit(solution)/shard_map/...hv,wv->...hw/dot_general | solution.py:77
  77.1 0.5 fusion.142
  78.7 0.7 convolution_add_fusion.2
  79.4 0.7 convolution_add_fusion
  80.0 0.7 convolution_add_fusion.1
  81.0 0.3 fusion.211
  82.4 0.6 pad_maximum_fusion.4
  (179 shorter events, 16.1 us)
Async XLA Ops:
  6.5 5.4 %copy-start.1 = (f32[2,16,512]{2,1,0:T(8,128)S(1)}, f32[2,16,512]{2,1,0:T(8,128)}, u32[]{:S(2)}) copy-start(f32[2,16,512]{2,1,0:T(8,128)} %param.5) | copy-start | bytes 196612
  6.5 53.4 %all-gather.3.cloned.1.call-start = ((), (), s32[]{:S(2)}) async-start(), calls=%async_computation | async-start | bytes 1531904 | tf_op jit(solution)/shard_map/all_gather | solution.py:159
  7.7 6.7 %copy-start.2 = (f32[3,16,512]{2,1,0:T(8,128)S(1)}, f32[3,16,512]{2,1,0:T(8,128)}, u32[]{:S(2)}) copy-start(f32[3,16,512]{2,1,0:T(8,128)} %param.3) | copy-start | bytes 294916
  7.7 6.8 %copy-start = (f32[6,16,512]{2,1,0:T(8,128)S(1)}, f32[6,16,512]{2,1,0:T(8,128)}, u32[]{:S(2)}) copy-start(f32[6,16,512]{2,1,0:T(8,128)} %param.4) | copy-start | bytes 589828
  14.6 7.1 %collective-permute-start = (f32[11,4,512]{2,1,0:T(4,128)S(1)}, f32[11,4,512]{2,1,0:T(4,128)S(1)}, u32[]{:S(2)}, u32[]{:S(2)}) collective-permute-start(f32[11,4,512]{2,1,0:T(4,128)S(1)} %get-tuple-element.94), channel_id=1, source_target_pairs={{0,4},{4,8},{8,12},{1,5},{5,9},{9,13},{2,6},{6,10},{10,14},{3,7},{... | collective-permute-start | bytes 270344 | tf_op jit(solution)/shard_map/ppermute | solution.py:29
  19.5 6.4 %collective-permute-start.1 = (f32[11,4,512]{2,1,0:T(4,128)S(1)}, f32[11,4,512]{2,1,0:T(4,128)S(1)}, u32[]{:S(2)}, u32[]{:S(2)}) collective-permute-start(f32[11,4,512]{2,1,0:T(4,128)S(1)} %get-tuple-element.95), channel_id=1, source_target_pairs={{4,0},{8,4},{12,8},{5,1},{9,5},{13,9},{6,2},{10,6},{14,10},{7,3},{... | collective-permute-start | bytes 270344 | tf_op jit(solution)/shard_map/ppermute | solution.py:31
  26.1 2.6 %collective-permute-start.2 = (f32[11,24,4]{2,1,0:T(8,128)S(1)}, f32[11,24,4]{2,1,0:T(8,128)S(1)}, u32[]{:S(2)}, u32[]{:S(2)}) collective-permute-start(f32[11,24,4]{2,1,0:T(8,128)S(1)} %get-tuple-element.88), channel_id=1, source_target_pairs={{0,1},{1,2},{2,3},{4,5},{5,6},{6,7},{8,9},{9,10},{10,11},{12,13},{... | collective-permute-start | bytes 12680 | tf_op jit(solution)/shard_map/ppermute | solution.py:29
  27.4 5.0 %collective-permute-start.3 = (f32[11,24,4]{2,1,0:T(8,128)S(1)}, f32[11,24,4]{2,1,0:T(8,128)S(1)}, u32[]{:S(2)}, u32[]{:S(2)}) collective-permute-start(f32[11,24,4]{2,1,0:T(8,128)S(1)} %get-tuple-element.89), channel_id=1, source_target_pairs={{1,0},{2,1},{3,2},{5,4},{6,5},{7,6},{9,8},{10,9},{11,10},{13,12},{... | collective-permute-start | bytes 12680 | tf_op jit(solution)/shard_map/ppermute | solution.py:31
Sparse Core Ops, SparseCore 0:
  14.6 43.2 all-gather.2

commit v5 on v4

--- a/solution.py
+++ b/solution.py
@@ -144,6 +144,16 @@
     return gather_grids([block])[0]
 
 
+def gather_axis(x, axis):
+    count = lax.axis_size(axis)
+    me = lax.axis_index(axis)
+    pieces = [x] + [
+        lax.ppermute(x, axis, [(i, (i + k) % count) for i in range(count)]) for k in range(1, count)
+    ]
+    order = (me - jnp.arange(count)) % count
+    return jnp.take(jnp.stack(pieces), order, axis=0, mode="clip")
+
+
 def gather_grids(blocks):
     count_rows = lax.axis_size(ROWS)
     count_cols = lax.axis_size(COLS)
@@ -156,7 +166,9 @@
         ],
         axis=1,
     )
-    stacked = lax.all_gather(flat, GRID, axis=0, tiled=False)
+    paired = gather_axis(flat, "stokes")
+    stacked = lax.all_gather(paired, ("tiles", "band"), axis=0, tiled=False)
+    stacked = stacked.reshape((count_rows * count_cols,) + flat.shape)
     grids = []
     offset = 0
     for b, run in zip(blocks, runs):

time: 90.3 us -> 108 us (1.20)
  blocking collectives: 24.1 us -> 32.4 us
  waiting for transfers between devices: 8.6 us -> 14.7 us
  starting transfers between devices: 8.82 us -> 12.6 us
    all_gather x1, blocking collectives: 24.1 us -> 32.4 us  [gather_grids(): stacked = lax.all_gather(paired, ('tiles', 'band'), axis=0, tiled=False)]
    all_gather x1, waiting for transfers between devices: 0.02 us -> 6.44 us  [gather_grids(): stacked = lax.all_gather(paired, ('tiles', 'band'), axis=0, tiled=False)]
    ppermute x0 -> x2, starting transfers between devices: none -> 4.16 us  [gather_axis(): lax.ppermute(x, axis, [(i, (i + k) % count) for i in range(count)])]
    gather x0 -> x2, local copies, waits for them, and re-layouts: none -> 1.82 us  [gather_axis(): return jnp.take(jnp.stack(pieces), order, axis=0, mode='clip')]
    slice x4 -> x6, local copies, waits for them, and re-layouts: 3.97 us -> 2.31 us  [gather_grids(): part = stacked[:, :, offset:offset + height * width]]
    ppermute x2, waiting for transfers between devices: 7.94 us -> 6.49 us  [with_halo(): lax.ppermute(head, axis, [(i + 1, i) for i in range(ends)])]
  transfers between devices with their start and end apart: 5 -> 7, of which waited for: 3 -> 5; matrix products, arithmetic and copies ran while one was open for 4% -> 5% of each run, Pallas kernels for 0% -> 0%
where the time goes in v5:
time: 108 us; the launch traced here: 107 us
  blocking collectives  32.4 us (30%)
  matrix products  16.5 us (15%)
  waiting for transfers between devices  14.7 us (14%)
  between operations  14.3 us (13%)
  starting transfers between devices  12.6 us (12%)
  other arithmetic  9.77 us (9%)
  local copies, waits for them, and re-layouts  7.12 us (7%)
    all_gather x1, blocking collectives, gather_grids(): stacked = lax.all_gather(paired, ('tiles', 'band'), axis=0, tiled=False)  32.4 us
    ppermute x2, waiting for transfers between devices, with_halo(): lax.ppermute(head, axis, [(i + 1, i) for i in range(ends)])  6.49 us
    all_gather x1, waiting for transfers between devices, gather_grids(): stacked = lax.all_gather(paired, ('tiles', 'band'), axis=0, tiled=False)  6.44 us
    ppermute x2, starting transfers between devices, with_halo(): lax.ppermute(tail, axis, [(i, i + 1) for i in range(ends)])  5.8 us
    dot_general x6, matrix products, prolong(): return jnp.einsum('...hv,wv->...hw', taller, pairs(width), precision=HIGH)  5.65 us
    dot_general x16, matrix products, sum_cols(): return jnp.einsum('...hw,wv->...hv', x, m, precision=HIGH)  5.09 us
    dot_general x16, matrix products, sum_rows(): return jnp.einsum('...hw,hv->...vw', x, m, precision=HIGH)  4.33 us
    ppermute x2, starting transfers between devices, gather_axis(): lax.ppermute(x, axis, [(i, (i + k) % count) for i in range(count)])  4.16 us
  transfers between devices with their start and end apart: 7, of which 5 were waited for; matrix products, arithmetic and copies ran while one was open for 5% of the time, Pallas kernels for 0%

profile of v5, /device:TPU:0, one launch (start us, length us, event | category | flops | bytes accessed | tf_op | source)
XLA Modules:
  0.0 107.3 jit_solution(17266305421276381083)
XLA Ops:
  6.8 1.0 fusion.490
  7.7 0.4 fusion.11
  9.3 1.1 %convolution_bitcast_fusion.2 = f32[6,8,512]{2,1,0:T(8,128)S(1)} fusion(f32[6,16,512]{2,1,0:T(8,128)} %param.4, s32[16]{0:T(128)S(1)} %get-tuple-element.139, s32[16]{0:T(128)S(1)} %get-tuple-element.140, pred[16]{0:T(512)(128)(4,1)S(1)} %compare_and_fusion.6), kind=kOutput, calls=%fused_computation.8 | convolution fusion | flops 4718848 | bytes 295056 | tf_op jit(solution)/shard_map/...hw,hv->...vw/dot_general | solution.py:55
  10.4 0.5 fusion.977
  13.8 0.5 collective-permute-start.5
  14.4 4.5 %collective-permute-start = (f32[11,4,512]{2,1,0:T(4,128)S(1)}, f32[11,4,512]{2,1,0:T(4,128)S(1)}, u32[]{:S(2)}, u32[]{:S(2)}) collective-permute-start(f32[11,4,512]{2,1,0:T(4,128)S(1)} %get-tuple-element.94), channel_id=1, source_target_pairs={{0,4},{4,8},{8,12},{1,5},{5,9},{9,13},{2,6},{6,10},{10,14},{3,7},{... | collective-permute-start | bytes 270344 | tf_op jit(solution)/shard_map/ppermute | solution.py:29
  19.0 1.3 %collective-permute-start.1 = (f32[11,4,512]{2,1,0:T(4,128)S(1)}, f32[11,4,512]{2,1,0:T(4,128)S(1)}, u32[]{:S(2)}, u32[]{:S(2)}) collective-permute-start(f32[11,4,512]{2,1,0:T(4,128)S(1)} %get-tuple-element.95), channel_id=1, source_target_pairs={{4,0},{8,4},{12,8},{5,1},{9,5},{13,9},{6,2},{10,6},{14,10},{7,3},{... | collective-permute-start | bytes 270344 | tf_op jit(solution)/shard_map/ppermute | solution.py:31
  20.5 0.9 collective-permute-done
  21.5 4.1 %collective-permute-done.1 = f32[11,4,512]{2,1,0:T(4,128)S(1)} collective-permute-done((f32[11,4,512]{2,1,0:T(4,128)S(1)}, f32[11,4,512]{2,1,0:T(4,128)S(1)}, u32[]{:S(2)}, u32[]{:S(2)}) %collective-permute-start.1) | collective-permute-done | bytes 90144 | tf_op jit(solution)/shard_map/ppermute | solution.py:31
  25.7 1.3 %collective-permute-start.2 = (f32[11,24,4]{2,1,0:T(8,128)S(1)}, f32[11,24,4]{2,1,0:T(8,128)S(1)}, u32[]{:S(2)}, u32[]{:S(2)}) collective-permute-start(f32[11,24,4]{2,1,0:T(8,128)S(1)} %get-tuple-element.88), channel_id=1, source_target_pairs={{0,1},{1,2},{2,3},{4,5},{5,6},{6,7},{8,9},{9,10},{10,11},{12,13},{... | collective-permute-start | bytes 12680 | tf_op jit(solution)/shard_map/ppermute | solution.py:29
  27.0 1.3 %collective-permute-start.3 = (f32[11,24,4]{2,1,0:T(8,128)S(1)}, f32[11,24,4]{2,1,0:T(8,128)S(1)}, u32[]{:S(2)}, u32[]{:S(2)}) collective-permute-start(f32[11,24,4]{2,1,0:T(8,128)S(1)} %get-tuple-element.89), channel_id=1, source_target_pairs={{1,0},{2,1},{3,2},{5,4},{6,5},{7,6},{9,8},{10,9},{11,10},{13,12},{... | collective-permute-start | bytes 12680 | tf_op jit(solution)/shard_map/ppermute | solution.py:31
  28.3 1.2 %gather_fusion.1 = f32[2,8,2816]{2,1,0:T(8,128)} fusion(f32[2,8,2816]{2,1,0:T(8,128)S(1)} %pad_maximum_fusion.1, s32[1024]{0:T(1024)S(1)} %pad_clamp_fusion), kind=kCustom, calls=%fused_computation.1 | custom fusion | bytes 360456 | tf_op jit(solution)/shard_map/jit(_take)/gather | solution.py:154
  29.6 2.4 %collective-permute-done.3 = f32[11,24,4]{2,1,0:T(8,128)S(1)} collective-permute-done((f32[11,24,4]{2,1,0:T(8,128)S(1)}, f32[11,24,4]{2,1,0:T(8,128)S(1)}, u32[]{:S(2)}, u32[]{:S(2)}) %collective-permute-start.3) | collective-permute-done | bytes 4256 | tf_op jit(solution)/shard_map/ppermute | solution.py:31
  34.6 0.5 fusion.979
  35.1 3.6 %collective-permute-start.4 = (f32[3,2048]{1,0:T(4,128)S(1)}, f32[3,2048]{1,0:T(4,128)S(1)}, u32[]{:S(2)}, u32[]{:S(2)}) collective-permute-start(f32[3,2048]{1,0:T(4,128)S(1)} %bitcast.918), channel_id=1, source_target_pairs={{0,1},{1,0},{2,3},{3,2},{4,5},{5,4},{6,7},{7,6},{8,9},{9,8},{10,11... | collective-permute-start | bytes 73736 | tf_op jit(solution)/shard_map/ppermute | solution.py:151
  38.7 0.8 collective-permute-done.4
  39.6 0.6 gather_fusion
  40.2 32.4 %all-gather = f32[16,3,2048]{2,1,0:T(4,128)S(1)} all-gather(f32[2,3,2048]{2,1,0:T(4,128)S(1)} %gather_fusion), channel_id=2, replica_groups=mesh['groups'=2,'tiles'=4,'band'=2,'stokes'=2] {'tiles','band'}, dimensions={0}, use_global_device_ids=true | all-gather | bytes 442368 | tf_op jit(solution)/shard_map/all_gather | solution.py:170
  72.9 6.4 %all-gather.4.cloned.1.call-done = f32[16,8,2816]{2,1,0:T(8,128)} async-done(((f32[2,8,2816]{2,1,0:T(8,128)}), f32[16,8,2816]{2,1,0:T(8,128)}) %all-gather.4.cloned.1.call-update) | async-done | bytes 1441808 | tf_op jit(solution)/shard_map/all_gather | solution.py:170
  79.3 0.8 slice.1941
  81.1 0.9 slice.1953
  83.0 0.6 slice-done.1
  84.3 0.5 fusion.74
  85.4 1.0 fusion.3
  87.0 0.4 fusion.975
  90.2 0.9 fusion.973
  91.9 2.4 %fusion.1 = f32[3,32,1024]{2,1,0:T(8,128)S(1)} fusion(f32[3,32,512]{2,1,0:T(8,128)S(1)} %convolution_bitcast_fusion, s32[1024]{0:T(1024)S(1)} %get-tuple-element.155, s32[1024]{0:T(1024)S(1)} %get-tuple-element.156, pred[1024]{0:T(1024)(128)(4,1)S(1)} %fusion.720), kind=kOutput, calls=%fused_computation.4 | convolution fusion | flops 605028352 | bytes 599040 | tf_op jit(solution)/shard_map/...hv,wv->...hw/dot_general | solution.py:77
  94.6 0.5 fusion.142
  96.1 0.7 convolution_add_fusion.2
  96.8 0.7 convolution_add_fusion
  97.5 0.7 convolution_add_fusion.1
  99.8 0.6 pad_maximum_fusion.5
  (179 shorter events, 17.5 us)
Async XLA Ops:
  6.5 5.4 %copy-start.1 = (f32[2,16,512]{2,1,0:T(8,128)S(1)}, f32[2,16,512]{2,1,0:T(8,128)}, u32[]{:S(2)}) copy-start(f32[2,16,512]{2,1,0:T(8,128)} %param.5) | copy-start | bytes 196612
  6.5 7.8 %copy-start.2 = (f32[3,16,512]{2,1,0:T(8,128)S(1)}, f32[3,16,512]{2,1,0:T(8,128)}, u32[]{:S(2)}) copy-start(f32[3,16,512]{2,1,0:T(8,128)} %param.3) | copy-start | bytes 294916
  6.5 72.8 %all-gather.4.cloned.1.call-start = ((), (), s32[]{:S(2)}) async-start(), calls=%async_computation | async-start | bytes 1622016 | tf_op jit(solution)/shard_map/all_gather | solution.py:170
  7.7 6.6 %copy-start = (f32[6,16,512]{2,1,0:T(8,128)S(1)}, f32[6,16,512]{2,1,0:T(8,128)}, u32[]{:S(2)}) copy-start(f32[6,16,512]{2,1,0:T(8,128)} %param.4) | copy-start | bytes 589828
  13.8 14.5 %collective-permute-start.5 = (f32[8,2816]{1,0:T(8,128)S(1)}, f32[8,2816]{1,0:T(8,128)S(1)}, u32[]{:S(2)}, u32[]{:S(2)}) collective-permute-start(f32[8,2816]{1,0:T(8,128)S(1)} %select_maximum_fusion), channel_id=1, source_target_pairs={{0,1},{1,0},{2,3},{3,2},{4,5},{5,4},{6,7},{7,6},{8,9},{9,8},{10,11... | collective-permute-start | bytes 270344 | tf_op jit(solution)/shard_map/ppermute | solution.py:151
  14.4 7.0 %collective-permute-start = (f32[11,4,512]{2,1,0:T(4,128)S(1)}, f32[11,4,512]{2,1,0:T(4,128)S(1)}, u32[]{:S(2)}, u32[]{:S(2)}) collective-permute-start(f32[11,4,512]{2,1,0:T(4,128)S(1)} %get-tuple-element.94), channel_id=1, source_target_pairs={{0,4},{4,8},{8,12},{1,5},{5,9},{9,13},{2,6},{6,10},{10,14},{3,7},{... | collective-permute-start | bytes 270344 | tf_op jit(solution)/shard_map/ppermute | solution.py:29
  19.0 6.6 %collective-permute-start.1 = (f32[11,4,512]{2,1,0:T(4,128)S(1)}, f32[11,4,512]{2,1,0:T(4,128)S(1)}, u32[]{:S(2)}, u32[]{:S(2)}) collective-permute-start(f32[11,4,512]{2,1,0:T(4,128)S(1)} %get-tuple-element.95), channel_id=1, source_target_pairs={{4,0},{8,4},{12,8},{5,1},{9,5},{13,9},{6,2},{10,6},{14,10},{7,3},{... | collective-permute-start | bytes 270344 | tf_op jit(solution)/shard_map/ppermute | solution.py:31
  25.7 3.9 %collective-permute-start.2 = (f32[11,24,4]{2,1,0:T(8,128)S(1)}, f32[11,24,4]{2,1,0:T(8,128)S(1)}, u32[]{:S(2)}, u32[]{:S(2)}) collective-permute-start(f32[11,24,4]{2,1,0:T(8,128)S(1)} %get-tuple-element.88), channel_id=1, source_target_pairs={{0,1},{1,2},{2,3},{4,5},{5,6},{6,7},{8,9},{9,10},{10,11},{12,13},{... | collective-permute-start | bytes 12680 | tf_op jit(solution)/shard_map/ppermute | solution.py:29
  27.0 5.0 %collective-permute-start.3 = (f32[11,24,4]{2,1,0:T(8,128)S(1)}, f32[11,24,4]{2,1,0:T(8,128)S(1)}, u32[]{:S(2)}, u32[]{:S(2)}) collective-permute-start(f32[11,24,4]{2,1,0:T(8,128)S(1)} %get-tuple-element.89), channel_id=1, source_target_pairs={{1,0},{2,1},{3,2},{5,4},{6,5},{7,6},{9,8},{10,9},{11,10},{13,12},{... | collective-permute-start | bytes 12680 | tf_op jit(solution)/shard_map/ppermute | solution.py:31
  35.1 4.5 %collective-permute-start.4 = (f32[3,2048]{1,0:T(4,128)S(1)}, f32[3,2048]{1,0:T(4,128)S(1)}, u32[]{:S(2)}, u32[]{:S(2)}) collective-permute-start(f32[3,2048]{1,0:T(4,128)S(1)} %bitcast.918), channel_id=1, source_target_pairs={{0,1},{1,0},{2,3},{3,2},{4,5},{5,4},{6,7},{7,6},{8,9},{9,8},{10,11... | collective-permute-start | bytes 73736 | tf_op jit(solution)/shard_map/ppermute | solution.py:151
  80.4 2.2 %slice-start = ((f32[16,8,2816]{2,1,0:T(8,128)}), f32[16,8,2048]{2,1,0:T(8,128)S(1)}, s32[]{:S(2)}) async-start(f32[16,8,2816]{2,1,0:T(8,128)} %all-gather.4.cloned.1.call-done), calls=%async_computation.1 | async-start | bytes 2097152 | tf_op jit(solution)/shard_map/slice | solution.py:176
  82.6 1.0 slice-start.1
Sparse Core Ops, SparseCore 0:
  29.7 49.5 all-gather.3

commit v6 on v4

--- a/solution.py
+++ b/solution.py
@@ -234,18 +234,49 @@
     return iterate
 
 
+def spans(n, pick_last):
+    mats = []
+    for level in range(1, LEVELS):
+        size = 1 << level
+        rows = lax.broadcasted_iota(jnp.int32, (n, n // size), 0)
+        cols = lax.broadcasted_iota(jnp.int32, (n, n // size), 1)
+        hit = (rows == cols * size + size - 1) if pick_last else (rows // size == cols)
+        mats.append(hit.astype(jnp.float32))
+    return jnp.concatenate(mats, axis=1)
+
+
+def hierarchy_of(noise, down, right):
+    height, width = down.shape
+    row_sum, row_last = spans(height, False), spans(height, True)
+    col_sum, col_last = spans(width, False), spans(width, True)
+    tall = jnp.concatenate(
+        [
+            jnp.einsum("phw,hv->pvw", noise, row_sum, precision=HIGH),
+            jnp.einsum("hw,hv->vw", down, row_last, precision=HIGH)[None],
+        ]
+    )
+    both = jnp.einsum("pvw,wu->pvu", tall, col_sum, precision=HIGH)
+    wide = jnp.einsum(
+        "hv,hw->vw", row_sum, jnp.einsum("hw,wu->hu", right, col_last, precision=HIGH),
+        precision=HIGH,
+    )
+    noises, downs, rights = [noise], [down], [right]
+    row, col = 0, 0
+    for level in range(1, LEVELS):
+        rows, cols = height >> level, width >> level
+        noises.append(both[:6, row:row + rows, col:col + cols])
+        downs.append(both[6, row:row + rows, col:col + cols])
+        rights.append(wide[row:row + rows, col:col + cols])
+        row, col = row + rows, col + cols
+    return noises, downs, rights
+
+
 def on_device(right_side, noise_block, edges):
     count_rows = lax.axis_size(ROWS)
     count_cols = lax.axis_size(COLS)
     height0, width0 = right_side.shape[1], right_side.shape[2]
 
-    noises = [noise_block]
-    downs = [edges[0]]
-    rights = [edges[1]]
-    for level in range(1, LEVELS):
-        noises.append(restrict_sum(noises[-1]))
-        downs.append(restrict_down(downs[-1]))
-        rights.append(restrict_right(rights[-1]))
+    noises, downs, rights = hierarchy_of(noise_block, edges[0], edges[1])
 
     gathered = LEVELS - 1
     for level in range(LEVELS):

time: 90.3 us -> 86 us (0.952)
  matrix products: 16.5 us -> 11.5 us
    dot_general x16 -> x4, matrix products: 4.34 us -> 0.69 us  [sum_rows(): return jnp.einsum('...hw,hv->...vw', x, m, precision=HIGH)]
    dot_general x16 -> x4, matrix products: 5.06 us -> 1.95 us  [sum_cols(): return jnp.einsum('...hw,wv->...hv', x, m, precision=HIGH)]
    dot_general x0 -> x5, matrix products: none -> 2.39 us  [the longest x1 1.17 us: hierarchy_of(): jnp.einsum('hw,wu->hu', right, col_last, precision=HIGH)]
where the time goes in v6:
time: 86 us; the launch traced here: 85.6 us
  blocking collectives  24.2 us (28%)
  between operations  14.5 us (17%)
  matrix products  11.5 us (13%)
  other arithmetic  10.9 us (13%)
  starting transfers between devices  8.82 us (10%)
  waiting for transfers between devices  8.54 us (10%)
  local copies, waits for them, and re-layouts  7.21 us (8%)
    all_gather x1, blocking collectives, gather_grids(): stacked = lax.all_gather(flat, GRID, axis=0, tiled=False)  24.2 us
    ppermute x2, waiting for transfers between devices, with_halo(): lax.ppermute(head, axis, [(i + 1, i) for i in range(ends)])  7.93 us
    ppermute x2, starting transfers between devices, with_halo(): lax.ppermute(tail, axis, [(i, i + 1) for i in range(ends)])  6.24 us
    dot_general x6, matrix products, prolong(): return jnp.einsum('...hv,wv->...hw', taller, pairs(width), precision=HIGH)  5.03 us
    slice x4, local copies, waits for them, and re-layouts, gather_grids(): part = stacked[:, :, offset:offset + height * width]  3.95 us
    ppermute x2, starting transfers between devices, with_halo(): lax.ppermute(head, axis, [(i + 1, i) for i in range(ends)])  2.58 us
    add x13, other arithmetic, smooth_whole(): i + OMEGA * (s - a) / d  2.27 us
    select_n x6, other arithmetic, sweep_ext(): return [jnp.where(mask, n, 0.0) for n in new]  1.98 us
  transfers between devices with their start and end apart: 5, of which 3 were waited for; matrix products, arithmetic and copies ran while one was open for 4% of the time, Pallas kernels for 0%

profile of v6, /device:TPU:0, one launch (start us, length us, event | category | flops | bytes accessed | tf_op | source)
XLA Modules:
  0.0 85.6 jit_solution(4963320202887205404)
XLA Ops:
  7.1 1.2 %fusion.11 = f32[480,16]{0,1:T(8,128)S(1)} fusion(pred[512,32]{1,0:T(32,128)(4,1)S(1)} %iota_compare_fusion.7, pred[512,64]{1,0:T(32,128)(4,1)S(1)} %iota_compare_fusion.8, pred[512,128]{1,0:T(32,128)(4,1)S(1)} %iota_compare_fusion.9, pred[512,256]{1,0:T(32,128)(4,1)S(1)} %iota_compare_fusion.5, f32[2,16,512]{2,1,0:T(8,128)} %param.5), kind=kOutput, calls=%fused_computation.24 | convolution fusion | flops 47923200 | bytes 309248 | tf_op jit(solution)/shard_map/hw,wu->hu/dot_general | solution.py:260
  9.4 0.6 fusion.12
  10.3 0.7 select_maximum_fusion
  11.1 4.9 %collective-permute-start = (f32[11,4,512]{2,1,0:T(4,128)S(1)}, f32[11,4,512]{2,1,0:T(4,128)S(1)}, u32[]{:S(2)}, u32[]{:S(2)}) collective-permute-start(f32[11,4,512]{2,1,0:T(4,128)S(1)} %get-tuple-element.94), channel_id=1, source_target_pairs={{0,4},{4,8},{8,12},{1,5},{5,9},{9,13},{2,6},{6,10},{10,14},{3,7},{... | collective-permute-start | bytes 270344 | tf_op jit(solution)/shard_map/ppermute | solution.py:29
  16.1 1.3 %collective-permute-start.1 = (f32[11,4,512]{2,1,0:T(4,128)S(1)}, f32[11,4,512]{2,1,0:T(4,128)S(1)}, u32[]{:S(2)}, u32[]{:S(2)}) collective-permute-start(f32[11,4,512]{2,1,0:T(4,128)S(1)} %get-tuple-element.95), channel_id=1, source_target_pairs={{4,0},{8,4},{12,8},{5,1},{9,5},{13,9},{6,2},{10,6},{14,10},{7,3},{... | collective-permute-start | bytes 270344 | tf_op jit(solution)/shard_map/ppermute | solution.py:31
  17.6 0.6 collective-permute-done
  18.2 4.3 %collective-permute-done.1 = f32[11,4,512]{2,1,0:T(4,128)S(1)} collective-permute-done((f32[11,4,512]{2,1,0:T(4,128)S(1)}, f32[11,4,512]{2,1,0:T(4,128)S(1)}, u32[]{:S(2)}, u32[]{:S(2)}) %collective-permute-start.1) | collective-permute-done | bytes 90144 | tf_op jit(solution)/shard_map/ppermute | solution.py:31
  22.6 1.3 %collective-permute-start.2 = (f32[11,24,4]{2,1,0:T(8,128)S(1)}, f32[11,24,4]{2,1,0:T(8,128)S(1)}, u32[]{:S(2)}, u32[]{:S(2)}) collective-permute-start(f32[11,24,4]{2,1,0:T(8,128)S(1)} %get-tuple-element.88), channel_id=1, source_target_pairs={{0,1},{1,2},{2,3},{4,5},{5,6},{6,7},{8,9},{9,10},{10,11},{12,13},{... | collective-permute-start | bytes 12680 | tf_op jit(solution)/shard_map/ppermute | solution.py:29
  23.9 1.3 %collective-permute-start.3 = (f32[11,24,4]{2,1,0:T(8,128)S(1)}, f32[11,24,4]{2,1,0:T(8,128)S(1)}, u32[]{:S(2)}, u32[]{:S(2)}) collective-permute-start(f32[11,24,4]{2,1,0:T(8,128)S(1)} %get-tuple-element.89), channel_id=1, source_target_pairs={{1,0},{2,1},{3,2},{5,4},{6,5},{7,6},{9,8},{10,9},{11,10},{13,12},{... | collective-permute-start | bytes 12680 | tf_op jit(solution)/shard_map/ppermute | solution.py:31
  25.3 3.6 %collective-permute-done.3 = f32[11,24,4]{2,1,0:T(8,128)S(1)} collective-permute-done((f32[11,24,4]{2,1,0:T(8,128)S(1)}, f32[11,24,4]{2,1,0:T(8,128)S(1)}, u32[]{:S(2)}, u32[]{:S(2)}) %collective-permute-start.3) | collective-permute-done | bytes 4256 | tf_op jit(solution)/shard_map/ppermute | solution.py:31
  28.9 0.4 pad_maximum_fusion
  30.3 0.3 fusion.267
  31.5 0.3 fusion.23
  31.8 24.2 %all_gather.13 = f32[16,3,2048]{2,1,0:T(4,128)S(1)} all-gather(f32[1,3,2048]{2,1,0:T(4,128)S(1)} %all_gather.12), channel_id=1, replica_groups=mesh['groups'=2,'tiles'=4,'band'=2,'stokes'=2] {'tiles','band','stokes'}, dimensions={0}, use_global_device_ids=true | all-gather | bytes 417792 | tf_op jit(solution)/shard_map/all_gather | solution.py:159
  56.5 0.8 slice.1997
  57.3 0.8 slice.1985
  58.1 1.0 %slice.1973 = f32[16,8,512]{2,1,0:T(8,128)S(1)} slice(f32[16,8,2816]{2,1,0:T(8,128)} %bitcast.829), slice={[0:16], [0:8], [2048:2560]} | slice | bytes 524288 | tf_op jit(solution)/shard_map/slice | solution.py:164
  59.1 1.3 %slice.1961 = f32[16,8,2048]{2,1,0:T(8,128)S(1)} slice(f32[16,8,2816]{2,1,0:T(8,128)} %bitcast.830), slice={[0:16], [0:8], [0:2048]} | slice | bytes 2097152 | tf_op jit(solution)/shard_map/slice | solution.py:164
  62.1 0.3 copy.168
  63.3 0.5 fusion.84
  63.8 0.3 fusion.94
  64.4 1.0 %fusion.3 = f32[3,16,512]{2,1,0:T(8,128)S(1)} fusion(f32[3,16,1024]{2,1,0:T(8,128)S(1)} %convolution_bitcast_fusion.2, s32[1024]{0:T(1024)S(1)} %get-tuple-element.155, s32[1024]{0:T(1024)S(1)} %get-tuple-element.156, pred[1024]{0:T(1024)(128)(4,1)S(1)} %fusion.711), kind=kOutput, calls=%fused_computation.3 | convolution fusion | flops 303038464 | bytes 304128 | tf_op jit(solution)/shard_map/...hw,wv->...hv/dot_general | solution.py:59
  66.0 0.3 fusion.21
  70.1 2.4 %fusion.1 = f32[3,32,1024]{2,1,0:T(8,128)S(1)} fusion(f32[3,32,512]{2,1,0:T(8,128)S(1)} %convolution_bitcast_fusion, s32[1024]{0:T(1024)S(1)} %get-tuple-element.155, s32[1024]{0:T(1024)S(1)} %get-tuple-element.156, pred[1024]{0:T(1024)(128)(4,1)S(1)} %fusion.711), kind=kOutput, calls=%fused_computation.2 | convolution fusion | flops 605028352 | bytes 599040 | tf_op jit(solution)/shard_map/...hv,wv->...hw/dot_general | solution.py:77
  72.8 0.5 fusion.152
  73.3 0.3 fusion.164
  74.4 0.7 convolution_add_fusion.2
  75.1 0.7 convolution_add_fusion
  75.8 0.7 convolution_add_fusion.1
  76.8 0.3 fusion.224
  77.1 0.3 fusion.235
  78.1 0.6 pad_maximum_fusion.4
  (186 shorter events, 13.1 us)
Async XLA Ops:
  6.5 2.1 %copy-start = (f32[6,16,512]{2,1,0:T(8,128)S(1)}, f32[6,16,512]{2,1,0:T(8,128)}, u32[]{:S(2)}) copy-start(f32[6,16,512]{2,1,0:T(8,128)} %param.4) | copy-start | bytes 589828
  6.5 49.9 %all-gather.3.cloned.1.call-start = ((), (), s32[]{:S(2)}) async-start(), calls=%async_computation | async-start | bytes 1531904 | tf_op jit(solution)/shard_map/all_gather | solution.py:159
  6.8 2.3 %copy-start.1 = (f32[2,16,512]{2,1,0:T(8,128)S(1)}, f32[2,16,512]{2,1,0:T(8,128)}, u32[]{:S(2)}) copy-start(f32[2,16,512]{2,1,0:T(8,128)} %param.5) | copy-start | bytes 196612
  9.0 2.0 %copy-start.2 = (f32[3,16,512]{2,1,0:T(8,128)S(1)}, f32[3,16,512]{2,1,0:T(8,128)}, u32[]{:S(2)}) copy-start(f32[3,16,512]{2,1,0:T(8,128)} %param.3) | copy-start | bytes 294916
  11.1 7.1 %collective-permute-start = (f32[11,4,512]{2,1,0:T(4,128)S(1)}, f32[11,4,512]{2,1,0:T(4,128)S(1)}, u32[]{:S(2)}, u32[]{:S(2)}) collective-permute-start(f32[11,4,512]{2,1,0:T(4,128)S(1)} %get-tuple-element.94), channel_id=1, source_target_pairs={{0,4},{4,8},{8,12},{1,5},{5,9},{9,13},{2,6},{6,10},{10,14},{3,7},{... | collective-permute-start | bytes 270344 | tf_op jit(solution)/shard_map/ppermute | solution.py:29
  16.1 6.4 %collective-permute-start.1 = (f32[11,4,512]{2,1,0:T(4,128)S(1)}, f32[11,4,512]{2,1,0:T(4,128)S(1)}, u32[]{:S(2)}, u32[]{:S(2)}) collective-permute-start(f32[11,4,512]{2,1,0:T(4,128)S(1)} %get-tuple-element.95), channel_id=1, source_target_pairs={{4,0},{8,4},{12,8},{5,1},{9,5},{13,9},{6,2},{10,6},{14,10},{7,3},{... | collective-permute-start | bytes 270344 | tf_op jit(solution)/shard_map/ppermute | solution.py:31
  22.6 2.6 %collective-permute-start.2 = (f32[11,24,4]{2,1,0:T(8,128)S(1)}, f32[11,24,4]{2,1,0:T(8,128)S(1)}, u32[]{:S(2)}, u32[]{:S(2)}) collective-permute-start(f32[11,24,4]{2,1,0:T(8,128)S(1)} %get-tuple-element.88), channel_id=1, source_target_pairs={{0,1},{1,2},{2,3},{4,5},{5,6},{6,7},{8,9},{9,10},{10,11},{12,13},{... | collective-permute-start | bytes 12680 | tf_op jit(solution)/shard_map/ppermute | solution.py:29
  23.9 5.0 %collective-permute-start.3 = (f32[11,24,4]{2,1,0:T(8,128)S(1)}, f32[11,24,4]{2,1,0:T(8,128)S(1)}, u32[]{:S(2)}, u32[]{:S(2)}) collective-permute-start(f32[11,24,4]{2,1,0:T(8,128)S(1)} %get-tuple-element.89), channel_id=1, source_target_pairs={{1,0},{2,1},{3,2},{5,4},{6,5},{7,6},{9,8},{10,9},{11,10},{13,12},{... | collective-permute-start | bytes 12680 | tf_op jit(solution)/shard_map/ppermute | solution.py:31
Sparse Core Ops, SparseCore 0:
  11.1 43.0 all-gather.2

commit v7 on v6

--- a/solution.py
+++ b/solution.py
@@ -73,8 +73,8 @@
 
 def prolong(coarse):
     height, width = coarse.shape[-2] * 2, coarse.shape[-1] * 2
-    taller = jnp.einsum("...vw,hv->...hw", coarse, pairs(height), precision=HIGH)
-    return jnp.einsum("...hv,wv->...hw", taller, pairs(width), precision=HIGH)
+    wider = jnp.einsum("...hv,wv->...hw", coarse, pairs(width), precision=HIGH)
+    return jnp.einsum("...vw,hv->...hw", wider, pairs(height), precision=HIGH)
 
 
 def apply_planes(iterate, padded, noise, couplings):

time: 86 us -> 84.9 us (0.987)
  matrix products: 11.5 us -> 10.4 us
    dot_general x12, matrix products: 6.44 us -> 5.37 us  [the longest x6 3.83 us: prolong(): wider = jnp.einsum('...hv,wv->...hw', coarse, pairs(width), precision=HIGH)]
where the time goes in v7:
time: 84.9 us; the launch traced here: 84.5 us
  blocking collectives  24.2 us (29%)
  between operations  14.5 us (17%)
  other arithmetic  10.8 us (13%)
  matrix products  10.4 us (12%)
  starting transfers between devices  8.82 us (10%)
  waiting for transfers between devices  8.54 us (10%)
  local copies, waits for them, and re-layouts  7.21 us (8%)
    all_gather x1, blocking collectives, gather_grids(): stacked = lax.all_gather(flat, GRID, axis=0, tiled=False)  24.2 us
    ppermute x2, waiting for transfers between devices, with_halo(): lax.ppermute(head, axis, [(i + 1, i) for i in range(ends)])  7.93 us
    ppermute x2, starting transfers between devices, with_halo(): lax.ppermute(tail, axis, [(i, i + 1) for i in range(ends)])  6.24 us
    slice x4, local copies, waits for them, and re-layouts, gather_grids(): part = stacked[:, :, offset:offset + height * width]  3.95 us
    dot_general x6, matrix products, prolong(): wider = jnp.einsum('...hv,wv->...hw', coarse, pairs(width), precision=HIGH)  3.83 us
    ppermute x2, starting transfers between devices, with_halo(): lax.ppermute(head, axis, [(i + 1, i) for i in range(ends)])  2.58 us
    add x13, other arithmetic, smooth_whole(): i + OMEGA * (s - a) / d  2.27 us
    select_n x6, other arithmetic, sweep_ext(): return [jnp.where(mask, n, 0.0) for n in new]  1.98 us
  transfers between devices with their start and end apart: 5, of which 3 were waited for; matrix products, arithmetic and copies ran while one was open for 4% of the time, Pallas kernels for 0%

profile of v7, /device:TPU:0, one launch (start us, length us, event | category | flops | bytes accessed | tf_op | source)
XLA Modules:
  0.0 84.5 jit_solution(3972437012401868476)
XLA Ops:
  7.1 1.2 %fusion.11 = f32[480,16]{0,1:T(8,128)S(1)} fusion(pred[512,32]{1,0:T(32,128)(4,1)S(1)} %iota_compare_fusion.7, pred[512,64]{1,0:T(32,128)(4,1)S(1)} %iota_compare_fusion.8, pred[512,128]{1,0:T(32,128)(4,1)S(1)} %iota_compare_fusion.9, pred[512,256]{1,0:T(32,128)(4,1)S(1)} %iota_compare_fusion.5, f32[2,16,512]{2,1,0:T(8,128)} %param.5), kind=kOutput, calls=%fused_computation.24 | convolution fusion | flops 47923200 | bytes 309248 | tf_op jit(solution)/shard_map/hw,wu->hu/dot_general | solution.py:260
  9.4 0.6 fusion.12
  10.3 0.7 select_maximum_fusion
  11.1 4.9 %collective-permute-start = (f32[11,4,512]{2,1,0:T(4,128)S(1)}, f32[11,4,512]{2,1,0:T(4,128)S(1)}, u32[]{:S(2)}, u32[]{:S(2)}) collective-permute-start(f32[11,4,512]{2,1,0:T(4,128)S(1)} %get-tuple-element.94), channel_id=1, source_target_pairs={{0,4},{4,8},{8,12},{1,5},{5,9},{9,13},{2,6},{6,10},{10,14},{3,7},{... | collective-permute-start | bytes 270344 | tf_op jit(solution)/shard_map/ppermute | solution.py:29
  16.1 1.3 %collective-permute-start.1 = (f32[11,4,512]{2,1,0:T(4,128)S(1)}, f32[11,4,512]{2,1,0:T(4,128)S(1)}, u32[]{:S(2)}, u32[]{:S(2)}) collective-permute-start(f32[11,4,512]{2,1,0:T(4,128)S(1)} %get-tuple-element.95), channel_id=1, source_target_pairs={{4,0},{8,4},{12,8},{5,1},{9,5},{13,9},{6,2},{10,6},{14,10},{7,3},{... | collective-permute-start | bytes 270344 | tf_op jit(solution)/shard_map/ppermute | solution.py:31
  17.6 0.6 collective-permute-done
  18.2 4.3 %collective-permute-done.1 = f32[11,4,512]{2,1,0:T(4,128)S(1)} collective-permute-done((f32[11,4,512]{2,1,0:T(4,128)S(1)}, f32[11,4,512]{2,1,0:T(4,128)S(1)}, u32[]{:S(2)}, u32[]{:S(2)}) %collective-permute-start.1) | collective-permute-done | bytes 90144 | tf_op jit(solution)/shard_map/ppermute | solution.py:31
  22.6 1.3 %collective-permute-start.2 = (f32[11,24,4]{2,1,0:T(8,128)S(1)}, f32[11,24,4]{2,1,0:T(8,128)S(1)}, u32[]{:S(2)}, u32[]{:S(2)}) collective-permute-start(f32[11,24,4]{2,1,0:T(8,128)S(1)} %get-tuple-element.88), channel_id=1, source_target_pairs={{0,1},{1,2},{2,3},{4,5},{5,6},{6,7},{8,9},{9,10},{10,11},{12,13},{... | collective-permute-start | bytes 12680 | tf_op jit(solution)/shard_map/ppermute | solution.py:29
  23.9 1.3 %collective-permute-start.3 = (f32[11,24,4]{2,1,0:T(8,128)S(1)}, f32[11,24,4]{2,1,0:T(8,128)S(1)}, u32[]{:S(2)}, u32[]{:S(2)}) collective-permute-start(f32[11,24,4]{2,1,0:T(8,128)S(1)} %get-tuple-element.89), channel_id=1, source_target_pairs={{1,0},{2,1},{3,2},{5,4},{6,5},{7,6},{9,8},{10,9},{11,10},{13,12},{... | collective-permute-start | bytes 12680 | tf_op jit(solution)/shard_map/ppermute | solution.py:31
  25.3 3.6 %collective-permute-done.3 = f32[11,24,4]{2,1,0:T(8,128)S(1)} collective-permute-done((f32[11,24,4]{2,1,0:T(8,128)S(1)}, f32[11,24,4]{2,1,0:T(8,128)S(1)}, u32[]{:S(2)}, u32[]{:S(2)}) %collective-permute-start.3) | collective-permute-done | bytes 4256 | tf_op jit(solution)/shard_map/ppermute | solution.py:31
  28.9 0.4 pad_maximum_fusion
  30.3 0.3 fusion.270
  31.5 0.3 fusion.26
  31.8 24.2 %all_gather.13 = f32[16,3,2048]{2,1,0:T(4,128)S(1)} all-gather(f32[1,3,2048]{2,1,0:T(4,128)S(1)} %all_gather.12), channel_id=1, replica_groups=mesh['groups'=2,'tiles'=4,'band'=2,'stokes'=2] {'tiles','band','stokes'}, dimensions={0}, use_global_device_ids=true | all-gather | bytes 417792 | tf_op jit(solution)/shard_map/all_gather | solution.py:159
  56.5 0.8 %slice.1997 = f32[16,8,32]{2,1,0:T(8,128)S(1)} slice(f32[16,8,2816]{2,1,0:T(8,128)} %bitcast.827), slice={[0:16], [0:8], [2688:2720]} | slice | bytes 32768 | tf_op jit(solution)/shard_map/slice | solution.py:164
  57.3 0.8 slice.1985
  58.1 1.0 %slice.1973 = f32[16,8,512]{2,1,0:T(8,128)S(1)} slice(f32[16,8,2816]{2,1,0:T(8,128)} %bitcast.829), slice={[0:16], [0:8], [2048:2560]} | slice | bytes 524288 | tf_op jit(solution)/shard_map/slice | solution.py:164
  59.1 1.3 %slice.1961 = f32[16,8,2048]{2,1,0:T(8,128)S(1)} slice(f32[16,8,2816]{2,1,0:T(8,128)} %bitcast.830), slice={[0:16], [0:8], [0:2048]} | slice | bytes 2097152 | tf_op jit(solution)/shard_map/slice | solution.py:164
  62.1 0.3 copy.168
  63.3 0.5 fusion.87
  63.8 0.3 fusion.97
  64.4 1.0 %fusion.3 = f32[3,16,512]{2,1,0:T(8,128)S(1)} fusion(f32[3,16,1024]{2,1,0:T(8,128)S(1)} %convolution_bitcast_fusion.2, s32[1024]{0:T(1024)S(1)} %get-tuple-element.155, s32[1024]{0:T(1024)S(1)} %get-tuple-element.156, pred[1024]{0:T(1024)(128)(4,1)S(1)} %fusion.711), kind=kOutput, calls=%fused_computation.4 | convolution fusion | flops 303038464 | bytes 304128 | tf_op jit(solution)/shard_map/...hw,wv->...hv/dot_general | solution.py:59
  66.0 0.3 fusion.24
  69.8 1.3 %fusion.1 = f32[3,16,1024]{2,1,0:T(8,128)S(1)} fusion(s32[1024]{0:T(1024)S(1)} %get-tuple-element.155, s32[1024]{0:T(1024)S(1)} %get-tuple-element.156, pred[1024]{0:T(1024)(128)(4,1)S(1)} %fusion.711, f32[1,16,512]{2,1,0:T(8,128)S(1)} %get-tuple-element.97, f32[1,16,512]{2,1,0:T(8,128)S(1)} %get-tuple-element.96, f32[1,16,512]{2,1,0:T(8,128)S(1)} %get-tuple-element.10), kind=kOutput, calls=%fused_computation.3 | convolution fusion | flops 303087616 | bytes 304128 | tf_op jit(solution)/shard_map/...hv,wv->...hw/dot_general | solution.py:76
  71.2 0.4 convolution_bitcast_fusion
  71.8 0.5 fusion.155
  72.3 0.3 fusion.167
  72.7 0.6 fusion.21
  73.3 0.6 fusion.20
  74.0 0.6 fusion.19
  75.7 0.3 fusion.227
  77.0 0.6 pad_maximum_fusion.4
  (186 shorter events, 13.2 us)
Async XLA Ops:
  6.5 2.1 %copy-start = (f32[6,16,512]{2,1,0:T(8,128)S(1)}, f32[6,16,512]{2,1,0:T(8,128)}, u32[]{:S(2)}) copy-start(f32[6,16,512]{2,1,0:T(8,128)} %param.4) | copy-start | bytes 589828
  6.5 49.9 %all-gather.3.cloned.1.call-start = ((), (), s32[]{:S(2)}) async-start(), calls=%async_computation | async-start | bytes 1531904 | tf_op jit(solution)/shard_map/all_gather | solution.py:159
  6.8 2.3 %copy-start.1 = (f32[2,16,512]{2,1,0:T(8,128)S(1)}, f32[2,16,512]{2,1,0:T(8,128)}, u32[]{:S(2)}) copy-start(f32[2,16,512]{2,1,0:T(8,128)} %param.5) | copy-start | bytes 196612
  9.0 2.0 %copy-start.2 = (f32[3,16,512]{2,1,0:T(8,128)S(1)}, f32[3,16,512]{2,1,0:T(8,128)}, u32[]{:S(2)}) copy-start(f32[3,16,512]{2,1,0:T(8,128)} %param.3) | copy-start | bytes 294916
  11.1 7.1 %collective-permute-start = (f32[11,4,512]{2,1,0:T(4,128)S(1)}, f32[11,4,512]{2,1,0:T(4,128)S(1)}, u32[]{:S(2)}, u32[]{:S(2)}) collective-permute-start(f32[11,4,512]{2,1,0:T(4,128)S(1)} %get-tuple-element.94), channel_id=1, source_target_pairs={{0,4},{4,8},{8,12},{1,5},{5,9},{9,13},{2,6},{6,10},{10,14},{3,7},{... | collective-permute-start | bytes 270344 | tf_op jit(solution)/shard_map/ppermute | solution.py:29
  16.1 6.4 %collective-permute-start.1 = (f32[11,4,512]{2,1,0:T(4,128)S(1)}, f32[11,4,512]{2,1,0:T(4,128)S(1)}, u32[]{:S(2)}, u32[]{:S(2)}) collective-permute-start(f32[11,4,512]{2,1,0:T(4,128)S(1)} %get-tuple-element.95), channel_id=1, source_target_pairs={{4,0},{8,4},{12,8},{5,1},{9,5},{13,9},{6,2},{10,6},{14,10},{7,3},{... | collective-permute-start | bytes 270344 | tf_op jit(solution)/shard_map/ppermute | solution.py:31
  22.6 2.6 %collective-permute-start.2 = (f32[11,24,4]{2,1,0:T(8,128)S(1)}, f32[11,24,4]{2,1,0:T(8,128)S(1)}, u32[]{:S(2)}, u32[]{:S(2)}) collective-permute-start(f32[11,24,4]{2,1,0:T(8,128)S(1)} %get-tuple-element.88), channel_id=1, source_target_pairs={{0,1},{1,2},{2,3},{4,5},{5,6},{6,7},{8,9},{9,10},{10,11},{12,13},{... | collective-permute-start | bytes 12680 | tf_op jit(solution)/shard_map/ppermute | solution.py:29
  23.9 5.0 %collective-permute-start.3 = (f32[11,24,4]{2,1,0:T(8,128)S(1)}, f32[11,24,4]{2,1,0:T(8,128)S(1)}, u32[]{:S(2)}, u32[]{:S(2)}) collective-permute-start(f32[11,24,4]{2,1,0:T(8,128)S(1)} %get-tuple-element.89), channel_id=1, source_target_pairs={{1,0},{2,1},{3,2},{5,4},{6,5},{7,6},{9,8},{10,9},{11,10},{13,12},{... | collective-permute-start | bytes 12680 | tf_op jit(solution)/shard_map/ppermute | solution.py:31
Sparse Core Ops, SparseCore 0:
  11.1 43.0 all-gather.2

commit v8 on v7

--- a/solution.py
+++ b/solution.py
@@ -174,8 +174,12 @@
 def own_window(whole, height, width, ring):
     row = lax.axis_index(ROWS) * height
     col = lax.axis_index(COLS) * width
-    padded = jnp.pad(whole, ring) if ring else whole
-    return lax.dynamic_slice(padded, (row, col), (height + 2 * ring, width + 2 * ring))
+    lead = whole.shape[:-2]
+    pads = [(0, 0)] * len(lead) + [(ring, ring), (ring, ring)]
+    padded = jnp.pad(whole, pads) if ring else whole
+    return lax.dynamic_slice(
+        padded, (0,) * len(lead) + (row, col), lead + (height + 2 * ring, width + 2 * ring)
+    )
 
 
 def inside(height, width, ext):
@@ -221,9 +225,8 @@
     residual = [s - a for s, a in zip(crops(source, HALO), image)]
     coarse = below(residual)
     ring = (POST + 1) // 2
-    iterate = [
-        i + crop(prolong(c), 2 * ring - POST) for i, c in zip(crops(iterate, ext - POST), coarse)
-    ]
+    fine = crop(prolong(coarse), 2 * ring - POST)
+    iterate = [i + fine[k] for k, i in enumerate(crops(iterate, ext - POST))]
     for sweep_index in range(POST):
         ext = POST - 1 - sweep_index
         cut = HALO - ext
@@ -325,9 +328,9 @@
             coarse_source = restrict_sum(jnp.stack(residual))
             if level + 1 == gathered:
                 correction = cycle_whole(gather_grid(coarse_source), hierarchy, gathered)
-                return [own_window(c, height // 2, width // 2, ring) for c in correction]
+                return own_window(jnp.stack(correction), height // 2, width // 2, ring)
             coarse = run(level + 1, list(with_halo(coarse_source, HALO)))
-            return list(with_halo(jnp.stack(coarse), ring))
+            return with_halo(jnp.stack(coarse), ring)
 
         return level_split(source, noise, couplings, below)
 

time: 84.9 us -> 82.9 us (0.976)
  matrix products: 10.4 us -> 8.55 us
    dot_general x6 -> x4, matrix products: 3.83 us -> 2.39 us  [prolong(): wider = jnp.einsum('...hv,wv->...hw', coarse, pairs(width), precision=HIGH)]
    add x13 -> x10, other arithmetic: 2.27 us -> 1.15 us  [smooth_whole(): i + OMEGA * (s - a) / d]
where the time goes in v8:
time: 82.9 us; the launch traced here: 82.5 us
  blocking collectives  24.2 us (29%)
  between operations  14.4 us (17%)
  other arithmetic  10.8 us (13%)
  starting transfers between devices  8.82 us (11%)
  matrix products  8.55 us (10%)
  waiting for transfers between devices  8.47 us (10%)
  local copies, waits for them, and re-layouts  7.21 us (9%)
    all_gather x1, blocking collectives, gather_grids(): stacked = lax.all_gather(flat, GRID, axis=0, tiled=False)  24.2 us
    ppermute x2, waiting for transfers between devices, with_halo(): lax.ppermute(head, axis, [(i + 1, i) for i in range(ends)])  7.94 us
    ppermute x2, starting transfers between devices, with_halo(): lax.ppermute(tail, axis, [(i, i + 1) for i in range(ends)])  6.23 us
    slice x4, local copies, waits for them, and re-layouts, gather_grids(): part = stacked[:, :, offset:offset + height * width]  3.95 us
    ppermute x2, starting transfers between devices, with_halo(): lax.ppermute(head, axis, [(i + 1, i) for i in range(ends)])  2.58 us
    dot_general x4, matrix products, prolong(): wider = jnp.einsum('...hv,wv->...hw', coarse, pairs(width), precision=HIGH)  2.39 us
    select_n x6, other arithmetic, sweep_ext(): return [jnp.where(mask, n, 0.0) for n in new]  1.99 us
    dot_general x4, matrix products, sum_cols(): return jnp.einsum('...hw,wv->...hv', x, m, precision=HIGH)  1.95 us
  transfers between devices with their start and end apart: 5, of which 3 were waited for; matrix products, arithmetic and copies ran while one was open for 4% of the time, Pallas kernels for 0%

profile of v8, /device:TPU:0, one launch (start us, length us, event | category | flops | bytes accessed | tf_op | source)
XLA Modules:
  0.0 82.5 jit_solution(9206071206041679363)
XLA Ops:
  7.1 1.2 %fusion.11 = f32[480,16]{0,1:T(8,128)S(1)} fusion(pred[512,32]{1,0:T(32,128)(4,1)S(1)} %iota_compare_fusion.6, pred[512,64]{1,0:T(32,128)(4,1)S(1)} %iota_compare_fusion.7, pred[512,128]{1,0:T(32,128)(4,1)S(1)} %iota_compare_fusion.8, pred[512,256]{1,0:T(32,128)(4,1)S(1)} %iota_compare_fusion.4, f32[2,16,512]{2,1,0:T(8,128)} %param.5), kind=kOutput, calls=%fused_computation.22 | convolution fusion | flops 47923200 | bytes 309248 | tf_op jit(solution)/shard_map/hw,wu->hu/dot_general | solution.py:263
  9.4 0.6 fusion.12
  10.3 0.7 select_maximum_fusion
  11.1 4.9 %collective-permute-start = (f32[11,4,512]{2,1,0:T(4,128)S(1)}, f32[11,4,512]{2,1,0:T(4,128)S(1)}, u32[]{:S(2)}, u32[]{:S(2)}) collective-permute-start(f32[11,4,512]{2,1,0:T(4,128)S(1)} %get-tuple-element.94), channel_id=1, source_target_pairs={{0,4},{4,8},{8,12},{1,5},{5,9},{9,13},{2,6},{6,10},{10,14},{3,7},{... | collective-permute-start | bytes 270344 | tf_op jit(solution)/shard_map/ppermute | solution.py:29
  16.0 1.3 %collective-permute-start.1 = (f32[11,4,512]{2,1,0:T(4,128)S(1)}, f32[11,4,512]{2,1,0:T(4,128)S(1)}, u32[]{:S(2)}, u32[]{:S(2)}) collective-permute-start(f32[11,4,512]{2,1,0:T(4,128)S(1)} %get-tuple-element.95), channel_id=1, source_target_pairs={{4,0},{8,4},{12,8},{5,1},{9,5},{13,9},{6,2},{10,6},{14,10},{7,3},{... | collective-permute-start | bytes 270344 | tf_op jit(solution)/shard_map/ppermute | solution.py:31
  17.7 0.5 collective-permute-done
  18.1 4.3 %collective-permute-done.1 = f32[11,4,512]{2,1,0:T(4,128)S(1)} collective-permute-done((f32[11,4,512]{2,1,0:T(4,128)S(1)}, f32[11,4,512]{2,1,0:T(4,128)S(1)}, u32[]{:S(2)}, u32[]{:S(2)}) %collective-permute-start.1) | collective-permute-done | bytes 90144 | tf_op jit(solution)/shard_map/ppermute | solution.py:31
  22.6 1.3 %collective-permute-start.2 = (f32[11,24,4]{2,1,0:T(8,128)S(1)}, f32[11,24,4]{2,1,0:T(8,128)S(1)}, u32[]{:S(2)}, u32[]{:S(2)}) collective-permute-start(f32[11,24,4]{2,1,0:T(8,128)S(1)} %get-tuple-element.86), channel_id=1, source_target_pairs={{0,1},{1,2},{2,3},{4,5},{5,6},{6,7},{8,9},{9,10},{10,11},{12,13},{... | collective-permute-start | bytes 12680 | tf_op jit(solution)/shard_map/ppermute | solution.py:29
  23.9 1.3 %collective-permute-start.3 = (f32[11,24,4]{2,1,0:T(8,128)S(1)}, f32[11,24,4]{2,1,0:T(8,128)S(1)}, u32[]{:S(2)}, u32[]{:S(2)}) collective-permute-start(f32[11,24,4]{2,1,0:T(8,128)S(1)} %get-tuple-element.87), channel_id=1, source_target_pairs={{1,0},{2,1},{3,2},{5,4},{6,5},{7,6},{9,8},{10,9},{11,10},{13,12},{... | collective-permute-start | bytes 12680 | tf_op jit(solution)/shard_map/ppermute | solution.py:31
  25.2 3.6 %collective-permute-done.3 = f32[11,24,4]{2,1,0:T(8,128)S(1)} collective-permute-done((f32[11,24,4]{2,1,0:T(8,128)S(1)}, f32[11,24,4]{2,1,0:T(8,128)S(1)}, u32[]{:S(2)}, u32[]{:S(2)}) %collective-permute-start.3) | collective-permute-done | bytes 4256 | tf_op jit(solution)/shard_map/ppermute | solution.py:31
  28.8 0.4 pad_maximum_fusion
  29.6 0.3 fusion.276
  30.0 0.3 fusion.286
  30.3 0.3 fusion.297
  31.4 0.3 fusion.26
  31.8 24.2 %all_gather.13 = f32[16,3,2048]{2,1,0:T(4,128)S(1)} all-gather(f32[1,3,2048]{2,1,0:T(4,128)S(1)} %all_gather.12), channel_id=1, replica_groups=mesh['groups'=2,'tiles'=4,'band'=2,'stokes'=2] {'tiles','band','stokes'}, dimensions={0}, use_global_device_ids=true | all-gather | bytes 417792 | tf_op jit(solution)/shard_map/all_gather | solution.py:159
  56.4 0.8 %slice.2009 = f32[16,8,32]{2,1,0:T(8,128)S(1)} slice(f32[16,8,2816]{2,1,0:T(8,128)} %bitcast.849), slice={[0:16], [0:8], [2688:2720]} | slice | bytes 32768 | tf_op jit(solution)/shard_map/slice | solution.py:164
  57.3 0.8 %slice.1997 = f32[16,8,128]{2,1,0:T(8,128)S(1)} slice(f32[16,8,2816]{2,1,0:T(8,128)} %bitcast.850), slice={[0:16], [0:8], [2560:2688]} | slice | bytes 131072 | tf_op jit(solution)/shard_map/slice | solution.py:164
  58.1 1.0 %slice.1985 = f32[16,8,512]{2,1,0:T(8,128)S(1)} slice(f32[16,8,2816]{2,1,0:T(8,128)} %bitcast.851), slice={[0:16], [0:8], [2048:2560]} | slice | bytes 524288 | tf_op jit(solution)/shard_map/slice | solution.py:164
  59.1 1.3 %slice.1973 = f32[16,8,2048]{2,1,0:T(8,128)S(1)} slice(f32[16,8,2816]{2,1,0:T(8,128)} %bitcast.852), slice={[0:16], [0:8], [0:2048]} | slice | bytes 2097152 | tf_op jit(solution)/shard_map/slice | solution.py:164
  62.0 0.3 copy.168
  63.2 0.5 fusion.81
  64.3 1.0 %fusion.3 = f32[3,16,512]{2,1,0:T(8,128)S(1)} fusion(f32[3,16,1024]{2,1,0:T(8,128)S(1)} %convolution_bitcast_fusion.2, s32[1024]{0:T(1024)S(1)} %get-tuple-element.164, s32[1024]{0:T(1024)S(1)} %get-tuple-element.165, pred[1024]{0:T(1024)(128)(4,1)S(1)} %fusion.739), kind=kOutput, calls=%fused_computation.4 | convolution fusion | flops 303038464 | bytes 304128 | tf_op jit(solution)/shard_map/...hw,wv->...hv/dot_general | solution.py:59
  65.9 0.3 fusion.24
  69.7 1.3 %fusion.1 = f32[3,16,1024]{2,1,0:T(8,128)S(1)} fusion(s32[1024]{0:T(1024)S(1)} %get-tuple-element.164, s32[1024]{0:T(1024)S(1)} %get-tuple-element.165, pred[1024]{0:T(1024)(128)(4,1)S(1)} %fusion.739, f32[1,16,512]{2,1,0:T(8,128)S(1)} %get-tuple-element.97, f32[1,16,512]{2,1,0:T(8,128)S(1)} %get-tuple-element.96, f32[1,16,512]{2,1,0:T(8,128)S(1)} %get-tuple-element.8), kind=kOutput, calls=%fused_computation.3 | convolution fusion | flops 303087616 | bytes 304128 | tf_op jit(solution)/shard_map/...hv,wv->...hw/dot_general | solution.py:76
  71.1 0.4 convolution_bitcast_fusion
  71.7 0.5 fusion.185
  72.5 0.5 fusion.20
  73.4 0.3 fusion.251
  73.7 0.3 fusion.262
  74.0 0.3 fusion.241
  75.0 0.6 pad_maximum_fusion.4
  (181 shorter events, 12.1 us)
Async XLA Ops:
  6.5 2.1 %copy-start = (f32[6,16,512]{2,1,0:T(8,128)S(1)}, f32[6,16,512]{2,1,0:T(8,128)}, u32[]{:S(2)}) copy-start(f32[6,16,512]{2,1,0:T(8,128)} %param.4) | copy-start | bytes 589828
  6.5 49.9 %all-gather.3.cloned.1.call-start = ((), (), s32[]{:S(2)}) async-start(), calls=%async_computation | async-start | bytes 1531904 | tf_op jit(solution)/shard_map/all_gather | solution.py:159
  6.8 2.3 %copy-start.1 = (f32[2,16,512]{2,1,0:T(8,128)S(1)}, f32[2,16,512]{2,1,0:T(8,128)}, u32[]{:S(2)}) copy-start(f32[2,16,512]{2,1,0:T(8,128)} %param.5) | copy-start | bytes 196612
  8.9 2.0 %copy-start.2 = (f32[3,16,512]{2,1,0:T(8,128)S(1)}, f32[3,16,512]{2,1,0:T(8,128)}, u32[]{:S(2)}) copy-start(f32[3,16,512]{2,1,0:T(8,128)} %param.3) | copy-start | bytes 294916
  11.1 7.1 %collective-permute-start = (f32[11,4,512]{2,1,0:T(4,128)S(1)}, f32[11,4,512]{2,1,0:T(4,128)S(1)}, u32[]{:S(2)}, u32[]{:S(2)}) collective-permute-start(f32[11,4,512]{2,1,0:T(4,128)S(1)} %get-tuple-element.94), channel_id=1, source_target_pairs={{0,4},{4,8},{8,12},{1,5},{5,9},{9,13},{2,6},{6,10},{10,14},{3,7},{... | collective-permute-start | bytes 270344 | tf_op jit(solution)/shard_map/ppermute | solution.py:29
  16.0 6.4 %collective-permute-start.1 = (f32[11,4,512]{2,1,0:T(4,128)S(1)}, f32[11,4,512]{2,1,0:T(4,128)S(1)}, u32[]{:S(2)}, u32[]{:S(2)}) collective-permute-start(f32[11,4,512]{2,1,0:T(4,128)S(1)} %get-tuple-element.95), channel_id=1, source_target_pairs={{4,0},{8,4},{12,8},{5,1},{9,5},{13,9},{6,2},{10,6},{14,10},{7,3},{... | collective-permute-start | bytes 270344 | tf_op jit(solution)/shard_map/ppermute | solution.py:31
  22.6 2.6 %collective-permute-start.2 = (f32[11,24,4]{2,1,0:T(8,128)S(1)}, f32[11,24,4]{2,1,0:T(8,128)S(1)}, u32[]{:S(2)}, u32[]{:S(2)}) collective-permute-start(f32[11,24,4]{2,1,0:T(8,128)S(1)} %get-tuple-element.86), channel_id=1, source_target_pairs={{0,1},{1,2},{2,3},{4,5},{5,6},{6,7},{8,9},{9,10},{10,11},{12,13},{... | collective-permute-start | bytes 12680 | tf_op jit(solution)/shard_map/ppermute | solution.py:29
  23.9 5.0 %collective-permute-start.3 = (f32[11,24,4]{2,1,0:T(8,128)S(1)}, f32[11,24,4]{2,1,0:T(8,128)S(1)}, u32[]{:S(2)}, u32[]{:S(2)}) collective-permute-start(f32[11,24,4]{2,1,0:T(8,128)S(1)} %get-tuple-element.87), channel_id=1, source_target_pairs={{1,0},{2,1},{3,2},{5,4},{6,5},{7,6},{9,8},{10,9},{11,10},{13,12},{... | collective-permute-start | bytes 12680 | tf_op jit(solution)/shard_map/ppermute | solution.py:31
Sparse Core Ops, SparseCore 0:
  11.1 43.0 all-gather.2

commit v9 on v8

--- a/solution.py
+++ b/solution.py
@@ -144,6 +144,27 @@
     return gather_grids([block])[0]
 
 
+def gather_axis(x, axis):
+    count = lax.axis_size(axis)
+    me = lax.axis_index(axis)
+    pieces = [x] + [
+        lax.ppermute(x, axis, [(i, (i + k) % count) for i in range(count)]) for k in range(1, count)
+    ]
+    order = (me - jnp.arange(count)) % count
+    return jnp.take(jnp.stack(pieces), order, axis=0, mode="clip")
+
+
+def gather_by_shifts(block):
+    count_rows = lax.axis_size(ROWS)
+    count_cols = lax.axis_size(COLS)
+    planes, height, width = block.shape
+    stacked = gather_axis(gather_axis(block, COLS), ROWS)
+    whole = stacked.transpose(2, 0, 3, 1, 4).reshape(
+        planes, count_rows * height, count_cols * width
+    )
+    return [whole[k] for k in range(planes)]
+
+
 def gather_grids(blocks):
     count_rows = lax.axis_size(ROWS)
     count_cols = lax.axis_size(COLS)
@@ -327,7 +348,7 @@
         def below(residual):
             coarse_source = restrict_sum(jnp.stack(residual))
             if level + 1 == gathered:
-                correction = cycle_whole(gather_grid(coarse_source), hierarchy, gathered)
+                correction = cycle_whole(gather_by_shifts(coarse_source), hierarchy, gathered)
                 return own_window(jnp.stack(correction), height // 2, width // 2, ring)
             coarse = run(level + 1, list(with_halo(coarse_source, HALO)))
             return with_halo(jnp.stack(coarse), ring)

time: 82.9 us -> 82.5 us (level)
  blocking collectives: 24.2 us -> 0 us
  starting transfers between devices: 8.82 us -> 20.7 us
  waiting for transfers between devices: 8.47 us -> 18.8 us
  local copies, waits for them, and re-layouts: 7.21 us -> 8.05 us
    all_gather x1 -> x0, blocking collectives: 24.2 us -> none  [gather_grids(): stacked = lax.all_gather(flat, GRID, axis=0, tiled=False)]
    ppermute x0 -> x6, starting transfers between devices: none -> 11.9 us  [gather_axis(): lax.ppermute(x, axis, [(i, (i + k) % count) for i in range(count)])]
    ppermute x0 -> x6, waiting for transfers between devices: none -> 10.2 us  [gather_axis(): lax.ppermute(x, axis, [(i, (i + k) % count) for i in range(count)])]
    gather x0 -> x2, local copies, waits for them, and re-layouts: none -> 1.13 us  [gather_axis(): return jnp.take(jnp.stack(pieces), order, axis=0, mode='clip')]
  transfers between devices with their start and end apart: 5 -> 11, of which waited for: 3 -> 7; matrix products, arithmetic and copies ran while one was open for 4% -> 5% of each run, Pallas kernels for 0% -> 0%
where the time goes in v9:
time: 82.5 us; the launch traced here: 82.2 us
  starting transfers between devices  20.7 us (25%)
  waiting for transfers between devices  18.8 us (23%)
  between operations  14.4 us (17%)
  other arithmetic  10.9 us (13%)
  matrix products  9.35 us (11%)
  local copies, waits for them, and re-layouts  8.05 us (10%)
    ppermute x6, starting transfers between devices, gather_axis(): lax.ppermute(x, axis, [(i, (i + k) % count) for i in range(count)])  11.9 us
    ppermute x6, waiting for transfers between devices, gather_axis(): lax.ppermute(x, axis, [(i, (i + k) % count) for i in range(count)])  10.2 us
    ppermute x2, waiting for transfers between devices, with_halo(): lax.ppermute(head, axis, [(i + 1, i) for i in range(ends)])  7.95 us
    ppermute x2, starting transfers between devices, with_halo(): lax.ppermute(tail, axis, [(i, i + 1) for i in range(ends)])  6.23 us
    slice x4, local copies, waits for them, and re-layouts, gather_grids(): part = stacked[:, :, offset:offset + height * width]  3.95 us
    dot_general x4, matrix products, prolong(): wider = jnp.einsum('...hv,wv->...hw', coarse, pairs(width), precision=HIGH)  2.66 us
    ppermute x2, starting transfers between devices, with_halo(): lax.ppermute(head, axis, [(i + 1, i) for i in range(ends)])  2.58 us
    select_n x6, other arithmetic, sweep_ext(): return [jnp.where(mask, n, 0.0) for n in new]  1.99 us
  transfers between devices with their start and end apart: 11, of which 7 were waited for; matrix products, arithmetic and copies ran while one was open for 5% of the time, Pallas kernels for 0%

profile of v9, /device:TPU:0, one launch (start us, length us, event | category | flops | bytes accessed | tf_op | source)
XLA Modules:
  0.0 82.2 jit_solution(3014769469337355880)
XLA Ops:
  7.1 1.6 %fusion.21 = f32[480,16]{1,0:T(8,128)S(1)} fusion(pred[512,32]{1,0:T(32,128)(4,1)S(1)} %iota_compare_fusion.6, pred[512,64]{1,0:T(32,128)(4,1)S(1)} %iota_compare_fusion.7, pred[512,128]{1,0:T(32,128)(4,1)S(1)} %iota_compare_fusion.8, pred[512,256]{1,0:T(32,128)(4,1)S(1)} %iota_compare_fusion.4, f32[2,16,512]{2,1,0:T(8,128)} %param.5), kind=kOutput, calls=%fused_computation.43 | convolution fusion | flops 48168960 | bytes 309248 | tf_op jit(solution)/shard_map/hw,wu->hu/dot_general | solution.py:284
  9.9 0.6 fusion.11
  10.8 0.7 select_maximum_fusion
  11.6 4.9 %collective-permute-start = (f32[11,4,512]{2,1,0:T(4,128)S(1)}, f32[11,4,512]{2,1,0:T(4,128)S(1)}, u32[]{:S(2)}, u32[]{:S(2)}) collective-permute-start(f32[11,4,512]{2,1,0:T(4,128)S(1)} %get-tuple-element.94), channel_id=1, source_target_pairs={{0,4},{4,8},{8,12},{1,5},{5,9},{9,13},{2,6},{6,10},{10,14},{3,7},{... | collective-permute-start | bytes 270344 | tf_op jit(solution)/shard_map/ppermute | solution.py:29
  16.6 1.3 %collective-permute-start.1 = (f32[11,4,512]{2,1,0:T(4,128)S(1)}, f32[11,4,512]{2,1,0:T(4,128)S(1)}, u32[]{:S(2)}, u32[]{:S(2)}) collective-permute-start(f32[11,4,512]{2,1,0:T(4,128)S(1)} %get-tuple-element.95), channel_id=1, source_target_pairs={{4,0},{8,4},{12,8},{5,1},{9,5},{13,9},{6,2},{10,6},{14,10},{7,3},{... | collective-permute-start | bytes 270344 | tf_op jit(solution)/shard_map/ppermute | solution.py:31
  18.2 0.5 collective-permute-done
  18.7 4.3 %collective-permute-done.1 = f32[11,4,512]{2,1,0:T(4,128)S(1)} collective-permute-done((f32[11,4,512]{2,1,0:T(4,128)S(1)}, f32[11,4,512]{2,1,0:T(4,128)S(1)}, u32[]{:S(2)}, u32[]{:S(2)}) %collective-permute-start.1) | collective-permute-done | bytes 90144 | tf_op jit(solution)/shard_map/ppermute | solution.py:31
  23.1 1.3 %collective-permute-start.2 = (f32[11,24,4]{2,1,0:T(8,128)S(1)}, f32[11,24,4]{2,1,0:T(8,128)S(1)}, u32[]{:S(2)}, u32[]{:S(2)}) collective-permute-start(f32[11,24,4]{2,1,0:T(8,128)S(1)} %get-tuple-element.86), channel_id=1, source_target_pairs={{0,1},{1,2},{2,3},{4,5},{5,6},{6,7},{8,9},{9,10},{10,11},{12,13},{... | collective-permute-start | bytes 12680 | tf_op jit(solution)/shard_map/ppermute | solution.py:29
  24.4 1.3 %collective-permute-start.3 = (f32[11,24,4]{2,1,0:T(8,128)S(1)}, f32[11,24,4]{2,1,0:T(8,128)S(1)}, u32[]{:S(2)}, u32[]{:S(2)}) collective-permute-start(f32[11,24,4]{2,1,0:T(8,128)S(1)} %get-tuple-element.87), channel_id=1, source_target_pairs={{1,0},{2,1},{3,2},{5,4},{6,5},{7,6},{9,8},{10,9},{11,10},{13,12},{... | collective-permute-start | bytes 12680 | tf_op jit(solution)/shard_map/ppermute | solution.py:31
  25.8 3.6 %collective-permute-done.3 = f32[11,24,4]{2,1,0:T(8,128)S(1)} collective-permute-done((f32[11,24,4]{2,1,0:T(8,128)S(1)}, f32[11,24,4]{2,1,0:T(8,128)S(1)}, u32[]{:S(2)}, u32[]{:S(2)}) %collective-permute-start.3) | collective-permute-done | bytes 4256 | tf_op jit(solution)/shard_map/ppermute | solution.py:31
  29.4 0.4 pad_maximum_fusion
  32.5 5.5 %collective-permute-start.5 = (f32[3,8,256]{2,1,0:T(8,128)S(1)}, f32[3,8,256]{2,1,0:T(8,128)S(1)}, u32[]{:S(2)}, u32[]{:S(2)}) collective-permute-start(f32[3,8,256]{2,1,0:T(8,128)S(1)} %fusion.26), channel_id=1, source_target_pairs={{0,2},{1,3},{2,0},{3,1},{4,6},{5,7},{6,4},{7,5},{8,10},{9,11},{10,... | collective-permute-start | bytes 73736 | tf_op jit(solution)/shard_map/ppermute | solution.py:151
  38.0 2.0 %collective-permute-done.5 = f32[3,8,256]{2,1,0:T(8,128)S(1)} collective-permute-done((f32[3,8,256]{2,1,0:T(8,128)S(1)}, f32[3,8,256]{2,1,0:T(8,128)S(1)}, u32[]{:S(2)}, u32[]{:S(2)}) %collective-permute-start.5) | collective-permute-done | bytes 24608 | tf_op jit(solution)/shard_map/ppermute | solution.py:151
  40.0 1.5 %collective-permute-done.4 = f32[3,8,256]{2,1,0:T(8,128)S(1)} collective-permute-done((f32[3,8,256]{2,1,0:T(8,128)S(1)}, f32[3,8,256]{2,1,0:T(8,128)S(1)}, u32[]{:S(2)}, u32[]{:S(2)}) %collective-permute-start.4) | collective-permute-done | bytes 24608 | tf_op jit(solution)/shard_map/ppermute | solution.py:151
  41.5 0.6 gather_fusion
  42.1 2.4 %collective-permute-start.8 = (f32[4,3,8,256]{3,2,1,0:T(8,128)S(1)}, f32[4,3,8,256]{3,2,1,0:T(8,128)S(1)}, u32[]{:S(2)}, u32[]{:S(2)}) collective-permute-start(f32[4,3,8,256]{3,2,1,0:T(8,128)S(1)} %gather_fusion), channel_id=1, source_target_pairs={{0,8},{4,12},{8,0},{12,4},{1,9},{5,13},{9,1},{13,5},{2,10},{6,14},... | collective-permute-start | bytes 294920 | tf_op jit(solution)/shard_map/ppermute | solution.py:151
  44.5 3.8 %collective-permute-start.9 = (f32[4,3,8,256]{3,2,1,0:T(8,128)S(1)}, f32[4,3,8,256]{3,2,1,0:T(8,128)S(1)}, u32[]{:S(2)}, u32[]{:S(2)}) collective-permute-start(f32[4,3,8,256]{3,2,1,0:T(8,128)S(1)} %gather_fusion), channel_id=1, source_target_pairs={{0,12},{4,0},{8,4},{12,8},{1,13},{5,1},{9,5},{13,9},{2,14},{6,2},{... | collective-permute-start | bytes 294920 | tf_op jit(solution)/shard_map/ppermute | solution.py:151
  48.3 6.7 %collective-permute-done.8 = f32[4,3,8,256]{3,2,1,0:T(8,128)S(1)} collective-permute-done((f32[4,3,8,256]{3,2,1,0:T(8,128)S(1)}, f32[4,3,8,256]{3,2,1,0:T(8,128)S(1)}, u32[]{:S(2)}, u32[]{:S(2)}) %collective-permute-start.8) | collective-permute-done | bytes 98336 | tf_op jit(solution)/shard_map/ppermute | solution.py:151
  55.0 0.6 gather_fusion.1
  55.8 0.8 %slice.2013 = f32[16,8,32]{2,1,0:T(8,128)S(1)} slice(f32[16,8,2816]{2,1,0:T(8,128)} %bitcast.859), slice={[0:16], [0:8], [2688:2720]} | slice | bytes 32768 | tf_op jit(solution)/shard_map/slice | solution.py:185
  56.6 0.8 %slice.2001 = f32[16,8,128]{2,1,0:T(8,128)S(1)} slice(f32[16,8,2816]{2,1,0:T(8,128)} %bitcast.860), slice={[0:16], [0:8], [2560:2688]} | slice | bytes 131072 | tf_op jit(solution)/shard_map/slice | solution.py:185
  57.5 1.0 %slice.1989 = f32[16,8,512]{2,1,0:T(8,128)S(1)} slice(f32[16,8,2816]{2,1,0:T(8,128)} %bitcast.861), slice={[0:16], [0:8], [2048:2560]} | slice | bytes 524288 | tf_op jit(solution)/shard_map/slice | solution.py:185
  58.5 1.3 %slice.1977 = f32[16,8,2048]{2,1,0:T(8,128)S(1)} slice(f32[16,8,2816]{2,1,0:T(8,128)} %bitcast.862), slice={[0:16], [0:8], [0:2048]} | slice | bytes 2097152 | tf_op jit(solution)/shard_map/slice | solution.py:185
  61.4 0.3 copy.139
  62.6 0.5 fusion.81
  63.7 1.0 %fusion.3 = f32[3,16,512]{2,1,0:T(8,128)S(1)} fusion(f32[3,16,1024]{2,1,0:T(8,128)S(1)} %convolution_bitcast_fusion.2, s32[1024]{0:T(1024)S(1)} %get-tuple-element.164, s32[1024]{0:T(1024)S(1)} %get-tuple-element.165, pred[1024]{0:T(1024)(128)(4,1)S(1)} %fusion.739), kind=kOutput, calls=%fused_computation.6 | convolution fusion | flops 303038464 | bytes 304128 | tf_op jit(solution)/shard_map/...hw,wv->...hv/dot_general | solution.py:59
  65.3 0.3 fusion.24
  69.1 1.3 %fusion.1 = f32[3,16,1024]{2,1,0:T(8,128)S(1)} fusion(s32[1024]{0:T(1024)S(1)} %get-tuple-element.164, s32[1024]{0:T(1024)S(1)} %get-tuple-element.165, pred[1024]{0:T(1024)(128)(4,1)S(1)} %fusion.739, f32[1,16,512]{2,1,0:T(8,128)S(1)} %get-tuple-element.97, f32[1,16,512]{2,1,0:T(8,128)S(1)} %get-tuple-element.96, f32[1,16,512]{2,1,0:T(8,128)S(1)} %get-tuple-element.8), kind=kOutput, calls=%fused_computation.5 | convolution fusion | flops 303087616 | bytes 304128 | tf_op jit(solution)/shard_map/...hv,wv->...hw/dot_general | solution.py:76
  70.5 0.4 convolution_bitcast_fusion
  71.1 0.5 fusion.185
  71.9 0.8 fusion.19
  74.7 0.6 pad_maximum_fusion.6
  (197 shorter events, 14.7 us)
Async XLA Ops:
  6.5 2.7 %copy-start = (f32[6,16,512]{2,1,0:T(8,128)S(1)}, f32[6,16,512]{2,1,0:T(8,128)}, u32[]{:S(2)}) copy-start(f32[6,16,512]{2,1,0:T(8,128)} %param.4) | copy-start | bytes 589828
  6.5 49.3 %all-gather.3.cloned.1.call-start = ((), (), s32[]{:S(2)}) async-start(), calls=%async_computation | async-start | bytes 1531904 | tf_op jit(solution)/shard_map/all_gather | solution.py:180
  7.1 2.6 %copy-start.1 = (f32[2,16,512]{2,1,0:T(8,128)S(1)}, f32[2,16,512]{2,1,0:T(8,128)}, u32[]{:S(2)}) copy-start(f32[2,16,512]{2,1,0:T(8,128)} %param.5) | copy-start | bytes 196612
  9.5 2.0 %copy-start.2 = (f32[3,16,512]{2,1,0:T(8,128)S(1)}, f32[3,16,512]{2,1,0:T(8,128)}, u32[]{:S(2)}) copy-start(f32[3,16,512]{2,1,0:T(8,128)} %param.3) | copy-start | bytes 294916
  11.6 7.1 %collective-permute-start = (f32[11,4,512]{2,1,0:T(4,128)S(1)}, f32[11,4,512]{2,1,0:T(4,128)S(1)}, u32[]{:S(2)}, u32[]{:S(2)}) collective-permute-start(f32[11,4,512]{2,1,0:T(4,128)S(1)} %get-tuple-element.94), channel_id=1, source_target_pairs={{0,4},{4,8},{8,12},{1,5},{5,9},{9,13},{2,6},{6,10},{10,14},{3,7},{... | collective-permute-start | bytes 270344 | tf_op jit(solution)/shard_map/ppermute | solution.py:29
  16.6 6.4 %collective-permute-start.1 = (f32[11,4,512]{2,1,0:T(4,128)S(1)}, f32[11,4,512]{2,1,0:T(4,128)S(1)}, u32[]{:S(2)}, u32[]{:S(2)}) collective-permute-start(f32[11,4,512]{2,1,0:T(4,128)S(1)} %get-tuple-element.95), channel_id=1, source_target_pairs={{4,0},{8,4},{12,8},{5,1},{9,5},{13,9},{6,2},{10,6},{14,10},{7,3},{... | collective-permute-start | bytes 270344 | tf_op jit(solution)/shard_map/ppermute | solution.py:31
  23.1 2.6 %collective-permute-start.2 = (f32[11,24,4]{2,1,0:T(8,128)S(1)}, f32[11,24,4]{2,1,0:T(8,128)S(1)}, u32[]{:S(2)}, u32[]{:S(2)}) collective-permute-start(f32[11,24,4]{2,1,0:T(8,128)S(1)} %get-tuple-element.86), channel_id=1, source_target_pairs={{0,1},{1,2},{2,3},{4,5},{5,6},{6,7},{8,9},{9,10},{10,11},{12,13},{... | collective-permute-start | bytes 12680 | tf_op jit(solution)/shard_map/ppermute | solution.py:29
  24.4 5.0 %collective-permute-start.3 = (f32[11,24,4]{2,1,0:T(8,128)S(1)}, f32[11,24,4]{2,1,0:T(8,128)S(1)}, u32[]{:S(2)}, u32[]{:S(2)}) collective-permute-start(f32[11,24,4]{2,1,0:T(8,128)S(1)} %get-tuple-element.87), channel_id=1, source_target_pairs={{1,0},{2,1},{3,2},{5,4},{6,5},{7,6},{9,8},{10,9},{11,10},{13,12},{... | collective-permute-start | bytes 12680 | tf_op jit(solution)/shard_map/ppermute | solution.py:31
  32.3 5.7 %collective-permute-start.6 = (f32[3,8,256]{2,1,0:T(8,128)S(1)}, f32[3,8,256]{2,1,0:T(8,128)S(1)}, u32[]{:S(2)}, u32[]{:S(2)}) collective-permute-start(f32[3,8,256]{2,1,0:T(8,128)S(1)} %fusion.26), channel_id=1, source_target_pairs={{0,3},{1,0},{2,1},{3,2},{4,7},{5,4},{6,5},{7,6},{8,11},{9,8},{10,9... | collective-permute-start | bytes 73736 | tf_op jit(solution)/shard_map/ppermute | solution.py:151
  32.5 7.5 %collective-permute-start.5 = (f32[3,8,256]{2,1,0:T(8,128)S(1)}, f32[3,8,256]{2,1,0:T(8,128)S(1)}, u32[]{:S(2)}, u32[]{:S(2)}) collective-permute-start(f32[3,8,256]{2,1,0:T(8,128)S(1)} %fusion.26), channel_id=1, source_target_pairs={{0,2},{1,3},{2,0},{3,1},{4,6},{5,7},{6,4},{7,5},{8,10},{9,11},{10,... | collective-permute-start | bytes 73736 | tf_op jit(solution)/shard_map/ppermute | solution.py:151
  38.0 3.6 %collective-permute-start.4 = (f32[3,8,256]{2,1,0:T(8,128)S(1)}, f32[3,8,256]{2,1,0:T(8,128)S(1)}, u32[]{:S(2)}, u32[]{:S(2)}) collective-permute-start(f32[3,8,256]{2,1,0:T(8,128)S(1)} %fusion.26), channel_id=1, source_target_pairs={{0,1},{1,2},{2,3},{3,0},{4,5},{5,6},{6,7},{7,4},{8,9},{9,10},{10,1... | collective-permute-start | bytes 73736 | tf_op jit(solution)/shard_map/ppermute | solution.py:151
  42.1 12.9 %collective-permute-start.8 = (f32[4,3,8,256]{3,2,1,0:T(8,128)S(1)}, f32[4,3,8,256]{3,2,1,0:T(8,128)S(1)}, u32[]{:S(2)}, u32[]{:S(2)}) collective-permute-start(f32[4,3,8,256]{3,2,1,0:T(8,128)S(1)} %gather_fusion), channel_id=1, source_target_pairs={{0,8},{4,12},{8,0},{12,4},{1,9},{5,13},{9,1},{13,5},{2,10},{6,14},... | collective-permute-start | bytes 294920 | tf_op jit(solution)/shard_map/ppermute | solution.py:151
  44.5 10.5 %collective-permute-start.7 = (f32[4,3,8,256]{3,2,1,0:T(8,128)S(1)}, f32[4,3,8,256]{3,2,1,0:T(8,128)S(1)}, u32[]{:S(2)}, u32[]{:S(2)}) collective-permute-start(f32[4,3,8,256]{3,2,1,0:T(8,128)S(1)} %gather_fusion), channel_id=1, source_target_pairs={{0,4},{4,8},{8,12},{12,0},{1,5},{5,9},{9,13},{13,1},{2,6},{6,10},{... | collective-permute-start | bytes 294920 | tf_op jit(solution)/shard_map/ppermute | solution.py:151
  44.5 10.5 %collective-permute-start.9 = (f32[4,3,8,256]{3,2,1,0:T(8,128)S(1)}, f32[4,3,8,256]{3,2,1,0:T(8,128)S(1)}, u32[]{:S(2)}, u32[]{:S(2)}) collective-permute-start(f32[4,3,8,256]{3,2,1,0:T(8,128)S(1)} %gather_fusion), channel_id=1, source_target_pairs={{0,12},{4,0},{8,4},{12,8},{1,13},{5,1},{9,5},{13,9},{2,14},{6,2},{... | collective-permute-start | bytes 294920 | tf_op jit(solution)/shard_map/ppermute | solution.py:151
Sparse Core Ops, SparseCore 0:
  11.6 44.1 all-gather.2

commit v10 on v8

--- a/solution.py
+++ b/solution.py
@@ -148,25 +148,27 @@
     count_rows = lax.axis_size(ROWS)
     count_cols = lax.axis_size(COLS)
     planes = blocks[0].shape[0]
-    runs = [-(-b.shape[1] * b.shape[2] // 128) * 128 for b in blocks]
-    flat = jnp.concatenate(
-        [
-            jnp.pad(b.reshape(planes, -1), ((0, 0), (0, run - b.shape[1] * b.shape[2])))
-            for b, run in zip(blocks, runs)
-        ],
-        axis=1,
-    )
-    stacked = lax.all_gather(flat, GRID, axis=0, tiled=False)
+    tiles = []
+    for b in blocks:
+        run = b.shape[1] * b.shape[2]
+        padded = jnp.pad(b.reshape(planes, run), ((0, 0), (0, -run % 128)))
+        tiles.append(padded.reshape(planes, -1, 128).transpose(1, 0, 2))
+    packed = jnp.concatenate(tiles, axis=0)
+    stacked = lax.all_gather(packed, GRID, axis=1, tiled=False)
     grids = []
-    offset = 0
-    for b, run in zip(blocks, runs):
+    first = 0
+    for b, t in zip(blocks, tiles):
         _, height, width = b.shape
-        part = stacked[:, :, offset:offset + height * width]
-        offset += run
-        part = part.reshape(count_rows, count_cols, planes, height, width)
-        whole = part.transpose(2, 0, 3, 1, 4).reshape(
-            planes, count_rows * height, count_cols * width
-        )
+        part = stacked[first:first + t.shape[0]]
+        first += t.shape[0]
+        if width % 128 == 0:
+            part = part.reshape(height, width // 128, count_rows, count_cols, planes, 128)
+            whole = part.transpose(4, 2, 0, 3, 1, 5)
+        else:
+            part = part.transpose(2, 1, 0, 3).reshape(planes, count_rows, count_cols, -1)
+            part = part[..., : height * width].reshape(planes, count_rows, count_cols, height, width)
+            whole = part.transpose(0, 1, 3, 2, 4)
+        whole = whole.reshape(planes, count_rows * height, count_cols * width)
         grids.append([whole[k] for k in range(planes)])
     return grids
 

time: 82.9 us -> 79.2 us (0.955)
  local copies, waits for them, and re-layouts: 7.21 us -> 4.41 us
    slice x4, local copies, waits for them, and re-layouts: 3.95 us -> 0.47 us  [gather_grids(): part = stacked[first:first + t.shape[0]]]
    transpose x0 -> x4, local copies, waits for them, and re-layouts: none -> 0.92 us  [the longest x3 0.92 us: gather_grids(): part.transpose(2, 1, 0, 3).reshape(planes, count_rows, count_cols, -1)]
where the time goes in v10:
time: 79.2 us; the launch traced here: 78.9 us
  blocking collectives  23.5 us (30%)
  between operations  14.4 us (18%)
  other arithmetic  10.8 us (14%)
  starting transfers between devices  8.82 us (11%)
  matrix products  8.54 us (11%)
  waiting for transfers between devices  8.47 us (11%)
  local copies, waits for them, and re-layouts  4.41 us (6%)
    all_gather x1, blocking collectives, gather_grids(): stacked = lax.all_gather(packed, GRID, axis=1, tiled=False)  23.5 us
    ppermute x2, waiting for transfers between devices, with_halo(): lax.ppermute(head, axis, [(i + 1, i) for i in range(ends)])  7.94 us
    ppermute x2, starting transfers between devices, with_halo(): lax.ppermute(tail, axis, [(i, i + 1) for i in range(ends)])  6.24 us
    ppermute x2, starting transfers between devices, with_halo(): lax.ppermute(head, axis, [(i + 1, i) for i in range(ends)])  2.58 us
    dot_general x4, matrix products, prolong(): wider = jnp.einsum('...hv,wv->...hw', coarse, pairs(width), precision=HIGH)  2.39 us
    select_n x6, other arithmetic, sweep_ext(): return [jnp.where(mask, n, 0.0) for n in new]  1.99 us
    dot_general x4, matrix products, sum_cols(): return jnp.einsum('...hw,wv->...hv', x, m, precision=HIGH)  1.95 us
  transfers between devices with their start and end apart: 5, of which 3 were waited for; matrix products, arithmetic and copies ran while one was open for 4% of the time, Pallas kernels for 0%

profile of v10, /device:TPU:0, one launch (start us, length us, event | category | flops | bytes accessed | tf_op | source)
XLA Modules:
  0.0 78.9 jit_solution(387844043084996683)
XLA Ops:
  7.1 1.2 %fusion.11 = f32[480,16]{0,1:T(8,128)S(1)} fusion(pred[512,32]{1,0:T(32,128)(4,1)S(1)} %iota_compare_fusion.6, pred[512,64]{1,0:T(32,128)(4,1)S(1)} %iota_compare_fusion.7, pred[512,128]{1,0:T(32,128)(4,1)S(1)} %iota_compare_fusion.8, pred[512,256]{1,0:T(32,128)(4,1)S(1)} %iota_compare_fusion.4, f32[2,16,512]{2,1,0:T(8,128)} %param.5), kind=kOutput, calls=%fused_computation.22 | convolution fusion | flops 47923200 | bytes 309248 | tf_op jit(solution)/shard_map/hw,wu->hu/dot_general | solution.py:265
  9.4 0.6 fusion.12
  10.3 0.6 pad_maximum_fusion.5
  11.1 4.9 %collective-permute-start = (f32[11,4,512]{2,1,0:T(4,128)S(1)}, f32[11,4,512]{2,1,0:T(4,128)S(1)}, u32[]{:S(2)}, u32[]{:S(2)}) collective-permute-start(f32[11,4,512]{2,1,0:T(4,128)S(1)} %get-tuple-element.96), channel_id=1, source_target_pairs={{0,4},{4,8},{8,12},{1,5},{5,9},{9,13},{2,6},{6,10},{10,14},{3,7},{... | collective-permute-start | bytes 270344 | tf_op jit(solution)/shard_map/ppermute | solution.py:29
  16.1 1.3 %collective-permute-start.1 = (f32[11,4,512]{2,1,0:T(4,128)S(1)}, f32[11,4,512]{2,1,0:T(4,128)S(1)}, u32[]{:S(2)}, u32[]{:S(2)}) collective-permute-start(f32[11,4,512]{2,1,0:T(4,128)S(1)} %get-tuple-element.97), channel_id=1, source_target_pairs={{4,0},{8,4},{12,8},{5,1},{9,5},{13,9},{6,2},{10,6},{14,10},{7,3},{... | collective-permute-start | bytes 270344 | tf_op jit(solution)/shard_map/ppermute | solution.py:31
  17.7 0.5 collective-permute-done
  18.2 4.3 %collective-permute-done.1 = f32[11,4,512]{2,1,0:T(4,128)S(1)} collective-permute-done((f32[11,4,512]{2,1,0:T(4,128)S(1)}, f32[11,4,512]{2,1,0:T(4,128)S(1)}, u32[]{:S(2)}, u32[]{:S(2)}) %collective-permute-start.1) | collective-permute-done | bytes 90144 | tf_op jit(solution)/shard_map/ppermute | solution.py:31
  22.6 1.3 %collective-permute-start.2 = (f32[11,24,4]{2,1,0:T(8,128)S(1)}, f32[11,24,4]{2,1,0:T(8,128)S(1)}, u32[]{:S(2)}, u32[]{:S(2)}) collective-permute-start(f32[11,24,4]{2,1,0:T(8,128)S(1)} %get-tuple-element.88), channel_id=1, source_target_pairs={{0,1},{1,2},{2,3},{4,5},{5,6},{6,7},{8,9},{9,10},{10,11},{12,13},{... | collective-permute-start | bytes 12680 | tf_op jit(solution)/shard_map/ppermute | solution.py:29
  23.9 1.3 %collective-permute-start.3 = (f32[11,24,4]{2,1,0:T(8,128)S(1)}, f32[11,24,4]{2,1,0:T(8,128)S(1)}, u32[]{:S(2)}, u32[]{:S(2)}) collective-permute-start(f32[11,24,4]{2,1,0:T(8,128)S(1)} %get-tuple-element.89), channel_id=1, source_target_pairs={{1,0},{2,1},{3,2},{5,4},{6,5},{7,6},{9,8},{10,9},{11,10},{13,12},{... | collective-permute-start | bytes 12680 | tf_op jit(solution)/shard_map/ppermute | solution.py:31
  25.2 3.6 %collective-permute-done.3 = f32[11,24,4]{2,1,0:T(8,128)S(1)} collective-permute-done((f32[11,24,4]{2,1,0:T(8,128)S(1)}, f32[11,24,4]{2,1,0:T(8,128)S(1)}, u32[]{:S(2)}, u32[]{:S(2)}) %collective-permute-start.3) | collective-permute-done | bytes 4256 | tf_op jit(solution)/shard_map/ppermute | solution.py:31
  28.9 0.4 pad_maximum_fusion
  29.7 0.3 fusion.276
  30.0 0.3 fusion.286
  30.3 0.3 fusion.297
  31.5 0.3 fusion.26
  31.8 23.5 %all-gather = f32[16,48,128]{2,0,1:T(8,128)S(1)} all-gather(f32[16,3,128]{2,0,1:T(8,128)S(1)} %bitcast.873), channel_id=2, replica_groups=mesh['groups'=2,'tiles'=4,'band'=2,'stokes'=2] {'tiles','band','stokes'}, dimensions={1}, use_global_device_ids=true | all-gather | bytes 417792 | tf_op jit(solution)/shard_map/all_gather | solution.py:157
  55.4 0.9 %slice_bitcast_fusion.3 = (f32[8,16,1,128]{3,0,1,2:T(8,128)S(1)}, f32[8,16,1,128]{3,0,1,2:T(8,128)S(1)}) fusion(f32[22,128,128]{2,1,0:T(8,128)} %all-gather.4.cloned.1.call-done), kind=kLoop, calls=%fused_computation.363 | loop fusion | bytes 262144 | tf_op jit(solution)/shard_map/transpose | solution.py:168
  57.9 0.5 slice-done
  58.4 0.6 copy.178
  59.6 0.5 fusion.81
  60.1 0.3 fusion.91
  60.7 1.0 %fusion.3 = f32[3,16,512]{2,1,0:T(8,128)S(1)} fusion(f32[3,16,1024]{2,1,0:T(8,128)S(1)} %convolution_bitcast_fusion.2, s32[1024]{0:T(1024)S(1)} %get-tuple-element.166, s32[1024]{0:T(1024)S(1)} %get-tuple-element.167, pred[1024]{0:T(1024)(128)(4,1)S(1)} %fusion.739), kind=kOutput, calls=%fused_computation.4 | convolution fusion | flops 303038464 | bytes 304128 | tf_op jit(solution)/shard_map/...hw,wv->...hv/dot_general | solution.py:59
  62.3 0.3 fusion.24
  66.2 1.3 %fusion.1 = f32[3,16,1024]{2,1,0:T(8,128)S(1)} fusion(s32[1024]{0:T(1024)S(1)} %get-tuple-element.166, s32[1024]{0:T(1024)S(1)} %get-tuple-element.167, pred[1024]{0:T(1024)(128)(4,1)S(1)} %fusion.739, f32[1,16,512]{2,1,0:T(8,128)S(1)} %get-tuple-element.99, f32[1,16,512]{2,1,0:T(8,128)S(1)} %get-tuple-element.98, f32[1,16,512]{2,1,0:T(8,128)S(1)} %get-tuple-element.8), kind=kOutput, calls=%fused_computation.3 | convolution fusion | flops 303087616 | bytes 304128 | tf_op jit(solution)/shard_map/...hv,wv->...hw/dot_general | solution.py:76
  67.5 0.4 convolution_bitcast_fusion
  68.2 0.5 fusion.185
  68.6 0.3 fusion.186
  69.0 0.5 fusion.20
  69.8 0.3 fusion.251
  70.1 0.3 fusion.262
  70.4 0.3 fusion.241
  71.4 0.6 pad_maximum_fusion.4
  (179 shorter events, 11.0 us)
Async XLA Ops:
  6.5 2.1 %copy-start = (f32[6,16,512]{2,1,0:T(8,128)S(1)}, f32[6,16,512]{2,1,0:T(8,128)}, u32[]{:S(2)}) copy-start(f32[6,16,512]{2,1,0:T(8,128)} %param.4) | copy-start | bytes 589828
  6.5 48.9 %all-gather.4.cloned.1.call-start = ((), (), s32[]{:S(2)}) async-start(), calls=%async_computation | async-start | bytes 1531904 | tf_op jit(solution)/shard_map/all_gather | solution.py:157
  6.8 2.3 %copy-start.1 = (f32[2,16,512]{2,1,0:T(8,128)S(1)}, f32[2,16,512]{2,1,0:T(8,128)}, u32[]{:S(2)}) copy-start(f32[2,16,512]{2,1,0:T(8,128)} %param.5) | copy-start | bytes 196612
  9.4 1.6 %copy-start.2 = (f32[3,16,512]{2,1,0:T(8,128)S(1)}, f32[3,16,512]{2,1,0:T(8,128)}, u32[]{:S(2)}) copy-start(f32[3,16,512]{2,1,0:T(8,128)} %param.3) | copy-start | bytes 294916
  11.1 7.1 %collective-permute-start = (f32[11,4,512]{2,1,0:T(4,128)S(1)}, f32[11,4,512]{2,1,0:T(4,128)S(1)}, u32[]{:S(2)}, u32[]{:S(2)}) collective-permute-start(f32[11,4,512]{2,1,0:T(4,128)S(1)} %get-tuple-element.96), channel_id=1, source_target_pairs={{0,4},{4,8},{8,12},{1,5},{5,9},{9,13},{2,6},{6,10},{10,14},{3,7},{... | collective-permute-start | bytes 270344 | tf_op jit(solution)/shard_map/ppermute | solution.py:29
  16.1 6.4 %collective-permute-start.1 = (f32[11,4,512]{2,1,0:T(4,128)S(1)}, f32[11,4,512]{2,1,0:T(4,128)S(1)}, u32[]{:S(2)}, u32[]{:S(2)}) collective-permute-start(f32[11,4,512]{2,1,0:T(4,128)S(1)} %get-tuple-element.97), channel_id=1, source_target_pairs={{4,0},{8,4},{12,8},{5,1},{9,5},{13,9},{6,2},{10,6},{14,10},{7,3},{... | collective-permute-start | bytes 270344 | tf_op jit(solution)/shard_map/ppermute | solution.py:31
  22.6 2.6 %collective-permute-start.2 = (f32[11,24,4]{2,1,0:T(8,128)S(1)}, f32[11,24,4]{2,1,0:T(8,128)S(1)}, u32[]{:S(2)}, u32[]{:S(2)}) collective-permute-start(f32[11,24,4]{2,1,0:T(8,128)S(1)} %get-tuple-element.88), channel_id=1, source_target_pairs={{0,1},{1,2},{2,3},{4,5},{5,6},{6,7},{8,9},{9,10},{10,11},{12,13},{... | collective-permute-start | bytes 12680 | tf_op jit(solution)/shard_map/ppermute | solution.py:29
  23.9 5.0 %collective-permute-start.3 = (f32[11,24,4]{2,1,0:T(8,128)S(1)}, f32[11,24,4]{2,1,0:T(8,128)S(1)}, u32[]{:S(2)}, u32[]{:S(2)}) collective-permute-start(f32[11,24,4]{2,1,0:T(8,128)S(1)} %get-tuple-element.89), channel_id=1, source_target_pairs={{1,0},{2,1},{3,2},{5,4},{6,5},{7,6},{9,8},{10,9},{11,10},{13,12},{... | collective-permute-start | bytes 12680 | tf_op jit(solution)/shard_map/ppermute | solution.py:31
  57.2 1.2 %slice-start = ((f32[22,128,128]{2,1,0:T(8,128)}), f32[16,128,128]{2,1,0:T(8,128)S(1)}, s32[]{:S(2)}) async-start(f32[22,128,128]{2,1,0:T(8,128)} %all-gather.4.cloned.1.call-done), calls=%async_computation.1 | async-start | bytes 2097152 | tf_op jit(solution)/shard_map/slice | solution.py:162
  57.9 1.1 %slice-start.1 = ((f32[22,128,128]{2,1,0:T(8,128)}), f32[4,128,128]{2,1,0:T(8,128)S(1)}, s32[]{:S(2)}) async-start(f32[22,128,128]{2,1,0:T(8,128)} %all-gather.4.cloned.1.call-done), calls=%async_computation.2 | async-start | bytes 524288 | tf_op jit(solution)/shard_map/slice | solution.py:162
Sparse Core Ops, SparseCore 0:
  11.1 42.0 all-gather.3

commit v11 on v10

--- a/solution.py
+++ b/solution.py
@@ -131,12 +131,43 @@
         iterate = smooth_whole(iterate, source, noise, couplings, diagonal)
     image = apply_planes(iterate, [jnp.pad(p, 1) for p in iterate], noise, couplings)
     residual = restrict_sum(jnp.stack([s - a for s, a in zip(source, image)]))
-    coarse = prolong(
-        jnp.stack(cycle_whole([residual[k] for k in range(3)], hierarchy[1:], level_index + 1))
-    )
+    coarse = prolong(cycle_stacked(residual, hierarchy[1:], level_index + 1))
     iterate = [iterate[k] + coarse[k] for k in range(3)]
     for sweep_index in range(POST):
         iterate = smooth_whole(iterate, source, noise, couplings, diagonal)
+    return iterate
+
+
+def apply_stacked(iterate, noise, couplings):
+    padded = jnp.pad(iterate, ((0, 0), (1, 1), (1, 1)))
+    first = noise[0] * iterate[0] + noise[3] * iterate[1] + noise[4] * iterate[2]
+    second = noise[3] * iterate[0] + noise[1] * iterate[1] + noise[5] * iterate[2]
+    third = noise[4] * iterate[0] + noise[5] * iterate[1] + noise[2] * iterate[2]
+    totals = couplings[0] + couplings[1] + couplings[2] + couplings[3]
+    neighbours = (
+        couplings[0] * padded[:, 2:, 1:-1]
+        + couplings[1] * padded[:, :-2, 1:-1]
+        + couplings[2] * padded[:, 1:-1, 2:]
+        + couplings[3] * padded[:, 1:-1, :-2]
+    )
+    return jnp.stack([first, second, third]) + totals * iterate - neighbours
+
+
+def cycle_stacked(source, hierarchy, level_index):
+    noise, down, right = hierarchy[0]
+    noise = jnp.stack(noise)
+    couplings = jnp.stack(couplings_from(down, right))
+    diagonal = noise[0:3] + (couplings[0] + couplings[1] + couplings[2] + couplings[3])
+    iterate = OMEGA * source / diagonal
+    sweeps = COARSE_SWEEPS - 1 if level_index == LEVELS - 1 else PRE - 1
+    for sweep_index in range(sweeps):
+        iterate = iterate + OMEGA * (source - apply_stacked(iterate, noise, couplings)) / diagonal
+    if level_index == LEVELS - 1:
+        return iterate
+    residual = restrict_sum(source - apply_stacked(iterate, noise, couplings))
+    iterate = iterate + prolong(cycle_stacked(residual, hierarchy[1:], level_index + 1))
+    for sweep_index in range(POST):
+        iterate = iterate + OMEGA * (source - apply_stacked(iterate, noise, couplings)) / diagonal
     return iterate
 
 

time: 79.2 us -> 100 us (1.26)
  local copies, waits for them, and re-layouts: 4.41 us -> 17.1 us
  other arithmetic: 10.8 us -> 19.2 us
  waiting for transfers between devices: 8.47 us -> 3.51 us
  blocking collectives: 23.5 us -> 26 us
  matrix products: 8.54 us -> 9.64 us
    another operation x0 -> x13, local copies, waits for them, and re-layouts: none -> 7.12 us  [the longest x3 2.13 us: apply_stacked(): noise[5] * iterate[2]]
    ppermute x2, waiting for transfers between devices: 7.94 us -> 3.47 us  [with_halo(): lax.ppermute(head, axis, [(i + 1, i) for i in range(ends)])]
    slice x13 -> x22, local copies, waits for them, and re-layouts: 0.22 us -> 3.69 us  [gather_grids(): grids.append([whole[k] for k in range(planes)])]
    div x8, other arithmetic: 0.04 us -> 3.51 us  [pairs(): hit = rows // 2 == cols if pick is None else rows == 2 * cols + pick]
    and x8, other arithmetic: 0.06 us -> 3.31 us  [pairs(): hit = rows // 2 == cols if pick is None else rows == 2 * cols + pick]
    all_gather x1, blocking collectives: 23.5 us -> 26 us  [gather_grids(): stacked = lax.all_gather(packed, GRID, axis=1, tiled=False)]
    unnamed x10 -> x88, local copies, waits for them, and re-layouts: 0.05 us -> 2.31 us
    squeeze x16 -> x0, local copies, waits for them, and re-layouts: 1.34 us -> none  [gather_grids(): grids.append([whole[k] for k in range(planes)])]
  transfers between devices with their start and end apart: 5 -> 5, of which waited for: 3 -> 1; matrix products, arithmetic and copies ran while one was open for 4% -> 12% of each run, Pallas kernels for 0% -> 0%
where the time goes in v11:
time: 100 us; the launch traced here: 99.2 us
  blocking collectives  26 us (26%)
  other arithmetic  19.2 us (19%)
  local copies, waits for them, and re-layouts  17.1 us (17%)
  between operations  14.9 us (15%)
  matrix products  9.64 us (10%)
  starting transfers between devices  8.99 us (9%)
  waiting for transfers between devices  3.51 us (4%)
    all_gather x1, blocking collectives, gather_grids(): stacked = lax.all_gather(packed, GRID, axis=1, tiled=False)  26 us
    ppermute x2, starting transfers between devices, with_halo(): lax.ppermute(tail, axis, [(i, i + 1) for i in range(ends)])  6.4 us
    slice x22, local copies, waits for them, and re-layouts, gather_grids(): grids.append([whole[k] for k in range(planes)])  3.69 us
    div x8, other arithmetic, pairs(): hit = rows // 2 == cols if pick is None else rows == 2 * cols + pick  3.51 us
    ppermute x2, waiting for transfers between devices, with_halo(): lax.ppermute(head, axis, [(i + 1, i) for i in range(ends)])  3.47 us
    and x8, other arithmetic, pairs(): hit = rows // 2 == cols if pick is None else rows == 2 * cols + pick  3.31 us
    dot_general x4, matrix products, prolong(): wider = jnp.einsum('...hv,wv->...hw', coarse, pairs(width), precision=HIGH)  3.28 us
    ppermute x2, starting transfers between devices, with_halo(): lax.ppermute(head, axis, [(i + 1, i) for i in range(ends)])  2.58 us
  transfers between devices with their start and end apart: 5, of which 1 were waited for; matrix products, arithmetic and copies ran while one was open for 12% of the time, Pallas kernels for 0%

profile of v11, /device:TPU:0, one launch (start us, length us, event | category | flops | bytes accessed | tf_op | source)
XLA Modules:
  0.0 99.2 jit_solution(7979716573703364066)
XLA Ops:
  7.1 1.2 %fusion.13 = f32[480,16]{0,1:T(8,128)S(1)} fusion(pred[512,32]{1,0:T(32,128)(4,1)S(1)} %iota_compare_fusion.6, pred[512,64]{1,0:T(32,128)(4,1)S(1)} %iota_compare_fusion.7, pred[512,128]{1,0:T(32,128)(4,1)S(1)} %iota_compare_fusion.8, pred[512,256]{1,0:T(32,128)(4,1)S(1)} %iota_compare_fusion.4, f32[2,16,512]{2,1,0:T(8,128)} %param.5), kind=kOutput, calls=%fused_computation.24 | convolution fusion | flops 47923200 | bytes 309248 | tf_op jit(solution)/shard_map/hw,wu->hu/dot_general | solution.py:296
  10.4 0.6 pad_maximum_fusion.5
  11.2 4.9 %collective-permute-start = (f32[11,4,512]{2,1,0:T(4,128)S(1)}, f32[11,4,512]{2,1,0:T(4,128)S(1)}, u32[]{:S(2)}, u32[]{:S(2)}) collective-permute-start(f32[11,4,512]{2,1,0:T(4,128)S(1)} %get-tuple-element.54), channel_id=1, source_target_pairs={{0,4},{4,8},{8,12},{1,5},{5,9},{9,13},{2,6},{6,10},{10,14},{3,7},{... | collective-permute-start | bytes 270344 | tf_op jit(solution)/shard_map/ppermute | solution.py:29
  16.1 1.3 %collective-permute-start.1 = (f32[11,4,512]{2,1,0:T(4,128)S(1)}, f32[11,4,512]{2,1,0:T(4,128)S(1)}, u32[]{:S(2)}, u32[]{:S(2)}) collective-permute-start(f32[11,4,512]{2,1,0:T(4,128)S(1)} %get-tuple-element.55), channel_id=1, source_target_pairs={{4,0},{8,4},{12,8},{5,1},{9,5},{13,9},{6,2},{10,6},{14,10},{7,3},{... | collective-permute-start | bytes 270344 | tf_op jit(solution)/shard_map/ppermute | solution.py:31
  24.2 0.8 iota_compare_fusion.1
  26.3 1.5 %collective-permute-start.2 = (f32[11,24,4]{2,1,0:T(8,128)S(1)}, f32[11,24,4]{2,1,0:T(8,128)S(1)}, u32[]{:S(2)}, u32[]{:S(2)}) collective-permute-start(f32[11,24,4]{2,1,0:T(8,128)S(1)} %get-tuple-element.46), channel_id=1, source_target_pairs={{0,1},{1,2},{2,3},{4,5},{5,6},{6,7},{8,9},{9,10},{10,11},{12,13},{... | collective-permute-start | bytes 12680 | tf_op jit(solution)/shard_map/ppermute | solution.py:29
  27.8 1.3 %collective-permute-start.3 = (f32[11,24,4]{2,1,0:T(8,128)S(1)}, f32[11,24,4]{2,1,0:T(8,128)S(1)}, u32[]{:S(2)}, u32[]{:S(2)}) collective-permute-start(f32[11,24,4]{2,1,0:T(8,128)S(1)} %get-tuple-element.47), channel_id=1, source_target_pairs={{1,0},{2,1},{3,2},{5,4},{6,5},{7,6},{9,8},{10,9},{11,10},{13,12},{... | collective-permute-start | bytes 12680 | tf_op jit(solution)/shard_map/ppermute | solution.py:31
  29.2 3.5 %collective-permute-done.3 = f32[11,24,4]{2,1,0:T(8,128)S(1)} collective-permute-done((f32[11,24,4]{2,1,0:T(8,128)S(1)}, f32[11,24,4]{2,1,0:T(8,128)S(1)}, u32[]{:S(2)}, u32[]{:S(2)}) %collective-permute-start.3) | collective-permute-done | bytes 4256 | tf_op jit(solution)/shard_map/ppermute | solution.py:31
  35.6 26.0 %all-gather = f32[16,48,128]{2,0,1:T(8,128)S(1)} all-gather(f32[16,3,128]{2,0,1:T(8,128)S(1)} %bitcast.330), channel_id=2, replica_groups=mesh['groups'=2,'tiles'=4,'band'=2,'stokes'=2] {'tiles','band','stokes'}, dimensions={1}, use_global_device_ids=true | all-gather | bytes 417792 | tf_op jit(solution)/shard_map/all_gather | solution.py:188
  61.7 0.9 slice_bitcast_fusion.3
  62.6 0.7 squeeze_stack_squeeze.42
  63.6 0.7 squeeze_stack_squeeze.40
  64.3 0.7 squeeze_stack_squeeze.44
  65.0 0.7 squeeze_stack_squeeze.43
  65.9 0.7 squeeze_stack_squeeze.39
  66.6 0.7 squeeze_stack_squeeze.38
  67.3 0.7 squeeze_stack_squeeze.36
  68.0 0.7 squeeze_stack_squeeze.35
  68.9 1.3 %slice.1743 = f32[16,128,128]{2,1,0:T(8,128)S(1)} slice(f32[22,128,128]{2,1,0:T(8,128)} %all-gather.4.cloned.1.call-done), slice={[0:16], [0:128], [0:128]} | slice | bytes 2097152 | tf_op jit(solution)/shard_map/slice | solution.py:193
  71.2 0.7 fusion.662
  72.0 0.8 slice.1428
  72.8 0.8 slice.1426
  73.6 0.8 slice.1424
  74.4 0.8 squeeze_stack_squeeze.34
  75.1 0.8 squeeze_stack_squeeze.33
  75.9 0.8 copy.88
  76.7 0.8 copy.89
  77.4 0.9 pad_slice_fusion.82
  80.1 1.0 multiply_divide_fusion.2
  85.1 1.4 %fusion.1 = f32[3,16,1024]{2,1,0:T(8,128)S(1)} fusion(s32[1024]{0:T(1024)S(1)} %copy-done.24, s32[1024]{0:T(1024)S(1)} %copy-done.25, pred[1024]{0:T(1024)(128)(4,1)S(1)} %copy-done.40, f32[3,16,512]{2,1,0:T(8,128)S(1)} %fusion.223, f32[3,16,512]{2,1,0:T(8,128)S(1)} %get-tuple-element.140, f32[1,16,512]{2,1,0:T(8,128)S(1)} %get-tuple-element.69, ...), kind=kOutput, calls=%fused_computation.3 | convolution fusion | flops 303505408 | bytes 762880 | tf_op jit(solution)/shard_map/...hv,wv->...hw/dot_general | solution.py:76
  88.4 1.3 %fusion.22 = f32[3,10,516]{2,1,0:T(8,128)S(1)} fusion(s32[516]{0:T(1024)S(1)} %copy-done.22, s32[516]{0:T(1024)S(1)} %copy-done.23, pred[516]{0:T(1024)(128)(4,1)S(1)} %copy-done.39, s32[]{:T(128)S(6)} %select_n.163, s32[]{:T(128)S(6)} %select_n.164, f32[1,32,1024]{2,1,0:T(8,128)S(1)} %get-tuple-element.32, f32[1,32,1024]{2,1,0:T(8,128)S(1)} %get-tuple-element.31, ...), kind=kOutput, calls=%fused_computation.38 | convolution fusion | flops 48347136 | bytes 498692 | tf_op jit(solution)/shard_map/...hv,wv->...hw/dot_general | solution.py:76
  91.7 0.6 pad_maximum_fusion.4
  (265 shorter events, 24.6 us)
Async XLA Ops:
  6.5 2.1 %copy-start = (f32[6,16,512]{2,1,0:T(8,128)S(1)}, f32[6,16,512]{2,1,0:T(8,128)}, u32[]{:S(2)}) copy-start(f32[6,16,512]{2,1,0:T(8,128)} %param.4) | copy-start | bytes 589828
  6.5 55.1 %all-gather.4.cloned.1.call-start = ((), (), s32[]{:S(2)}) async-start(), calls=%async_computation | async-start | bytes 1531904 | tf_op jit(solution)/shard_map/all_gather | solution.py:188
  6.7 28.5 %copy-start.34 = (pred[512]{0:T(512)(128)(4,1)}, pred[512]{0:T(512)(128)(4,1)S(1)}, u32[]{:S(2)}) copy-start(pred[512]{0:T(512)(128)(4,1)S(1)} %get-tuple-element.147) | copy-start | bytes 1540
  6.8 28.5 %copy-start.17 = (s32[512]{0:T(512)}, s32[512]{0:T(512)S(1)}, u32[]{:S(2)}) copy-start(s32[512]{0:T(512)S(1)} %get-tuple-element.157) | copy-start | bytes 6148
  6.8 28.5 %copy-start.19 = (s32[512]{0:T(512)}, s32[512]{0:T(512)S(1)}, u32[]{:S(2)}) copy-start(s32[512]{0:T(512)S(1)} %get-tuple-element.158) | copy-start | bytes 6148
  6.8 2.3 %copy-start.7 = (f32[2,16,512]{2,1,0:T(8,128)S(1)}, f32[2,16,512]{2,1,0:T(8,128)}, u32[]{:S(2)}) copy-start(f32[2,16,512]{2,1,0:T(8,128)} %param.5) | copy-start | bytes 196612
  7.1 28.0 %copy-start.13 = (pred[16,8]{0,1:T(8,128)(4,1)}, pred[16,8]{0,1:T(8,128)(4,1)S(1)}, u32[]{:S(2)}) copy-start(pred[16,8]{0,1:T(8,128)(4,1)S(1)} %iota_compare_fusion.18) | copy-start | bytes 388
  9.4 1.6 %copy-start.12 = (f32[3,16,512]{2,1,0:T(8,128)S(1)}, f32[3,16,512]{2,1,0:T(8,128)}, u32[]{:S(2)}) copy-start(f32[3,16,512]{2,1,0:T(8,128)} %param.3) | copy-start | bytes 294916
  11.2 15.0 %collective-permute-start = (f32[11,4,512]{2,1,0:T(4,128)S(1)}, f32[11,4,512]{2,1,0:T(4,128)S(1)}, u32[]{:S(2)}, u32[]{:S(2)}) collective-permute-start(f32[11,4,512]{2,1,0:T(4,128)S(1)} %get-tuple-element.54), channel_id=1, source_target_pairs={{0,4},{4,8},{8,12},{1,5},{5,9},{9,13},{2,6},{6,10},{10,14},{3,7},{... | collective-permute-start | bytes 270344 | tf_op jit(solution)/shard_map/ppermute | solution.py:29
  16.1 10.1 %collective-permute-start.1 = (f32[11,4,512]{2,1,0:T(4,128)S(1)}, f32[11,4,512]{2,1,0:T(4,128)S(1)}, u32[]{:S(2)}, u32[]{:S(2)}) collective-permute-start(f32[11,4,512]{2,1,0:T(4,128)S(1)} %get-tuple-element.55), channel_id=1, source_target_pairs={{4,0},{8,4},{12,8},{5,1},{9,5},{13,9},{6,2},{10,6},{14,10},{7,3},{... | collective-permute-start | bytes 270344 | tf_op jit(solution)/shard_map/ppermute | solution.py:31
  26.3 2.8 %collective-permute-start.2 = (f32[11,24,4]{2,1,0:T(8,128)S(1)}, f32[11,24,4]{2,1,0:T(8,128)S(1)}, u32[]{:S(2)}, u32[]{:S(2)}) collective-permute-start(f32[11,24,4]{2,1,0:T(8,128)S(1)} %get-tuple-element.46), channel_id=1, source_target_pairs={{0,1},{1,2},{2,3},{4,5},{5,6},{6,7},{8,9},{9,10},{10,11},{12,13},{... | collective-permute-start | bytes 12680 | tf_op jit(solution)/shard_map/ppermute | solution.py:29
  27.8 4.8 %collective-permute-start.3 = (f32[11,24,4]{2,1,0:T(8,128)S(1)}, f32[11,24,4]{2,1,0:T(8,128)S(1)}, u32[]{:S(2)}, u32[]{:S(2)}) collective-permute-start(f32[11,24,4]{2,1,0:T(8,128)S(1)} %get-tuple-element.47), channel_id=1, source_target_pairs={{1,0},{2,1},{3,2},{5,4},{6,5},{7,6},{9,8},{10,9},{11,10},{13,12},{... | collective-permute-start | bytes 12680 | tf_op jit(solution)/shard_map/ppermute | solution.py:31
  80.1 1.4 %copy-start.4 = (f32[8,256]{1,0:T(8,128)S(1)}, f32[8,256]{1,0:T(8,128)}, u32[]{:S(2)}) copy-start(f32[8,256]{1,0:T(8,128)} %squeeze_stack_squeeze.36) | copy-start | bytes 24580
  80.1 1.4 %copy-start.6 = (f32[8,256]{1,0:T(8,128)S(1)}, f32[8,256]{1,0:T(8,128)}, u32[]{:S(2)}) copy-start(f32[8,256]{1,0:T(8,128)} %squeeze_stack_squeeze.35) | copy-start | bytes 24580
  80.1 1.4 %copy-start.14 = (pred[16,8]{0,1:T(8,128)(4,1)S(1)}, pred[16,8]{0,1:T(8,128)(4,1)}, u32[]{:S(2)}) copy-start(pred[16,8]{0,1:T(8,128)(4,1)} %copy-done.13) | copy-start | bytes 388
  81.2 1.2 %copy-start.8 = (f32[4,128]{1,0:T(4,128)S(1)}, f32[4,128]{1,0:T(4,128)}, u32[]{:S(2)}) copy-start(f32[4,128]{1,0:T(4,128)} %squeeze_stack_squeeze.40) | copy-start | bytes 6148
  81.2 1.3 %copy-start.26 = (pred[8]{0:T(512)(128)(4,1)S(1)}, pred[8]{0:T(512)(128)(4,1)}, u32[]{:S(2)}) copy-start(pred[8]{0:T(512)(128)(4,1)} %compare_and_fusion.1) | copy-start | bytes 28
  81.2 1.3 %copy-start.27 = (s32[8]{0:T(128)S(1)}, s32[8]{0:T(128)}, u32[]{:S(2)}) copy-start(s32[8]{0:T(128)} %get-tuple-element.173) | copy-start | bytes 100
  81.2 1.3 %copy-start.28 = (s32[8]{0:T(128)S(1)}, s32[8]{0:T(128)}, u32[]{:S(2)}) copy-start(s32[8]{0:T(128)} %get-tuple-element.174) | copy-start | bytes 100
  81.2 1.5 %copy-start.32 = (s32[256]{0:T(256)S(1)}, s32[256]{0:T(256)}, u32[]{:S(2)}) copy-start(s32[256]{0:T(256)} %get-tuple-element.175) | copy-start | bytes 3076
  81.2 1.5 %copy-start.33 = (s32[256]{0:T(256)S(1)}, s32[256]{0:T(256)}, u32[]{:S(2)}) copy-start(s32[256]{0:T(256)} %get-tuple-element.176) | copy-start | bytes 3076
  81.2 1.5 %copy-start.41 = (pred[256]{0:T(512)(128)(4,1)S(1)}, pred[256]{0:T(512)(128)(4,1)}, u32[]{:S(2)}) copy-start(pred[256]{0:T(512)(128)(4,1)} %compare_and_fusion) | copy-start | bytes 772
  81.3 1.8 %copy-start.9 = (f32[1,4,128]{2,1,0:T(4,128)S(1)}, f32[1,4,128]{2,1,0:T(4,128)}, u32[]{:S(2)}) copy-start(f32[1,4,128]{2,1,0:T(4,128)} %squeeze_stack_squeeze.42) | copy-start | bytes 6148
  81.3 1.8 %copy-start.10 = (f32[1,4,128]{2,1,0:T(4,128)S(1)}, f32[1,4,128]{2,1,0:T(4,128)}, u32[]{:S(2)}) copy-start(f32[1,4,128]{2,1,0:T(4,128)} %squeeze_stack_squeeze.44) | copy-start | bytes 6148
  81.3 1.8 %copy-start.11 = (f32[1,4,128]{2,1,0:T(4,128)S(1)}, f32[1,4,128]{2,1,0:T(4,128)}, u32[]{:S(2)}) copy-start(f32[1,4,128]{2,1,0:T(4,128)} %squeeze_stack_squeeze.43) | copy-start | bytes 6148
  87.7 2.0 %copy-start.36 = (pred[20]{0:T(512)(128)(4,1)S(1)}, pred[20]{0:T(512)(128)(4,1)}, u32[]{:S(2)}) copy-start(pred[20]{0:T(512)(128)(4,1)} %compare_and_fusion.6) | copy-start | bytes 64
  87.7 2.0 %copy-start.37 = (s32[20]{0:T(128)S(1)}, s32[20]{0:T(128)}, u32[]{:S(2)}) copy-start(s32[20]{0:T(128)} %get-tuple-element.181) | copy-start | bytes 244
  87.7 2.0 %copy-start.38 = (s32[20]{0:T(128)S(1)}, s32[20]{0:T(128)}, u32[]{:S(2)}) copy-start(s32[20]{0:T(128)} %get-tuple-element.182) | copy-start | bytes 244
  88.1 2.0 %copy-start.2 = (f32[22,518]{1,0:T(8,128)S(1)}, f32[22,518]{1,0:T(8,128)}, u32[]{:S(2)}) copy-start(f32[22,518]{1,0:T(8,128)} %copy-done.1) | copy-start | bytes 136756
  88.1 2.0 %copy-start.15 = (pred[514]{0:T(1024)(128)(4,1)S(1)}, pred[514]{0:T(1024)(128)(4,1)}, u32[]{:S(2)}) copy-start(pred[514]{0:T(1024)(128)(4,1)} %get-tuple-element.183) | copy-start | bytes 1546
  88.1 2.0 %copy-start.16 = (pred[514]{0:T(1024)(128)(4,1)S(1)}, pred[514]{0:T(1024)(128)(4,1)}, u32[]{:S(2)}) copy-start(pred[514]{0:T(1024)(128)(4,1)} %get-tuple-element.184) | copy-start | bytes 1546
  88.1 2.0 %copy-start.21 = (pred[18]{0:T(512)(128)(4,1)S(1)}, pred[18]{0:T(512)(128)(4,1)}, u32[]{:S(2)}) copy-start(pred[18]{0:T(512)(128)(4,1)} %compare_and_fusion.9) | copy-start | bytes 58
  (16 other events, 12.7 us)
Sparse Core Ops, SparseCore 0:
  11.2 41.9 all-gather.3

commit v12 on v10

--- a/solution.py
+++ b/solution.py
@@ -73,8 +73,21 @@
 
 def prolong(coarse):
     height, width = coarse.shape[-2] * 2, coarse.shape[-1] * 2
-    wider = jnp.einsum("...hv,wv->...hw", coarse, pairs(width), precision=HIGH)
-    return jnp.einsum("...vw,hv->...hw", wider, pairs(height), precision=HIGH)
+    wider = copy_dot("...hv,wv->...hw", coarse, pairs(width))
+    return copy_dot("...vw,hv->...hw", wider, pairs(height))
+
+
+def copy_dot(spec, x, picks):
+    high = lax.reduce_precision(x, exponent_bits=8, mantissa_bits=7)
+    rest = x - high
+    middle = lax.reduce_precision(rest, exponent_bits=8, mantissa_bits=7)
+    low = rest - middle
+    picks = picks.astype(jnp.bfloat16)
+    part = [
+        jnp.einsum(spec, p.astype(jnp.bfloat16), picks, preferred_element_type=jnp.float32)
+        for p in (high, middle, low)
+    ]
+    return (part[0] + part[1]) + part[2]
 
 
 def apply_planes(iterate, padded, noise, couplings):

time: 79.2 us -> 88.3 us (1.11)
  matrix products: 8.54 us -> 11.4 us
  local copies, waits for them, and re-layouts: 4.41 us -> 7.14 us
  blocking collectives: 23.5 us -> 25.5 us
  waiting for transfers between devices: 8.47 us -> 9.69 us
    all_gather x1, waiting for transfers between devices: 0.02 us -> 5.46 us  [gather_grids(): stacked = lax.all_gather(packed, GRID, axis=1, tiled=False)]
    ppermute x2, waiting for transfers between devices: 7.94 us -> 4.21 us  [with_halo(): lax.ppermute(head, axis, [(i + 1, i) for i in range(ends)])]
    dot_general x8 -> x24, matrix products: 3.51 us -> 6.55 us  [copy_dot(): jnp.einsum(spec, p.astype(jnp.bfloat16), picks, preferred_element_type=jn...]
    all_gather x1, blocking collectives: 23.5 us -> 25.5 us  [gather_grids(): stacked = lax.all_gather(packed, GRID, axis=1, tiled=False)]
    unnamed x10 -> x8, local copies, waits for them, and re-layouts: 0.05 us -> 1.89 us
  transfers between devices with their start and end apart: 5 -> 5, of which waited for: 3 -> 3; matrix products, arithmetic and copies ran while one was open for 4% -> 8% of each run, Pallas kernels for 0% -> 0%
where the time goes in v12:
time: 88.3 us; the launch traced here: 87.9 us
  blocking collectives  25.5 us (29%)
  between operations  14.4 us (16%)
  matrix products  11.4 us (13%)
  other arithmetic  10.9 us (12%)
  waiting for transfers between devices  9.69 us (11%)
  starting transfers between devices  8.82 us (10%)
  local copies, waits for them, and re-layouts  7.14 us (8%)
    all_gather x1, blocking collectives, gather_grids(): stacked = lax.all_gather(packed, GRID, axis=1, tiled=False)  25.5 us
    dot_general x24, matrix products, copy_dot(): jnp.einsum(spec, p.astype(jnp.bfloat16), picks, preferred_element_type=jn...  6.55 us
    ppermute x2, starting transfers between devices, with_halo(): lax.ppermute(tail, axis, [(i, i + 1) for i in range(ends)])  6.23 us
    all_gather x1, waiting for transfers between devices, gather_grids(): stacked = lax.all_gather(packed, GRID, axis=1, tiled=False)  5.46 us
    ppermute x2, waiting for transfers between devices, with_halo(): lax.ppermute(head, axis, [(i + 1, i) for i in range(ends)])  4.21 us
    ppermute x2, starting transfers between devices, with_halo(): lax.ppermute(head, axis, [(i + 1, i) for i in range(ends)])  2.58 us
    select_n x6, other arithmetic, sweep_ext(): return [jnp.where(mask, n, 0.0) for n in new]  1.98 us
    dot_general x4, matrix products, sum_cols(): return jnp.einsum('...hw,wv->...hv', x, m, precision=HIGH)  1.95 us
  transfers between devices with their start and end apart: 5, of which 3 were waited for; matrix products, arithmetic and copies ran while one was open for 8% of the time, Pallas kernels for 0%

profile of v12, /device:TPU:0, one launch (start us, length us, event | category | flops | bytes accessed | tf_op | source)
XLA Modules:
  0.0 87.9 jit_solution(4949246692721155950)
XLA Ops:
  6.5 0.9 %constant_dynamic-update-slice_fusion.2 = f32[11,16,512]{2,1,0:T(8,128)S(1)} fusion(f32[3,16,512]{2,1,0:T(8,128)} %param.3), kind=kLoop, calls=%fused_computation.1195 | loop fusion | bytes 196608
  7.5 0.9 %constant_dynamic-update-slice_fusion.1 = f32[11,16,512]{2,1,0:T(8,128)S(1)} fusion(f32[11,16,512]{2,1,0:T(8,128)S(1)} %constant_dynamic-update-slice_fusion.2, f32[6,16,512]{2,1,0:T(8,128)} %param.4), kind=kLoop, calls=%fused_computation.1194 | loop fusion | bytes 393216
  8.4 0.9 %constant_dynamic-update-slice_fusion = f32[11,16,512]{2,1,0:T(8,128)S(1)} fusion(f32[11,16,512]{2,1,0:T(8,128)S(1)} %constant_dynamic-update-slice_fusion.1, f32[2,16,512]{2,1,0:T(8,128)} %param.5), kind=kLoop, calls=%fused_computation.1193 | loop fusion | bytes 131072 | tf_op jit(solution)/shard_map/concatenate | solution.py:327
  9.4 4.9 %collective-permute-start = (f32[11,4,512]{2,1,0:T(4,128)S(1)}, f32[11,4,512]{2,1,0:T(4,128)S(1)}, u32[]{:S(2)}, u32[]{:S(2)}) collective-permute-start(f32[11,4,512]{2,1,0:T(4,128)S(1)} %get-tuple-element.96), channel_id=1, source_target_pairs={{0,4},{4,8},{8,12},{1,5},{5,9},{9,13},{2,6},{6,10},{10,14},{3,7},{... | collective-permute-start | bytes 270344 | tf_op jit(solution)/shard_map/ppermute | solution.py:29
  14.3 1.3 %collective-permute-start.1 = (f32[11,4,512]{2,1,0:T(4,128)S(1)}, f32[11,4,512]{2,1,0:T(4,128)S(1)}, u32[]{:S(2)}, u32[]{:S(2)}) collective-permute-start(f32[11,4,512]{2,1,0:T(4,128)S(1)} %get-tuple-element.97), channel_id=1, source_target_pairs={{4,0},{8,4},{12,8},{5,1},{9,5},{13,9},{6,2},{10,6},{14,10},{7,3},{... | collective-permute-start | bytes 270344 | tf_op jit(solution)/shard_map/ppermute | solution.py:31
  16.1 0.4 fusion.24
  17.7 1.1 %fusion.25 = f32[7,15,480]{2,1,0:T(8,128)S(1)} fusion(f32[512,32]{0,1:T(8,128)S(1)} %fusion.277, f32[512,64]{0,1:T(8,128)S(1)} %fusion.222, f32[512,128]{0,1:T(8,128)S(1)} %fusion.65, f32[512,256]{0,1:T(8,128)S(1)} %fusion.32, f32[1,15,512]{2,1,0:T(8,128)S(1)} %convolution_bitcast_fusion.4, f32[6,15,512]{2,1,0:T(8,128)S(1)} %convolution_bitcast_fusion), kind=kOutput, calls=%fused_computation.48 | convolution fusion | flops 310448640 | bytes 1399680 | tf_op jit(solution)/shard_map/pvw,wu->pvu/dot_general | solution.py:276
  19.1 0.6 pad_maximum_fusion.6
  20.1 0.6 collective-permute-done.1
  20.8 1.3 %collective-permute-start.2 = (f32[11,24,4]{2,1,0:T(8,128)S(1)}, f32[11,24,4]{2,1,0:T(8,128)S(1)}, u32[]{:S(2)}, u32[]{:S(2)}) collective-permute-start(f32[11,24,4]{2,1,0:T(8,128)S(1)} %get-tuple-element.88), channel_id=1, source_target_pairs={{0,1},{1,2},{2,3},{4,5},{5,6},{6,7},{8,9},{9,10},{10,11},{12,13},{... | collective-permute-start | bytes 12680 | tf_op jit(solution)/shard_map/ppermute | solution.py:29
  22.2 1.3 %collective-permute-start.3 = (f32[11,24,4]{2,1,0:T(8,128)S(1)}, f32[11,24,4]{2,1,0:T(8,128)S(1)}, u32[]{:S(2)}, u32[]{:S(2)}) collective-permute-start(f32[11,24,4]{2,1,0:T(8,128)S(1)} %get-tuple-element.89), channel_id=1, source_target_pairs={{1,0},{2,1},{3,2},{5,4},{6,5},{7,6},{9,8},{10,9},{11,10},{13,12},{... | collective-permute-start | bytes 12680 | tf_op jit(solution)/shard_map/ppermute | solution.py:31
  23.5 3.6 %collective-permute-done.3 = f32[11,24,4]{2,1,0:T(8,128)S(1)} collective-permute-done((f32[11,24,4]{2,1,0:T(8,128)S(1)}, f32[11,24,4]{2,1,0:T(8,128)S(1)}, u32[]{:S(2)}, u32[]{:S(2)}) %collective-permute-start.3) | collective-permute-done | bytes 4256 | tf_op jit(solution)/shard_map/ppermute | solution.py:31
  27.1 0.4 pad_maximum_fusion
  27.9 0.3 fusion.316
  28.2 0.3 fusion.326
  28.6 0.3 fusion.337
  29.7 0.3 fusion.55
  30.1 25.5 %all-gather = f32[16,48,128]{2,0,1:T(8,128)S(1)} all-gather(f32[16,3,128]{2,0,1:T(8,128)S(1)} %bitcast.898), channel_id=2, replica_groups=mesh['groups'=2,'tiles'=4,'band'=2,'stokes'=2] {'tiles','band','stokes'}, dimensions={1}, use_global_device_ids=true | all-gather | bytes 417792 | tf_op jit(solution)/shard_map/all_gather | solution.py:170
  55.7 5.5 %all-gather.4.cloned.1.call-done = f32[22,128,128]{2,1,0:T(8,128)} async-done(((f32[22,8,128]{2,1,0:T(8,128)}), f32[22,128,128]{2,1,0:T(8,128)}) %all-gather.4.cloned.1.call-update) | async-done | bytes 1441808 | tf_op jit(solution)/shard_map/all_gather | solution.py:170
  61.1 0.9 %slice_bitcast_fusion.3 = (f32[8,16,1,128]{3,0,1,2:T(8,128)S(1)}, f32[8,16,1,128]{3,0,1,2:T(8,128)S(1)}) fusion(f32[22,128,128]{2,1,0:T(8,128)} %all-gather.4.cloned.1.call-done), kind=kLoop, calls=%fused_computation.427 | loop fusion | bytes 262144 | tf_op jit(solution)/shard_map/transpose | solution.py:181
  63.6 0.5 slice-done
  64.1 0.6 copy.192
  65.4 0.4 fusion.118
  65.8 0.3 fusion.128
  66.4 1.0 %fusion.1 = f32[3,16,512]{2,1,0:T(8,128)S(1)} fusion(f32[3,16,1024]{2,1,0:T(8,128)S(1)} %convolution_bitcast_fusion.1, s32[1024]{0:T(1024)S(1)} %get-tuple-element.166, s32[1024]{0:T(1024)S(1)} %get-tuple-element.167, pred[1024]{0:T(1024)(128)(4,1)S(1)} %fusion.790), kind=kOutput, calls=%fused_computation.3 | convolution fusion | flops 303038464 | bytes 304128 | tf_op jit(solution)/shard_map/...hw,wv->...hv/dot_general | solution.py:59
  68.1 0.3 fusion.53
  73.4 0.7 fusion.10
  74.1 0.7 convolution_add_fusion.3
  74.8 0.7 convolution_add_fusion.2
  76.5 0.5 fusion.225
  78.8 0.3 fusion.291
  80.4 0.6 pad_maximum_fusion.5
  (194 shorter events, 15.3 us)
Async XLA Ops:
  6.5 9.6 %copy-start.1 = (f32[2,16,512]{2,1,0:T(8,128)S(1)}, f32[2,16,512]{2,1,0:T(8,128)}, u32[]{:S(2)}) copy-start(f32[2,16,512]{2,1,0:T(8,128)} %param.5) | copy-start | bytes 196612
  6.5 54.6 %all-gather.4.cloned.1.call-start = ((), (), s32[]{:S(2)}) async-start(), calls=%async_computation | async-start | bytes 1531904 | tf_op jit(solution)/shard_map/all_gather | solution.py:170
  8.4 8.4 %copy-start = (f32[6,16,512]{2,1,0:T(8,128)S(1)}, f32[6,16,512]{2,1,0:T(8,128)}, u32[]{:S(2)}) copy-start(f32[6,16,512]{2,1,0:T(8,128)} %param.4) | copy-start | bytes 589828
  9.4 10.8 %collective-permute-start = (f32[11,4,512]{2,1,0:T(4,128)S(1)}, f32[11,4,512]{2,1,0:T(4,128)S(1)}, u32[]{:S(2)}, u32[]{:S(2)}) collective-permute-start(f32[11,4,512]{2,1,0:T(4,128)S(1)} %get-tuple-element.96), channel_id=1, source_target_pairs={{0,4},{4,8},{8,12},{1,5},{5,9},{9,13},{2,6},{6,10},{10,14},{3,7},{... | collective-permute-start | bytes 270344 | tf_op jit(solution)/shard_map/ppermute | solution.py:29
  14.3 6.4 %collective-permute-start.1 = (f32[11,4,512]{2,1,0:T(4,128)S(1)}, f32[11,4,512]{2,1,0:T(4,128)S(1)}, u32[]{:S(2)}, u32[]{:S(2)}) collective-permute-start(f32[11,4,512]{2,1,0:T(4,128)S(1)} %get-tuple-element.97), channel_id=1, source_target_pairs={{4,0},{8,4},{12,8},{5,1},{9,5},{13,9},{6,2},{10,6},{14,10},{7,3},{... | collective-permute-start | bytes 270344 | tf_op jit(solution)/shard_map/ppermute | solution.py:31
  20.8 2.6 %collective-permute-start.2 = (f32[11,24,4]{2,1,0:T(8,128)S(1)}, f32[11,24,4]{2,1,0:T(8,128)S(1)}, u32[]{:S(2)}, u32[]{:S(2)}) collective-permute-start(f32[11,24,4]{2,1,0:T(8,128)S(1)} %get-tuple-element.88), channel_id=1, source_target_pairs={{0,1},{1,2},{2,3},{4,5},{5,6},{6,7},{8,9},{9,10},{10,11},{12,13},{... | collective-permute-start | bytes 12680 | tf_op jit(solution)/shard_map/ppermute | solution.py:29
  22.2 5.0 %collective-permute-start.3 = (f32[11,24,4]{2,1,0:T(8,128)S(1)}, f32[11,24,4]{2,1,0:T(8,128)S(1)}, u32[]{:S(2)}, u32[]{:S(2)}) collective-permute-start(f32[11,24,4]{2,1,0:T(8,128)S(1)} %get-tuple-element.89), channel_id=1, source_target_pairs={{1,0},{2,1},{3,2},{5,4},{6,5},{7,6},{9,8},{10,9},{11,10},{13,12},{... | collective-permute-start | bytes 12680 | tf_op jit(solution)/shard_map/ppermute | solution.py:31
  62.9 1.2 %slice-start = ((f32[22,128,128]{2,1,0:T(8,128)}), f32[16,128,128]{2,1,0:T(8,128)S(1)}, s32[]{:S(2)}) async-start(f32[22,128,128]{2,1,0:T(8,128)} %all-gather.4.cloned.1.call-done), calls=%async_computation.1 | async-start | bytes 2097152 | tf_op jit(solution)/shard_map/slice | solution.py:175
  63.6 1.1 %slice-start.1 = ((f32[22,128,128]{2,1,0:T(8,128)}), f32[4,128,128]{2,1,0:T(8,128)S(1)}, s32[]{:S(2)}) async-start(f32[22,128,128]{2,1,0:T(8,128)} %all-gather.4.cloned.1.call-done), calls=%async_computation.2 | async-start | bytes 524288 | tf_op jit(solution)/shard_map/slice | solution.py:175
Sparse Core Ops, SparseCore 0:
  19.9 41.1 all-gather.3

commit v13 on v10

--- a/solution.py
+++ b/solution.py
@@ -19,20 +19,42 @@
 
 
 def with_halo(cells, width):
-    for axis, dim in ((ROWS, 1), (COLS, 2)):
+    count_rows = lax.axis_size(ROWS)
+    count_cols = lax.axis_size(COLS)
+    height, breadth = cells.shape[1], cells.shape[2]
+    top, bottom = cells[:, :width, :], cells[:, height - width:, :]
+    left, right = cells[:, :, :width], cells[:, :, breadth - width:]
+
+    def shift(block, axis, step):
         count = lax.axis_size(axis)
-        ends = count - 1
-        head = lax.slice_in_dim(cells, 0, width, axis=dim)
-        tail = lax.slice_in_dim(cells, cells.shape[dim] - width, cells.shape[dim], axis=dim)
-        cells = jnp.concatenate(
-            [
-                lax.ppermute(tail, axis, [(i, i + 1) for i in range(ends)]),
-                cells,
-                lax.ppermute(head, axis, [(i + 1, i) for i in range(ends)]),
-            ],
-            axis=dim,
-        )
-    return cells
+        return lax.ppermute(
+            block, axis, [(i, i + step) for i in range(count) if 0 <= i + step < count]
+        )
+
+    def diagonal(block, down, across):
+        pairs_ = []
+        for t in range(count_rows):
+            for c in range(count_cols):
+                if 0 <= t + down < count_rows and 0 <= c + across < count_cols:
+                    pairs_.append((t * count_cols + c, (t + down) * count_cols + c + across))
+        return lax.ppermute(block, GRID, pairs_)
+
+    north = shift(bottom, ROWS, 1)
+    south = shift(top, ROWS, -1)
+    west = shift(right, COLS, 1)
+    east = shift(left, COLS, -1)
+    north_west = diagonal(bottom[:, :, breadth - width:], 1, 1)
+    north_east = diagonal(bottom[:, :, :width], 1, -1)
+    south_west = diagonal(top[:, :, breadth - width:], -1, 1)
+    south_east = diagonal(top[:, :, :width], -1, -1)
+    return jnp.concatenate(
+        [
+            jnp.concatenate([north_west, north, north_east], axis=2),
+            jnp.concatenate([west, cells, east], axis=2),
+            jnp.concatenate([south_west, south, south_east], axis=2),
+        ],
+        axis=1,
+    )
 
 
 def crop(x, k):

time: 79.2 us -> 90 us (1.14)
  starting transfers between devices: 8.82 us -> 21.4 us
  waiting for transfers between devices: 8.47 us -> 5.13 us
  blocking collectives: 23.5 us -> 24.6 us
    ppermute x4 -> x8, starting transfers between devices: 8.82 us -> 21.4 us  [the longest x4 14.4 us: shift(): lax.ppermute(block, axis, [(i, i + step) for i in range(count) if 0 <= i...]
    ppermute x4 -> x8, waiting for transfers between devices: 8.43 us -> 5.09 us  [the longest x4 5.08 us: shift(): lax.ppermute(block, axis, [(i, i + step) for i in range(count) if 0 <= i...]
    all_gather x1, blocking collectives: 23.5 us -> 24.6 us  [gather_grids(): stacked = lax.all_gather(packed, GRID, axis=1, tiled=False)]
  transfers between devices with their start and end apart: 5 -> 9, of which waited for: 3 -> 2; matrix products, arithmetic and copies ran while one was open for 4% -> 4% of each run, Pallas kernels for 0% -> 0%
where the time goes in v13:
time: 90 us; the launch traced here: 89.6 us
  blocking collectives  24.6 us (27%)
  starting transfers between devices  21.4 us (24%)
  between operations  14.5 us (16%)
  other arithmetic  10.8 us (12%)
  matrix products  8.55 us (10%)
  waiting for transfers between devices  5.13 us (6%)
  local copies, waits for them, and re-layouts  4.6 us (5%)
    all_gather x1, blocking collectives, gather_grids(): stacked = lax.all_gather(packed, GRID, axis=1, tiled=False)  24.6 us
    ppermute x4, starting transfers between devices, shift(): lax.ppermute(block, axis, [(i, i + step) for i in range(count) if 0 <= i...  14.4 us
    ppermute x4, starting transfers between devices, diagonal(): return lax.ppermute(block, GRID, pairs_)  6.99 us
    ppermute x4, waiting for transfers between devices, shift(): lax.ppermute(block, axis, [(i, i + step) for i in range(count) if 0 <= i...  5.08 us
    dot_general x4, matrix products, prolong(): wider = jnp.einsum('...hv,wv->...hw', coarse, pairs(width), precision=HIGH)  2.39 us
    select_n x6, other arithmetic, sweep_ext(): return [jnp.where(mask, n, 0.0) for n in new]  1.98 us
    dot_general x4, matrix products, sum_cols(): return jnp.einsum('...hw,wv->...hv', x, m, precision=HIGH)  1.95 us
  transfers between devices with their start and end apart: 9, of which 2 were waited for; matrix products, arithmetic and copies ran while one was open for 4% of the time, Pallas kernels for 0%

profile of v13, /device:TPU:0, one launch (start us, length us, event | category | flops | bytes accessed | tf_op | source)
XLA Modules:
  0.0 89.6 jit_solution(17500093401495027645)
XLA Ops:
  7.1 1.2 %fusion.11 = f32[480,16]{0,1:T(8,128)S(1)} fusion(pred[512,32]{1,0:T(32,128)(4,1)S(1)} %iota_compare_fusion.6, pred[512,64]{1,0:T(32,128)(4,1)S(1)} %iota_compare_fusion.7, pred[512,128]{1,0:T(32,128)(4,1)S(1)} %iota_compare_fusion.8, pred[512,256]{1,0:T(32,128)(4,1)S(1)} %iota_compare_fusion.4, f32[2,16,512]{2,1,0:T(8,128)} %param.5), kind=kOutput, calls=%fused_computation.22 | convolution fusion | flops 47923200 | bytes 309248 | tf_op jit(solution)/shard_map/hw,wu->hu/dot_general | solution.py:287
  9.4 0.6 fusion.12
  10.3 0.6 pad_maximum_fusion.1
  11.2 4.4 %collective-permute-start = (f32[11,4,4]{2,1,0:T(4,128)S(1)}, f32[11,4,4]{2,1,0:T(4,128)S(1)}, u32[]{:S(2)}, u32[]{:S(2)}) collective-permute-start(f32[11,4,4]{2,1,0:T(4,128)S(1)} %get-tuple-element.94), channel_id=1, source_target_pairs={{0,5},{1,6},{2,7},{4,9},{5,10},{6,11},{8,13},{9,14},{10,15},{16,21... | collective-permute-start | bytes 2120 | tf_op jit(solution)/shard_map/ppermute | solution.py:40
  15.5 1.3 %collective-permute-start.7 = (f32[11,4,4]{2,1,0:T(4,128)S(1)}, f32[11,4,4]{2,1,0:T(4,128)S(1)}, u32[]{:S(2)}, u32[]{:S(2)}) collective-permute-start(f32[11,4,4]{2,1,0:T(4,128)S(1)} %get-tuple-element.95), channel_id=1, source_target_pairs={{5,0},{6,1},{7,2},{9,4},{10,5},{11,6},{13,8},{14,9},{15,10},{21,16... | collective-permute-start | bytes 2120 | tf_op jit(solution)/shard_map/ppermute | solution.py:40
  16.8 0.7 collective-permute-start.5
  17.5 0.7 collective-permute-start.2
  18.3 7.7 %collective-permute-start.3 = (f32[11,16,4]{2,1,0:T(8,128)S(1)}, f32[11,16,4]{2,1,0:T(8,128)S(1)}, u32[]{:S(2)}, u32[]{:S(2)}) collective-permute-start(f32[11,16,4]{2,1,0:T(8,128)S(1)} %get-tuple-element.100), channel_id=1, source_target_pairs={{0,1},{1,2},{2,3},{4,5},{5,6},{6,7},{8,9},{9,10},{10,11},{12,13},{... | collective-permute-start | bytes 8456 | tf_op jit(solution)/shard_map/ppermute | solution.py:30
  26.4 1.3 %collective-permute-start.4 = (f32[11,16,4]{2,1,0:T(8,128)S(1)}, f32[11,16,4]{2,1,0:T(8,128)S(1)}, u32[]{:S(2)}, u32[]{:S(2)}) collective-permute-start(f32[11,16,4]{2,1,0:T(8,128)S(1)} %get-tuple-element.101), channel_id=1, source_target_pairs={{1,0},{2,1},{3,2},{5,4},{6,5},{7,6},{9,8},{10,9},{11,10},{13,12},{... | collective-permute-start | bytes 8456 | tf_op jit(solution)/shard_map/ppermute | solution.py:30
  27.7 4.1 %collective-permute-start.1 = (f32[11,4,512]{2,1,0:T(4,128)S(1)}, f32[11,4,512]{2,1,0:T(4,128)S(1)}, u32[]{:S(2)}, u32[]{:S(2)}) collective-permute-start(f32[11,4,512]{2,1,0:T(4,128)S(1)} %get-tuple-element.98), channel_id=1, source_target_pairs={{0,4},{4,8},{8,12},{1,5},{5,9},{9,13},{2,6},{6,10},{10,14},{3,7},{... | collective-permute-start | bytes 270344 | tf_op jit(solution)/shard_map/ppermute | solution.py:30
  31.9 1.3 %collective-permute-start.6 = (f32[11,4,512]{2,1,0:T(4,128)S(1)}, f32[11,4,512]{2,1,0:T(4,128)S(1)}, u32[]{:S(2)}, u32[]{:S(2)}) collective-permute-start(f32[11,4,512]{2,1,0:T(4,128)S(1)} %get-tuple-element.99), channel_id=1, source_target_pairs={{4,0},{8,4},{12,8},{5,1},{9,5},{13,9},{6,2},{10,6},{14,10},{7,3},{... | collective-permute-start | bytes 270344 | tf_op jit(solution)/shard_map/ppermute | solution.py:30
  33.2 0.8 collective-permute-done.1
  34.0 4.3 %collective-permute-done.6 = f32[11,4,512]{2,1,0:T(4,128)S(1)} collective-permute-done((f32[11,4,512]{2,1,0:T(4,128)S(1)}, f32[11,4,512]{2,1,0:T(4,128)S(1)}, u32[]{:S(2)}, u32[]{:S(2)}) %collective-permute-start.6) | collective-permute-done | bytes 90144 | tf_op jit(solution)/shard_map/ppermute | solution.py:30
  38.3 0.4 maximum_maximum_fusion
  39.1 0.3 fusion.276
  39.4 0.3 fusion.286
  39.8 0.3 fusion.297
  40.9 0.3 fusion.26
  41.2 24.6 %all-gather = f32[16,48,128]{2,0,1:T(8,128)S(1)} all-gather(f32[16,3,128]{2,0,1:T(8,128)S(1)} %bitcast.873), channel_id=2, replica_groups=mesh['groups'=2,'tiles'=4,'band'=2,'stokes'=2] {'tiles','band','stokes'}, dimensions={1}, use_global_device_ids=true | all-gather | bytes 417792 | tf_op jit(solution)/shard_map/all_gather | solution.py:179
  66.0 0.9 slice_bitcast_fusion.3
  68.5 0.5 slice-done
  69.0 0.6 copy.178
  70.2 0.5 fusion.81
  70.7 0.3 fusion.91
  71.3 1.0 %fusion.3 = f32[3,16,512]{2,1,0:T(8,128)S(1)} fusion(f32[3,16,1024]{2,1,0:T(8,128)S(1)} %convolution_bitcast_fusion.2, s32[1024]{0:T(1024)S(1)} %get-tuple-element.170, s32[1024]{0:T(1024)S(1)} %get-tuple-element.171, pred[1024]{0:T(1024)(128)(4,1)S(1)} %fusion.739), kind=kOutput, calls=%fused_computation.4 | convolution fusion | flops 303038464 | bytes 304128 | tf_op jit(solution)/shard_map/...hw,wv->...hv/dot_general | solution.py:81
  72.9 0.3 fusion.24
  76.8 1.3 %fusion.1 = f32[3,16,1024]{2,1,0:T(8,128)S(1)} fusion(s32[1024]{0:T(1024)S(1)} %get-tuple-element.170, s32[1024]{0:T(1024)S(1)} %get-tuple-element.171, pred[1024]{0:T(1024)(128)(4,1)S(1)} %fusion.739, f32[1,16,512]{2,1,0:T(8,128)S(1)} %get-tuple-element.103, f32[1,16,512]{2,1,0:T(8,128)S(1)} %get-tuple-element.102, f32[1,16,512]{2,1,0:T(8,128)S(1)} %get-tuple-element.8), kind=kOutput, calls=%fused_computation.3 | convolution fusion | flops 303087616 | bytes 304128 | tf_op jit(solution)/shard_map/...hv,wv->...hw/dot_general | solution.py:98
  78.1 0.4 convolution_bitcast_fusion
  78.8 0.5 fusion.185
  79.3 0.3 fusion.186
  79.6 0.5 fusion.20
  82.1 0.6 pad_maximum_fusion
  (188 shorter events, 12.1 us)
Async XLA Ops:
  6.5 2.1 %copy-start = (f32[6,16,512]{2,1,0:T(8,128)S(1)}, f32[6,16,512]{2,1,0:T(8,128)}, u32[]{:S(2)}) copy-start(f32[6,16,512]{2,1,0:T(8,128)} %param.4) | copy-start | bytes 589828
  6.5 59.4 %all-gather.4.cloned.1.call-start = ((), (), s32[]{:S(2)}) async-start(), calls=%async_computation | async-start | bytes 1531904 | tf_op jit(solution)/shard_map/all_gather | solution.py:179
  6.8 2.3 %copy-start.1 = (f32[2,16,512]{2,1,0:T(8,128)S(1)}, f32[2,16,512]{2,1,0:T(8,128)}, u32[]{:S(2)}) copy-start(f32[2,16,512]{2,1,0:T(8,128)} %param.5) | copy-start | bytes 196612
  9.4 1.6 %copy-start.2 = (f32[3,16,512]{2,1,0:T(8,128)S(1)}, f32[3,16,512]{2,1,0:T(8,128)}, u32[]{:S(2)}) copy-start(f32[3,16,512]{2,1,0:T(8,128)} %param.3) | copy-start | bytes 294916
  11.2 15.2 %collective-permute-start = (f32[11,4,4]{2,1,0:T(4,128)S(1)}, f32[11,4,4]{2,1,0:T(4,128)S(1)}, u32[]{:S(2)}, u32[]{:S(2)}) collective-permute-start(f32[11,4,4]{2,1,0:T(4,128)S(1)} %get-tuple-element.94), channel_id=1, source_target_pairs={{0,5},{1,6},{2,7},{4,9},{5,10},{6,11},{8,13},{9,14},{10,15},{16,21... | collective-permute-start | bytes 2120 | tf_op jit(solution)/shard_map/ppermute | solution.py:40
  15.5 12.2 %collective-permute-start.7 = (f32[11,4,4]{2,1,0:T(4,128)S(1)}, f32[11,4,4]{2,1,0:T(4,128)S(1)}, u32[]{:S(2)}, u32[]{:S(2)}) collective-permute-start(f32[11,4,4]{2,1,0:T(4,128)S(1)} %get-tuple-element.95), channel_id=1, source_target_pairs={{5,0},{6,1},{7,2},{9,4},{10,5},{11,6},{13,8},{14,9},{15,10},{21,16... | collective-permute-start | bytes 2120 | tf_op jit(solution)/shard_map/ppermute | solution.py:40
  16.8 15.0 %collective-permute-start.5 = (f32[11,4,4]{2,1,0:T(4,128)S(1)}, f32[11,4,4]{2,1,0:T(4,128)S(1)}, u32[]{:S(2)}, u32[]{:S(2)}) collective-permute-start(f32[11,4,4]{2,1,0:T(4,128)S(1)} %get-tuple-element.96), channel_id=1, source_target_pairs={{4,1},{5,2},{6,3},{8,5},{9,6},{10,7},{12,9},{13,10},{14,11},{20,17... | collective-permute-start | bytes 2120 | tf_op jit(solution)/shard_map/ppermute | solution.py:40
  17.5 15.7 %collective-permute-start.2 = (f32[11,4,4]{2,1,0:T(4,128)S(1)}, f32[11,4,4]{2,1,0:T(4,128)S(1)}, u32[]{:S(2)}, u32[]{:S(2)}) collective-permute-start(f32[11,4,4]{2,1,0:T(4,128)S(1)} %get-tuple-element.97), channel_id=1, source_target_pairs={{1,4},{2,5},{3,6},{5,8},{6,9},{7,10},{9,12},{10,13},{11,14},{17,20... | collective-permute-start | bytes 2120 | tf_op jit(solution)/shard_map/ppermute | solution.py:40
  18.3 14.9 %collective-permute-start.3 = (f32[11,16,4]{2,1,0:T(8,128)S(1)}, f32[11,16,4]{2,1,0:T(8,128)S(1)}, u32[]{:S(2)}, u32[]{:S(2)}) collective-permute-start(f32[11,16,4]{2,1,0:T(8,128)S(1)} %get-tuple-element.100), channel_id=1, source_target_pairs={{0,1},{1,2},{2,3},{4,5},{5,6},{6,7},{8,9},{9,10},{10,11},{12,13},{... | collective-permute-start | bytes 8456 | tf_op jit(solution)/shard_map/ppermute | solution.py:30
  26.4 6.8 %collective-permute-start.4 = (f32[11,16,4]{2,1,0:T(8,128)S(1)}, f32[11,16,4]{2,1,0:T(8,128)S(1)}, u32[]{:S(2)}, u32[]{:S(2)}) collective-permute-start(f32[11,16,4]{2,1,0:T(8,128)S(1)} %get-tuple-element.101), channel_id=1, source_target_pairs={{1,0},{2,1},{3,2},{5,4},{6,5},{7,6},{9,8},{10,9},{11,10},{13,12},{... | collective-permute-start | bytes 8456 | tf_op jit(solution)/shard_map/ppermute | solution.py:30
  27.7 6.2 %collective-permute-start.1 = (f32[11,4,512]{2,1,0:T(4,128)S(1)}, f32[11,4,512]{2,1,0:T(4,128)S(1)}, u32[]{:S(2)}, u32[]{:S(2)}) collective-permute-start(f32[11,4,512]{2,1,0:T(4,128)S(1)} %get-tuple-element.98), channel_id=1, source_target_pairs={{0,4},{4,8},{8,12},{1,5},{5,9},{9,13},{2,6},{6,10},{10,14},{3,7},{... | collective-permute-start | bytes 270344 | tf_op jit(solution)/shard_map/ppermute | solution.py:30
  31.9 6.4 %collective-permute-start.6 = (f32[11,4,512]{2,1,0:T(4,128)S(1)}, f32[11,4,512]{2,1,0:T(4,128)S(1)}, u32[]{:S(2)}, u32[]{:S(2)}) collective-permute-start(f32[11,4,512]{2,1,0:T(4,128)S(1)} %get-tuple-element.99), channel_id=1, source_target_pairs={{4,0},{8,4},{12,8},{5,1},{9,5},{13,9},{6,2},{10,6},{14,10},{7,3},{... | collective-permute-start | bytes 270344 | tf_op jit(solution)/shard_map/ppermute | solution.py:30
  67.7 1.2 %slice-start = ((f32[22,128,128]{2,1,0:T(8,128)}), f32[16,128,128]{2,1,0:T(8,128)S(1)}, s32[]{:S(2)}) async-start(f32[22,128,128]{2,1,0:T(8,128)} %all-gather.4.cloned.1.call-done), calls=%async_computation.1 | async-start | bytes 2097152 | tf_op jit(solution)/shard_map/slice | solution.py:184
  68.5 1.1 %slice-start.1 = ((f32[22,128,128]{2,1,0:T(8,128)}), f32[4,128,128]{2,1,0:T(8,128)S(1)}, s32[]{:S(2)}) async-start(f32[22,128,128]{2,1,0:T(8,128)} %all-gather.4.cloned.1.call-done), calls=%async_computation.2 | async-start | bytes 524288 | tf_op jit(solution)/shard_map/slice | solution.py:184
Sparse Core Ops, SparseCore 0:
  11.1 41.3 all-gather.3

commit v14 on v10

--- a/solution.py
+++ b/solution.py
@@ -163,7 +163,15 @@
         first += t.shape[0]
         if width % 128 == 0:
             part = part.reshape(height, width // 128, count_rows, count_cols, planes, 128)
-            whole = part.transpose(4, 2, 0, 3, 1, 5)
+            grids.append(
+                [
+                    part[:, :, :, :, k, :]
+                    .transpose(2, 0, 3, 1, 4)
+                    .reshape(count_rows * height, count_cols * width)
+                    for k in range(planes)
+                ]
+            )
+            continue
         else:
             part = part.transpose(2, 1, 0, 3).reshape(planes, count_rows, count_cols, -1)
             part = part[..., : height * width].reshape(planes, count_rows, count_cols, height, width)

time: 79.2 us -> 81 us (1.023)
  local copies, waits for them, and re-layouts: 4.41 us -> 6.14 us
    slice x0 -> x3, local copies, waits for them, and re-layouts: none -> 1.25 us  [gather_grids(): part[:, :, :, :, k, :].transpose(2, 0, 3, 1, 4)]
where the time goes in v14:
time: 81 us; the launch traced here: 80.8 us
  blocking collectives  23.5 us (29%)
  between operations  14.5 us (18%)
  other arithmetic  10.8 us (13%)
  starting transfers between devices  8.82 us (11%)
  matrix products  8.53 us (11%)
  waiting for transfers between devices  8.47 us (10%)
  local copies, waits for them, and re-layouts  6.14 us (8%)
    all_gather x1, blocking collectives, gather_grids(): stacked = lax.all_gather(packed, GRID, axis=1, tiled=False)  23.5 us
    ppermute x2, waiting for transfers between devices, with_halo(): lax.ppermute(head, axis, [(i + 1, i) for i in range(ends)])  7.94 us
    ppermute x2, starting transfers between devices, with_halo(): lax.ppermute(tail, axis, [(i, i + 1) for i in range(ends)])  6.24 us
    ppermute x2, starting transfers between devices, with_halo(): lax.ppermute(head, axis, [(i + 1, i) for i in range(ends)])  2.58 us
    dot_general x4, matrix products, prolong(): wider = jnp.einsum('...hv,wv->...hw', coarse, pairs(width), precision=HIGH)  2.38 us
    select_n x6, other arithmetic, sweep_ext(): return [jnp.where(mask, n, 0.0) for n in new]  1.99 us
    dot_general x4, matrix products, sum_cols(): return jnp.einsum('...hw,wv->...hv', x, m, precision=HIGH)  1.95 us
  transfers between devices with their start and end apart: 5, of which 3 were waited for; matrix products, arithmetic and copies ran while one was open for 4% of the time, Pallas kernels for 0%

profile of v14, /device:TPU:0, one launch (start us, length us, event | category | flops | bytes accessed | tf_op | source)
XLA Modules:
  0.0 80.8 jit_solution(7079066517018999128)
XLA Ops:
  7.1 1.2 %fusion.11 = f32[480,16]{0,1:T(8,128)S(1)} fusion(pred[512,32]{1,0:T(32,128)(4,1)S(1)} %iota_compare_fusion.6, pred[512,64]{1,0:T(32,128)(4,1)S(1)} %iota_compare_fusion.7, pred[512,128]{1,0:T(32,128)(4,1)S(1)} %iota_compare_fusion.8, pred[512,256]{1,0:T(32,128)(4,1)S(1)} %iota_compare_fusion.4, f32[2,16,512]{2,1,0:T(8,128)} %param.5), kind=kOutput, calls=%fused_computation.21 | convolution fusion | flops 47923200 | bytes 309248 | tf_op jit(solution)/shard_map/hw,wu->hu/dot_general | solution.py:273
  9.4 0.6 fusion.12
  10.3 0.6 pad_maximum_fusion.5
  11.1 4.9 %collective-permute-start = (f32[11,4,512]{2,1,0:T(4,128)S(1)}, f32[11,4,512]{2,1,0:T(4,128)S(1)}, u32[]{:S(2)}, u32[]{:S(2)}) collective-permute-start(f32[11,4,512]{2,1,0:T(4,128)S(1)} %get-tuple-element.96), channel_id=1, source_target_pairs={{0,4},{4,8},{8,12},{1,5},{5,9},{9,13},{2,6},{6,10},{10,14},{3,7},{... | collective-permute-start | bytes 270344 | tf_op jit(solution)/shard_map/ppermute | solution.py:29
  16.1 1.3 %collective-permute-start.1 = (f32[11,4,512]{2,1,0:T(4,128)S(1)}, f32[11,4,512]{2,1,0:T(4,128)S(1)}, u32[]{:S(2)}, u32[]{:S(2)}) collective-permute-start(f32[11,4,512]{2,1,0:T(4,128)S(1)} %get-tuple-element.97), channel_id=1, source_target_pairs={{4,0},{8,4},{12,8},{5,1},{9,5},{13,9},{6,2},{10,6},{14,10},{7,3},{... | collective-permute-start | bytes 270344 | tf_op jit(solution)/shard_map/ppermute | solution.py:31
  17.7 0.5 collective-permute-done
  18.2 4.3 %collective-permute-done.1 = f32[11,4,512]{2,1,0:T(4,128)S(1)} collective-permute-done((f32[11,4,512]{2,1,0:T(4,128)S(1)}, f32[11,4,512]{2,1,0:T(4,128)S(1)}, u32[]{:S(2)}, u32[]{:S(2)}) %collective-permute-start.1) | collective-permute-done | bytes 90144 | tf_op jit(solution)/shard_map/ppermute | solution.py:31
  22.6 1.3 %collective-permute-start.2 = (f32[11,24,4]{2,1,0:T(8,128)S(1)}, f32[11,24,4]{2,1,0:T(8,128)S(1)}, u32[]{:S(2)}, u32[]{:S(2)}) collective-permute-start(f32[11,24,4]{2,1,0:T(8,128)S(1)} %get-tuple-element.88), channel_id=1, source_target_pairs={{0,1},{1,2},{2,3},{4,5},{5,6},{6,7},{8,9},{9,10},{10,11},{12,13},{... | collective-permute-start | bytes 12680 | tf_op jit(solution)/shard_map/ppermute | solution.py:29
  23.9 1.3 %collective-permute-start.3 = (f32[11,24,4]{2,1,0:T(8,128)S(1)}, f32[11,24,4]{2,1,0:T(8,128)S(1)}, u32[]{:S(2)}, u32[]{:S(2)}) collective-permute-start(f32[11,24,4]{2,1,0:T(8,128)S(1)} %get-tuple-element.89), channel_id=1, source_target_pairs={{1,0},{2,1},{3,2},{5,4},{6,5},{7,6},{9,8},{10,9},{11,10},{13,12},{... | collective-permute-start | bytes 12680 | tf_op jit(solution)/shard_map/ppermute | solution.py:31
  25.2 3.6 %collective-permute-done.3 = f32[11,24,4]{2,1,0:T(8,128)S(1)} collective-permute-done((f32[11,24,4]{2,1,0:T(8,128)S(1)}, f32[11,24,4]{2,1,0:T(8,128)S(1)}, u32[]{:S(2)}, u32[]{:S(2)}) %collective-permute-start.3) | collective-permute-done | bytes 4256 | tf_op jit(solution)/shard_map/ppermute | solution.py:31
  28.9 0.4 pad_maximum_fusion
  29.7 0.3 fusion.276
  30.0 0.3 fusion.286
  30.3 0.3 fusion.297
  31.5 0.3 fusion.26
  31.8 23.5 %all-gather = f32[16,48,128]{2,0,1:T(8,128)S(1)} all-gather(f32[16,3,128]{2,0,1:T(8,128)S(1)} %bitcast.929), channel_id=2, replica_groups=mesh['groups'=2,'tiles'=4,'band'=2,'stokes'=2] {'tiles','band','stokes'}, dimensions={1}, use_global_device_ids=true | all-gather | bytes 417792 | tf_op jit(solution)/shard_map/all_gather | solution.py:157
  55.4 0.9 %slice_bitcast_fusion.3 = (f32[8,16,1,128]{3,0,1,2:T(8,128)S(1)}, f32[8,16,1,128]{3,0,1,2:T(8,128)S(1)}) fusion(f32[22,128,128]{2,1,0:T(8,128)} %all-gather.4.cloned.1.call-done), kind=kLoop, calls=%fused_computation.360 | loop fusion | bytes 262144 | tf_op jit(solution)/shard_map/transpose | solution.py:176
  58.2 1.0 %slice-done.1 = f32[16,128,128]{2,1,0:T(8,128)S(1)} async-done(((f32[22,128,128]{2,1,0:T(8,128)}), f32[16,128,128]{2,1,0:T(8,128)S(1)}, s32[]{:S(2)}) %slice-start.1) | async-done | bytes 1048600 | tf_op jit(solution)/shard_map/slice | solution.py:162
  59.2 1.0 %fusion.985 = (f32[8,2,4,4,1,128]{5,4,3,2,1,0:T(1,128)S(1)}, f32[8,2,4,4,1,128]{5,4,3,2,1,0:T(1,128)S(1)}, f32[8,2,4,4,1,128]{5,4,3,2,1,0:T(1,128)S(1)}, f32[8,2...) fusion(f32[8,2,4,4,8,128]{5,4,3,2,1,0:T(8,128)S(1)} %bitcast.871), kind=kLoop, calls=%fused_computation.1502 | loop fusion | bytes 2097152 | tf_op jit(solution)/shard_map/slice | solution.py:168
  61.5 0.5 fusion.81
  61.9 0.3 fusion.91
  62.5 1.0 %fusion.3 = f32[3,16,512]{2,1,0:T(8,128)S(1)} fusion(f32[3,16,1024]{2,1,0:T(8,128)S(1)} %convolution_bitcast_fusion.2, s32[1024]{0:T(1024)S(1)} %get-tuple-element.166, s32[1024]{0:T(1024)S(1)} %get-tuple-element.167, pred[1024]{0:T(1024)(128)(4,1)S(1)} %fusion.739), kind=kOutput, calls=%fused_computation.4 | convolution fusion | flops 303038464 | bytes 304128 | tf_op jit(solution)/shard_map/...hw,wv->...hv/dot_general | solution.py:59
  64.2 0.3 fusion.24
  68.0 1.3 %fusion.1 = f32[3,16,1024]{2,1,0:T(8,128)S(1)} fusion(s32[1024]{0:T(1024)S(1)} %get-tuple-element.166, s32[1024]{0:T(1024)S(1)} %get-tuple-element.167, pred[1024]{0:T(1024)(128)(4,1)S(1)} %fusion.739, f32[1,16,512]{2,1,0:T(8,128)S(1)} %get-tuple-element.99, f32[1,16,512]{2,1,0:T(8,128)S(1)} %get-tuple-element.98, f32[1,16,512]{2,1,0:T(8,128)S(1)} %get-tuple-element.8), kind=kOutput, calls=%fused_computation.3 | convolution fusion | flops 303087616 | bytes 304128 | tf_op jit(solution)/shard_map/...hv,wv->...hw/dot_general | solution.py:76
  69.3 0.4 convolution_bitcast_fusion
  70.0 0.5 fusion.185
  70.5 0.3 fusion.186
  70.8 0.5 fusion.20
  71.6 0.3 fusion.251
  71.9 0.3 fusion.262
  72.3 0.3 fusion.241
  73.3 0.6 pad_maximum_fusion.4
  (195 shorter events, 11.7 us)
Async XLA Ops:
  6.5 2.1 %copy-start = (f32[6,16,512]{2,1,0:T(8,128)S(1)}, f32[6,16,512]{2,1,0:T(8,128)}, u32[]{:S(2)}) copy-start(f32[6,16,512]{2,1,0:T(8,128)} %param.4) | copy-start | bytes 589828
  6.5 48.9 %all-gather.4.cloned.1.call-start = ((), (), s32[]{:S(2)}) async-start(), calls=%async_computation | async-start | bytes 1531904 | tf_op jit(solution)/shard_map/all_gather | solution.py:157
  6.8 2.3 %copy-start.1 = (f32[2,16,512]{2,1,0:T(8,128)S(1)}, f32[2,16,512]{2,1,0:T(8,128)}, u32[]{:S(2)}) copy-start(f32[2,16,512]{2,1,0:T(8,128)} %param.5) | copy-start | bytes 196612
  9.4 1.6 %copy-start.2 = (f32[3,16,512]{2,1,0:T(8,128)S(1)}, f32[3,16,512]{2,1,0:T(8,128)}, u32[]{:S(2)}) copy-start(f32[3,16,512]{2,1,0:T(8,128)} %param.3) | copy-start | bytes 294916
  11.1 7.1 %collective-permute-start = (f32[11,4,512]{2,1,0:T(4,128)S(1)}, f32[11,4,512]{2,1,0:T(4,128)S(1)}, u32[]{:S(2)}, u32[]{:S(2)}) collective-permute-start(f32[11,4,512]{2,1,0:T(4,128)S(1)} %get-tuple-element.96), channel_id=1, source_target_pairs={{0,4},{4,8},{8,12},{1,5},{5,9},{9,13},{2,6},{6,10},{10,14},{3,7},{... | collective-permute-start | bytes 270344 | tf_op jit(solution)/shard_map/ppermute | solution.py:29
  16.1 6.4 %collective-permute-start.1 = (f32[11,4,512]{2,1,0:T(4,128)S(1)}, f32[11,4,512]{2,1,0:T(4,128)S(1)}, u32[]{:S(2)}, u32[]{:S(2)}) collective-permute-start(f32[11,4,512]{2,1,0:T(4,128)S(1)} %get-tuple-element.97), channel_id=1, source_target_pairs={{4,0},{8,4},{12,8},{5,1},{9,5},{13,9},{6,2},{10,6},{14,10},{7,3},{... | collective-permute-start | bytes 270344 | tf_op jit(solution)/shard_map/ppermute | solution.py:31
  22.6 2.6 %collective-permute-start.2 = (f32[11,24,4]{2,1,0:T(8,128)S(1)}, f32[11,24,4]{2,1,0:T(8,128)S(1)}, u32[]{:S(2)}, u32[]{:S(2)}) collective-permute-start(f32[11,24,4]{2,1,0:T(8,128)S(1)} %get-tuple-element.88), channel_id=1, source_target_pairs={{0,1},{1,2},{2,3},{4,5},{5,6},{6,7},{8,9},{9,10},{10,11},{12,13},{... | collective-permute-start | bytes 12680 | tf_op jit(solution)/shard_map/ppermute | solution.py:29
  23.9 5.0 %collective-permute-start.3 = (f32[11,24,4]{2,1,0:T(8,128)S(1)}, f32[11,24,4]{2,1,0:T(8,128)S(1)}, u32[]{:S(2)}, u32[]{:S(2)}) collective-permute-start(f32[11,24,4]{2,1,0:T(8,128)S(1)} %get-tuple-element.89), channel_id=1, source_target_pairs={{1,0},{2,1},{3,2},{5,4},{6,5},{7,6},{9,8},{10,9},{11,10},{13,12},{... | collective-permute-start | bytes 12680 | tf_op jit(solution)/shard_map/ppermute | solution.py:31
  55.4 2.6 %slice-start = ((f32[22,128,128]{2,1,0:T(8,128)}), f32[4,128,128]{2,1,0:T(8,128)S(1)}, s32[]{:S(2)}) async-start(f32[22,128,128]{2,1,0:T(8,128)} %all-gather.4.cloned.1.call-done), calls=%async_computation.1 | async-start | bytes 524288 | tf_op jit(solution)/shard_map/slice | solution.py:162
  58.0 1.2 %slice-start.1 = ((f32[22,128,128]{2,1,0:T(8,128)}), f32[16,128,128]{2,1,0:T(8,128)S(1)}, s32[]{:S(2)}) async-start(f32[22,128,128]{2,1,0:T(8,128)} %all-gather.4.cloned.1.call-done), calls=%async_computation.2 | async-start | bytes 2097152 | tf_op jit(solution)/shard_map/slice | solution.py:162
Sparse Core Ops, SparseCore 0:
  11.1 42.0 all-gather.3

commit v15 on v10

--- a/solution.py
+++ b/solution.py
@@ -173,9 +173,9 @@
     return grids
 
 
-def own_window(whole, height, width, ring):
-    row = lax.axis_index(ROWS) * height
-    col = lax.axis_index(COLS) * width
+def own_window(whole, height, width, ring, rimmed=0):
+    row = lax.axis_index(ROWS) * (height - 2 * rimmed)
+    col = lax.axis_index(COLS) * (width - 2 * rimmed)
     lead = whole.shape[:-2]
     pads = [(0, 0)] * len(lead) + [(ring, ring), (ring, ring)]
     padded = jnp.pad(whole, pads) if ring else whole
@@ -330,7 +330,8 @@
             coarse_source = restrict_sum(jnp.stack(residual))
             if level + 1 == gathered:
                 correction = cycle_whole(gather_grid(coarse_source), hierarchy, gathered)
-                return own_window(jnp.stack(correction), height // 2, width // 2, ring)
+                rimmed = jnp.stack([jnp.pad(c, ring) for c in correction])
+                return own_window(rimmed, height // 2 + 2 * ring, width // 2 + 2 * ring, 0, ring)
             coarse = run(level + 1, list(with_halo(coarse_source, HALO)))
             return with_halo(jnp.stack(coarse), ring)
 

time: 79.2 us -> 79.6 us (level)
    add x10 -> x12, other arithmetic: 1.15 us -> 1.99 us  [smooth_whole(): i + OMEGA * (s - a) / d]
    another operation x2 -> x0, other arithmetic: 0.8 us -> none  [below(): return own_window(jnp.stack(correction), height // 2, width // 2, ring)]
where the time goes in v15:
time: 79.6 us; the launch traced here: 79.3 us
  blocking collectives  23.5 us (30%)
  between operations  14.4 us (18%)
  other arithmetic  10.8 us (14%)
  starting transfers between devices  8.82 us (11%)
  waiting for transfers between devices  8.55 us (11%)
  matrix products  8.48 us (11%)
  local copies, waits for them, and re-layouts  4.75 us (6%)
    all_gather x1, blocking collectives, gather_grids(): stacked = lax.all_gather(packed, GRID, axis=1, tiled=False)  23.5 us
    ppermute x2, waiting for transfers between devices, with_halo(): lax.ppermute(head, axis, [(i + 1, i) for i in range(ends)])  7.94 us
    ppermute x2, starting transfers between devices, with_halo(): lax.ppermute(tail, axis, [(i, i + 1) for i in range(ends)])  6.23 us
    ppermute x2, starting transfers between devices, with_halo(): lax.ppermute(head, axis, [(i + 1, i) for i in range(ends)])  2.58 us
    dot_general x4, matrix products, prolong(): wider = jnp.einsum('...hv,wv->...hw', coarse, pairs(width), precision=HIGH)  2.32 us
    add x12, other arithmetic, smooth_whole(): i + OMEGA * (s - a) / d  1.99 us
    select_n x6, other arithmetic, sweep_ext(): return [jnp.where(mask, n, 0.0) for n in new]  1.98 us
    dot_general x4, matrix products, sum_cols(): return jnp.einsum('...hw,wv->...hv', x, m, precision=HIGH)  1.95 us
  transfers between devices with their start and end apart: 5, of which 3 were waited for; matrix products, arithmetic and copies ran while one was open for 4% of the time, Pallas kernels for 0%

profile of v15, /device:TPU:0, one launch (start us, length us, event | category | flops | bytes accessed | tf_op | source)
XLA Modules:
  0.0 79.3 jit_solution(7664601017360543727)
XLA Ops:
  7.1 1.2 %fusion.11 = f32[480,16]{0,1:T(8,128)S(1)} fusion(pred[512,32]{1,0:T(32,128)(4,1)S(1)} %iota_compare_fusion.4, pred[512,64]{1,0:T(32,128)(4,1)S(1)} %iota_compare_fusion.5, pred[512,128]{1,0:T(32,128)(4,1)S(1)} %iota_compare_fusion.6, pred[512,256]{1,0:T(32,128)(4,1)S(1)} %iota_compare_fusion.2, f32[2,16,512]{2,1,0:T(8,128)} %param.5), kind=kOutput, calls=%fused_computation.22 | convolution fusion | flops 47923200 | bytes 309248 | tf_op jit(solution)/shard_map/hw,wu->hu/dot_general | solution.py:265
  9.4 0.6 fusion.12
  10.4 0.6 pad_maximum_fusion.5
  11.1 4.9 %collective-permute-start = (f32[11,4,512]{2,1,0:T(4,128)S(1)}, f32[11,4,512]{2,1,0:T(4,128)S(1)}, u32[]{:S(2)}, u32[]{:S(2)}) collective-permute-start(f32[11,4,512]{2,1,0:T(4,128)S(1)} %get-tuple-element.96), channel_id=1, source_target_pairs={{0,4},{4,8},{8,12},{1,5},{5,9},{9,13},{2,6},{6,10},{10,14},{3,7},{... | collective-permute-start | bytes 270344 | tf_op jit(solution)/shard_map/ppermute | solution.py:29
  16.1 1.3 %collective-permute-start.1 = (f32[11,4,512]{2,1,0:T(4,128)S(1)}, f32[11,4,512]{2,1,0:T(4,128)S(1)}, u32[]{:S(2)}, u32[]{:S(2)}) collective-permute-start(f32[11,4,512]{2,1,0:T(4,128)S(1)} %get-tuple-element.97), channel_id=1, source_target_pairs={{4,0},{8,4},{12,8},{5,1},{9,5},{13,9},{6,2},{10,6},{14,10},{7,3},{... | collective-permute-start | bytes 270344 | tf_op jit(solution)/shard_map/ppermute | solution.py:31
  17.6 0.6 collective-permute-done
  18.2 4.3 %collective-permute-done.1 = f32[11,4,512]{2,1,0:T(4,128)S(1)} collective-permute-done((f32[11,4,512]{2,1,0:T(4,128)S(1)}, f32[11,4,512]{2,1,0:T(4,128)S(1)}, u32[]{:S(2)}, u32[]{:S(2)}) %collective-permute-start.1) | collective-permute-done | bytes 90144 | tf_op jit(solution)/shard_map/ppermute | solution.py:31
  22.6 1.3 %collective-permute-start.2 = (f32[11,24,4]{2,1,0:T(8,128)S(1)}, f32[11,24,4]{2,1,0:T(8,128)S(1)}, u32[]{:S(2)}, u32[]{:S(2)}) collective-permute-start(f32[11,24,4]{2,1,0:T(8,128)S(1)} %get-tuple-element.88), channel_id=1, source_target_pairs={{0,1},{1,2},{2,3},{4,5},{5,6},{6,7},{8,9},{9,10},{10,11},{12,13},{... | collective-permute-start | bytes 12680 | tf_op jit(solution)/shard_map/ppermute | solution.py:29
  23.9 1.3 %collective-permute-start.3 = (f32[11,24,4]{2,1,0:T(8,128)S(1)}, f32[11,24,4]{2,1,0:T(8,128)S(1)}, u32[]{:S(2)}, u32[]{:S(2)}) collective-permute-start(f32[11,24,4]{2,1,0:T(8,128)S(1)} %get-tuple-element.89), channel_id=1, source_target_pairs={{1,0},{2,1},{3,2},{5,4},{6,5},{7,6},{9,8},{10,9},{11,10},{13,12},{... | collective-permute-start | bytes 12680 | tf_op jit(solution)/shard_map/ppermute | solution.py:31
  25.3 3.6 %collective-permute-done.3 = f32[11,24,4]{2,1,0:T(8,128)S(1)} collective-permute-done((f32[11,24,4]{2,1,0:T(8,128)S(1)}, f32[11,24,4]{2,1,0:T(8,128)S(1)}, u32[]{:S(2)}, u32[]{:S(2)}) %collective-permute-start.3) | collective-permute-done | bytes 4256 | tf_op jit(solution)/shard_map/ppermute | solution.py:31
  28.9 0.4 pad_maximum_fusion
  29.7 0.3 fusion.249
  30.0 0.3 fusion.259
  30.4 0.3 fusion.270
  31.5 0.3 fusion.26
  31.8 23.5 %all-gather = f32[16,48,128]{2,0,1:T(8,128)S(1)} all-gather(f32[16,3,128]{2,0,1:T(8,128)S(1)} %bitcast.873), channel_id=2, replica_groups=mesh['groups'=2,'tiles'=4,'band'=2,'stokes'=2] {'tiles','band','stokes'}, dimensions={1}, use_global_device_ids=true | all-gather | bytes 417792 | tf_op jit(solution)/shard_map/all_gather | solution.py:157
  55.4 0.9 %slice_bitcast_fusion.3 = (f32[8,16,1,128]{3,0,1,2:T(8,128)S(1)}, f32[8,16,1,128]{3,0,1,2:T(8,128)S(1)}) fusion(f32[22,128,128]{2,1,0:T(8,128)} %all-gather.4.cloned.1.call-done), kind=kLoop, calls=%fused_computation.342 | loop fusion | bytes 262144 | tf_op jit(solution)/shard_map/transpose | solution.py:168
  58.0 0.5 slice-done
  58.4 0.6 copy.178
  59.7 0.5 fusion.81
  60.1 0.3 fusion.91
  60.7 1.0 %fusion.3 = f32[3,16,512]{2,1,0:T(8,128)S(1)} fusion(f32[3,16,1024]{2,1,0:T(8,128)S(1)} %convolution_bitcast_fusion.2, s32[1024]{0:T(1024)S(1)} %get-tuple-element.162, s32[1024]{0:T(1024)S(1)} %get-tuple-element.163, pred[1024]{0:T(1024)(128)(4,1)S(1)} %fusion.706), kind=kOutput, calls=%fused_computation.4 | convolution fusion | flops 303038464 | bytes 304128 | tf_op jit(solution)/shard_map/...hw,wv->...hv/dot_general | solution.py:59
  62.4 0.3 fusion.24
  66.2 1.3 %fusion.1 = f32[3,16,1024]{2,1,0:T(8,128)S(1)} fusion(s32[1024]{0:T(1024)S(1)} %get-tuple-element.162, s32[1024]{0:T(1024)S(1)} %get-tuple-element.163, pred[1024]{0:T(1024)(128)(4,1)S(1)} %fusion.706, f32[1,16,512]{2,1,0:T(8,128)S(1)} %get-tuple-element.99, f32[1,16,512]{2,1,0:T(8,128)S(1)} %get-tuple-element.98, f32[1,16,512]{2,1,0:T(8,128)S(1)} %get-tuple-element.8), kind=kOutput, calls=%fused_computation.3 | convolution fusion | flops 303087616 | bytes 304128 | tf_op jit(solution)/shard_map/...hv,wv->...hw/dot_general | solution.py:76
  67.5 0.4 convolution_bitcast_fusion
  68.2 0.5 fusion.173
  68.7 0.3 fusion.161
  69.4 0.4 fusion.20
  70.2 0.3 fusion.224
  70.5 0.3 fusion.235
  70.8 0.3 fusion.214
  71.8 0.6 pad_maximum_fusion.4
  (183 shorter events, 11.3 us)
Async XLA Ops:
  6.5 2.1 %copy-start = (f32[6,16,512]{2,1,0:T(8,128)S(1)}, f32[6,16,512]{2,1,0:T(8,128)}, u32[]{:S(2)}) copy-start(f32[6,16,512]{2,1,0:T(8,128)} %param.4) | copy-start | bytes 589828
  6.5 48.9 %all-gather.4.cloned.1.call-start = ((), (), s32[]{:S(2)}) async-start(), calls=%async_computation | async-start | bytes 1531904 | tf_op jit(solution)/shard_map/all_gather | solution.py:157
  6.8 2.3 %copy-start.1 = (f32[2,16,512]{2,1,0:T(8,128)S(1)}, f32[2,16,512]{2,1,0:T(8,128)}, u32[]{:S(2)}) copy-start(f32[2,16,512]{2,1,0:T(8,128)} %param.5) | copy-start | bytes 196612
  9.4 1.6 %copy-start.2 = (f32[3,16,512]{2,1,0:T(8,128)S(1)}, f32[3,16,512]{2,1,0:T(8,128)}, u32[]{:S(2)}) copy-start(f32[3,16,512]{2,1,0:T(8,128)} %param.3) | copy-start | bytes 294916
  11.1 7.1 %collective-permute-start = (f32[11,4,512]{2,1,0:T(4,128)S(1)}, f32[11,4,512]{2,1,0:T(4,128)S(1)}, u32[]{:S(2)}, u32[]{:S(2)}) collective-permute-start(f32[11,4,512]{2,1,0:T(4,128)S(1)} %get-tuple-element.96), channel_id=1, source_target_pairs={{0,4},{4,8},{8,12},{1,5},{5,9},{9,13},{2,6},{6,10},{10,14},{3,7},{... | collective-permute-start | bytes 270344 | tf_op jit(solution)/shard_map/ppermute | solution.py:29
  16.1 6.4 %collective-permute-start.1 = (f32[11,4,512]{2,1,0:T(4,128)S(1)}, f32[11,4,512]{2,1,0:T(4,128)S(1)}, u32[]{:S(2)}, u32[]{:S(2)}) collective-permute-start(f32[11,4,512]{2,1,0:T(4,128)S(1)} %get-tuple-element.97), channel_id=1, source_target_pairs={{4,0},{8,4},{12,8},{5,1},{9,5},{13,9},{6,2},{10,6},{14,10},{7,3},{... | collective-permute-start | bytes 270344 | tf_op jit(solution)/shard_map/ppermute | solution.py:31
  22.6 2.6 %collective-permute-start.2 = (f32[11,24,4]{2,1,0:T(8,128)S(1)}, f32[11,24,4]{2,1,0:T(8,128)S(1)}, u32[]{:S(2)}, u32[]{:S(2)}) collective-permute-start(f32[11,24,4]{2,1,0:T(8,128)S(1)} %get-tuple-element.88), channel_id=1, source_target_pairs={{0,1},{1,2},{2,3},{4,5},{5,6},{6,7},{8,9},{9,10},{10,11},{12,13},{... | collective-permute-start | bytes 12680 | tf_op jit(solution)/shard_map/ppermute | solution.py:29
  23.9 5.0 %collective-permute-start.3 = (f32[11,24,4]{2,1,0:T(8,128)S(1)}, f32[11,24,4]{2,1,0:T(8,128)S(1)}, u32[]{:S(2)}, u32[]{:S(2)}) collective-permute-start(f32[11,24,4]{2,1,0:T(8,128)S(1)} %get-tuple-element.89), channel_id=1, source_target_pairs={{1,0},{2,1},{3,2},{5,4},{6,5},{7,6},{9,8},{10,9},{11,10},{13,12},{... | collective-permute-start | bytes 12680 | tf_op jit(solution)/shard_map/ppermute | solution.py:31
  57.2 1.2 %slice-start = ((f32[22,128,128]{2,1,0:T(8,128)}), f32[16,128,128]{2,1,0:T(8,128)S(1)}, s32[]{:S(2)}) async-start(f32[22,128,128]{2,1,0:T(8,128)} %all-gather.4.cloned.1.call-done), calls=%async_computation.1 | async-start | bytes 2097152 | tf_op jit(solution)/shard_map/slice | solution.py:162
  58.0 1.1 %slice-start.1 = ((f32[22,128,128]{2,1,0:T(8,128)}), f32[4,128,128]{2,1,0:T(8,128)S(1)}, s32[]{:S(2)}) async-start(f32[22,128,128]{2,1,0:T(8,128)} %all-gather.4.cloned.1.call-done), calls=%async_computation.2 | async-start | bytes 524288 | tf_op jit(solution)/shard_map/slice | solution.py:162
Sparse Core Ops, SparseCore 0:
  11.2 42.0 all-gather.3
